TPU v7x, 512 devices: a whole 4x4x16 slice. The times are simulated.
512 devices in a mesh: cells: 128 (over y, z, core), dirs: 4 (over x).
Axes of the slice: x: 4, y: 4, z: 16, core: 2. Of those that a mesh axis runs over, the one named last changes fastest.
Arguments:
- incident: float32 [8192, 6144], P('cells', 'dirs'), may hold values from -24 to 24
- scattering: float32 [8192, 192], P('cells'), may hold values from 0.1 to 1
- translations: bfloat16 [8, 192, 192], replicated, may hold values from -1.5 to 1.5
- pair_sphere: int32 [8192, 16], P('cells'), may hold values from 0 to 8191, as said below
- pair_class: int32 [8192, 16], P('cells'), may hold values from 0 to 7
- pair_weight: bfloat16 [8192, 16], P('cells'), may hold values from 0.19921875 to 0.796875
- pair_mask: int32 [8192, 16], P('cells'), may hold values from 0 to 1, as said below
Outputs:
- solution: float32 [8192, 6144], P('cells', 'dirs')
- residual: float32 [8192, 6144], P('cells', 'dirs')
- dual_residual: float32 [8192, 6144], P('cells', 'dirs')
- direction: float32 [8192, 6144], P('cells', 'dirs')
Inputs may be any that keep to these rules, and one draw needn't show every extreme that they name: `pair_sphere`: sphere ids are cell-major: cell c holds spheres 64 c to 64 (c + 1) - 1, and the cells form a cycle. The slots of one sphere name distinct spheres, never the sphere itself; each named sphere lies in the sphere's own cell, or among the last 32 spheres of the previous cell, or among the first 32 spheres of the next cell. In every cell the first sphere names sphere 64 - 32 of the previous cell and the last sphere names sphere 32 - 1 of the next, both in live slots. `pair_mask`: the live slots of a sphere come first; the first and the last sphere of every cell have all 16 slots live, every sphere at least 8.
All inputs are finite; a program needn't handle non-finite values.
Results may differ from a plain program's by a relative error of at most 0.0003.
The roundings to bfloat16 on the way count: a program that leaves them out, or rounds other values in their place, can miss the bound.
Values may be sent and summed in bfloat16 or wider, within the bound.
No kernel may reach another device: no remote copies, remote signals or barrier semaphores. Data moves between devices by JAX's collectives and lax.ppermute only.
A program may use at most 64 MiB of HBM per device.

v0:
```python
import jax
import jax.numpy as jnp
from jax import lax
from jax.sharding import PartitionSpec as P


def extended(x, sides, width):
    for axis, dim in sides:
        devices, length = (lax.axis_size(axis), x.shape[dim])
        up = [(i, (i + 1) % devices) for i in range(devices)]
        down = [(j, i) for i, j in up]
        last = lax.slice_in_dim(x, length - width, length, axis=dim)
        leading = lax.slice_in_dim(x, 0, width, axis=dim)
        before = lax.ppermute(last, axis, up)
        after = lax.ppermute(leading, axis, down)
        x = jnp.concatenate([before, x, after], axis=dim)
    return x


def passed_along(x, axis, by):
    devices = lax.axis_size(axis)
    return lax.ppermute(x, axis, [(i, (i + by) % devices) for i in range(devices)])


def on_device(incident, scattering, translations, pair_sphere, pair_class, pair_weight, pair_mask):
    spheres = incident.shape[0]
    columns = incident.shape[1]
    order = translations.shape[1]
    groups = columns // order
    classes = translations.shape[0]
    extent = spheres + 2 * spheres
    source = incident.astype(jnp.bfloat16)
    padded = extended(source, (("cells", 0),), spheres)
    position = lax.axis_index("cells")
    cell_count = lax.axis_size("cells")
    owner = pair_sphere // spheres
    within = pair_sphere % spheres
    offset = (owner - position) % cell_count
    column = jnp.where(
        offset == 0,
        spheres + within,
        jnp.where(offset == 1, spheres + spheres + within, spheres - spheres + within),
    )
    placed = (column[:, :, None] == jnp.arange(extent, dtype=jnp.int32)[None, None, :]).astype(
        jnp.bfloat16
    )
    strength = pair_weight.astype(jnp.float32) * pair_mask.astype(jnp.float32)
    chosen = pair_class[:, :, None] == jnp.arange(classes, dtype=jnp.int32)[None, None, :]
    coupling = jnp.where(chosen, strength[:, :, None], jnp.float32(0.0)).astype(jnp.bfloat16)
    blocks = jnp.einsum("smk,smc->ksc", coupling, placed, preferred_element_type=jnp.float32)
    blocks_half = blocks.astype(jnp.bfloat16)

    def primal_step(total, pieces):
        block, operator = pieces
        summed = jnp.dot(block, padded, preferred_element_type=jnp.float32).astype(jnp.bfloat16)
        moved = jnp.dot(
            summed.reshape(spheres * groups, order), operator, preferred_element_type=jnp.float32
        )
        return (total + moved.reshape(spheres, columns), None)

    coupled, unused = lax.scan(
        primal_step, jnp.zeros((spheres, columns), jnp.float32), (blocks_half, translations)
    )
    gain = jnp.tile(scattering, (1, groups))
    image = incident - gain * coupled
    weighted = (gain * incident).astype(jnp.bfloat16)
    flat_weighted = weighted.reshape(spheres * groups, order)

    def dual_step(total, pieces):
        block, operator = pieces
        moved = lax.dot_general(
            flat_weighted, operator, (((1,), (1,)), ((), ())), preferred_element_type=jnp.float32
        )
        spread = lax.dot_general(
            block,
            moved.reshape(spheres, columns),
            (((0,), (0,)), ((), ())),
            precision=lax.Precision.HIGHEST,
            preferred_element_type=jnp.float32,
        )
        return (total + spread, None)

    contrib, unused_two = lax.scan(
        dual_step, jnp.zeros((extent, columns), jnp.float32), (blocks, translations)
    )
    lower_part = contrib[:spheres]
    upper_part = contrib[spheres + spheres :]
    from_next = passed_along(lower_part, "cells", -1)
    from_prev = passed_along(upper_part, "cells", 1)
    back = contrib[spheres : spheres + spheres]
    back = back.at[spheres - spheres :].add(from_next)
    back = back.at[:spheres].add(from_prev)
    dual_image = incident - back
    norm_old = lax.psum(jnp.sum(incident * incident), ("cells", "dirs"))
    curvature = lax.psum(jnp.sum(incident * image), ("cells", "dirs"))
    step_size = norm_old / curvature
    solution = step_size * incident
    residual = incident - step_size * image
    dual_residual = incident - step_size * dual_image
    norm_new = lax.psum(jnp.sum(residual * dual_residual), ("cells", "dirs"))
    direction = residual + norm_new / norm_old * incident
    return (solution, residual, dual_residual, direction)


def solution(mesh):
    placed = (
        P("cells", "dirs"),
        P("cells", None),
        P(),
        P("cells", None),
        P("cells", None),
        P("cells", None),
        P("cells", None),
    )
    return jax.shard_map(
        on_device,
        mesh=mesh,
        in_specs=placed,
        out_specs=(P("cells", "dirs"), P("cells", "dirs"), P("cells", "dirs"), P("cells", "dirs")),
        check_vma=False,
    )
```

profile of v0, /device:TPU:1, one launch (start us, length us, event | category | flops | bytes accessed | tf_op | source)
XLA Modules:
  0.0 300.5 jit_solution(9938853211131761298)
XLA Ops:
  0.6 1.0 convert_element_type.26
  1.7 8.8 %collective-permute-start.1 = (bf16[64,1536]{1,0:T(8,128)(2,1)S(1)}, bf16[64,1536]{1,0:T(8,128)(2,1)S(1)}, u32[]{:S(2)}, u32[]{:S(2)}) collective-permute-start(bf16[64,1536]{1,0:T(8,128)(2,1)S(1)} %convert_element_type.26), channel_id=1, source_target_pairs={{4,0},{8,4},{12,8},{16,12},{20,16},{24,20},{28,24},{32,28},{36,32}... | collective-permute-start | bytes 589832 | tf_op jit(solution)/shard_map/ppermute | solution.py:15
  10.4 1.9 collective-permute-start
  14.8 0.9 tile.4
  15.7 0.9 tile.10
  16.6 1.1 fusion.20
  17.8 1.5 collective-permute-done
  19.4 25.5 %while.26 = (s32[]{:T(128)}, f32[64,1536]{1,0:T(8,128)S(1)}, bf16[8,64,192]{2,1,0:T(8,128)(2,1)S(1)}, bf16[192,1536]{1,0:T(8,128)(2,1)S(1)}, bf16[8,192,192]{2,1,0:T(8,128)(2,1)}, /*index=5*/s32[]{:T(128)}, s32[]{:T(128)}) while((s32[]{:T(128)}, f32[64,1536]{1,0:T(8,128)S(1)}, bf16[8,64,192]{2,1,0:T(8,128)(2,1)S(1)}, ...), condition=%wide.region_3.4_spmd.clone, body=%wide.region_2.3_spmd.clone.sunk | while | flops 75792384 | bytes 5439647 | solution.py:61
  20.3 1.1 fusion.37
  23.5 1.1 fusion.37
  26.7 1.1 fusion.37
  29.9 1.1 fusion.37
  33.0 1.1 fusion.37
  36.2 1.1 fusion.37
  39.4 1.1 fusion.37
  42.6 1.1 fusion.37
  44.9 1.7 multiply_reduce_fusion.1
  46.8 31.9 %while.27 = (s32[]{:T(128)}, f32[192,1536]{1,0:T(8,128)S(1)}, f32[8,64,192]{2,0,1:T(8,128)}, bf16[8,192,192]{2,1,0:T(8,128)(2,1)}, bf16[512,192]{1,0:T(8,128)(2,1)S(1)}, /*index=5*/s32[]{:T(128)}, s32[]{:T(128)}) while((s32[]{:T(128)}, f32[192,1536]{1,0:T(8,128)S(1)}, f32[8,64,192]{2,0,1:T(8,128)}, bf16[8,192,192]{2,1,0:T(8,128)(2,1)}, ...), condition=%wide.region_7.8_spmd.clone, body=%wide.region_6.7_spmd.clone.sunk | while | flops 264830976 | bytes 5161063 | solution.py:83
  46.8 1.1 constant_dynamic-slice_fusion.2
  47.9 1.1 convolution_bitcast_fusion.3
  49.4 1.3 convolution_add_fusion.2
  50.8 1.1 constant_dynamic-slice_fusion.2
  51.9 1.1 convolution_bitcast_fusion.3
  53.4 1.3 convolution_add_fusion.2
  54.8 1.1 constant_dynamic-slice_fusion.2
  55.9 1.1 convolution_bitcast_fusion.3
  57.4 1.3 convolution_add_fusion.2
  58.8 1.1 constant_dynamic-slice_fusion.2
  59.9 1.1 convolution_bitcast_fusion.3
  61.4 1.3 convolution_add_fusion.2
  62.8 1.1 constant_dynamic-slice_fusion.2
  63.9 1.1 convolution_bitcast_fusion.3
  65.4 1.3 convolution_add_fusion.2
  66.8 1.1 constant_dynamic-slice_fusion.2
  67.9 1.1 convolution_bitcast_fusion.3
  69.4 1.3 convolution_add_fusion.2
  70.8 1.1 constant_dynamic-slice_fusion.2
  71.9 1.1 convolution_bitcast_fusion.3
  73.4 1.3 convolution_add_fusion.2
  74.8 1.1 constant_dynamic-slice_fusion.2
  75.9 1.1 convolution_bitcast_fusion.3
  77.4 1.3 convolution_add_fusion.2
  78.8 9.5 %collective-permute-start.2 = (f32[64,1536]{1,0:T(8,128)S(1)}, f32[64,1536]{1,0:T(8,128)S(1)}, u32[]{:S(2)}, u32[]{:S(2)}) collective-permute-start(f32[64,1536]{1,0:T(8,128)S(1)} %get-tuple-element.183), channel_id=1, source_target_pairs={{0,508},{4,0},{8,4},{12,8},{16,12},{20,16},{24,20},{28,24},{32,28}... | collective-permute-start | bytes 1179656 | tf_op jit(solution)/shard_map/ppermute | solution.py:22
  88.3 1.9 collective-permute-start.3
  90.3 105.4 %all-reduce = (f32[]{:T(128)}, f32[]{:T(128)}) all-reduce(f32[]{:T(128)} %get-tuple-element.157, f32[]{:T(128)} %get-tuple-element.156), channel_id=1, replica_groups=mesh['cells'=128,'dirs'=4] {'cells','dirs'}, use_global_device_ids=true, to_apply=%region_1.2 | all-reduce | flops 2 | bytes 16 | tf_op jit(solution)/shard_map/psum | solution.py:94
  197.0 2.5 multiply_reduce_fusion
  199.6 98.7 %psum.23 = f32[]{:T(128)} all-reduce(f32[]{:T(128)} %get-tuple-element.180), channel_id=1, replica_groups=mesh['cells'=128,'dirs'=4] {'cells','dirs'}, use_global_device_ids=true, to_apply=%region_9.10 | all-reduce | flops 1 | bytes 8 | tf_op jit(solution)/shard_map/psum | solution.py:100
  299.6 1.0 multiply_add_fusion
  (100 shorter events, 22.0 us)
Async XLA Ops:
  1.7 16.2 %collective-permute-start.1 = (bf16[64,1536]{1,0:T(8,128)(2,1)S(1)}, bf16[64,1536]{1,0:T(8,128)(2,1)S(1)}, u32[]{:S(2)}, u32[]{:S(2)}) collective-permute-start(bf16[64,1536]{1,0:T(8,128)(2,1)S(1)} %convert_element_type.26), channel_id=1, source_target_pairs={{4,0},{8,4},{12,8},{16,12},{20,16},{24,20},{28,24},{32,28},{36,32}... | collective-permute-start | bytes 589832 | tf_op jit(solution)/shard_map/ppermute | solution.py:15
  10.4 8.8 %collective-permute-start = (bf16[64,1536]{1,0:T(8,128)(2,1)S(1)}, bf16[64,1536]{1,0:T(8,128)(2,1)S(1)}, u32[]{:S(2)}, u32[]{:S(2)}) collective-permute-start(bf16[64,1536]{1,0:T(8,128)(2,1)S(1)} %convert_element_type.26), channel_id=1, source_target_pairs={{0,4},{4,8},{8,12},{12,16},{16,20},{20,24},{24,28},{28,32},{32,36}... | collective-permute-start | bytes 589832 | tf_op jit(solution)/shard_map/ppermute | solution.py:14
  19.3 25.5 %copy-start = (f32[64,1536]{1,0:T(8,128)S(1)}, f32[64,1536]{1,0:T(8,128)}, u32[]{:S(2)}) copy-start(f32[64,1536]{1,0:T(8,128)} %param.19) | copy-start | bytes 1179652
  19.4 0.7 copy-start.3
  21.6 1.0 copy-start.4
  22.6 0.7 copy-start.3
  24.8 1.0 copy-start.4
  25.7 0.7 copy-start.3
  28.0 1.0 copy-start.4
  28.9 0.7 copy-start.3
  31.2 1.0 copy-start.4
  32.1 0.7 copy-start.3
  34.3 1.0 copy-start.4
  35.3 0.7 copy-start.3
  37.5 1.0 copy-start.4
  38.5 0.7 copy-start.3
  40.7 1.0 copy-start.4
  41.7 0.7 copy-start.3
  43.9 1.0 copy-start.4
  78.7 118.3 %copy-start.1 = (f32[64,1536]{1,0:T(8,128)S(1)}, f32[64,1536]{1,0:T(8,128)}, u32[]{:S(2)}) copy-start(f32[64,1536]{1,0:T(8,128)} %tile.10) | copy-start | bytes 1179652
  78.8 118.2 %collective-permute-start.2 = (f32[64,1536]{1,0:T(8,128)S(1)}, f32[64,1536]{1,0:T(8,128)S(1)}, u32[]{:S(2)}, u32[]{:S(2)}) collective-permute-start(f32[64,1536]{1,0:T(8,128)S(1)} %get-tuple-element.183), channel_id=1, source_target_pairs={{0,508},{4,0},{8,4},{12,8},{16,12},{20,16},{24,20},{28,24},{32,28}... | collective-permute-start | bytes 1179656 | tf_op jit(solution)/shard_map/ppermute | solution.py:22
  88.3 108.7 %collective-permute-start.3 = (f32[64,1536]{1,0:T(8,128)S(1)}, f32[64,1536]{1,0:T(8,128)}, u32[]{:S(2)}, u32[]{:S(2)}) collective-permute-start(f32[64,1536]{1,0:T(8,128)S(1)} %get-tuple-element.184), channel_id=1, source_target_pairs={{0,4},{4,8},{8,12},{12,16},{16,20},{20,24},{24,28},{28,32},{32,36}... | collective-permute-start | bytes 1179656 | tf_op jit(solution)/shard_map/ppermute | solution.py:22
  199.6 101.0 %copy-start.2 = (f32[64,1536]{1,0:T(8,128)}, f32[64,1536]{1,0:T(8,128)S(1)}, u32[]{:S(2)}) copy-start(f32[64,1536]{1,0:T(8,128)S(1)} %get-tuple-element.182) | copy-start | bytes 1179652
where the time goes:
time: 302 us; the launch traced here: 301 us
  blocking collectives  204 us (68%)
  matrix products  31.6 us (10%)
  local copies, waits for them, and re-layouts  28.4 us (9%)
  starting transfers between devices  22.1 us (7%)
  other arithmetic  8.65 us (3%)
  between operations  3.46 us (1%)
    psum x1, blocking collectives, on_device(): norm_old = lax.psum(jnp.sum(incident * incident), ('cells', 'dirs'))  105 us
    psum x1, blocking collectives, on_device(): norm_new = lax.psum(jnp.sum(residual * dual_residual), ('cells', 'dirs'))  98.7 us
    ppermute x2, starting transfers between devices, passed_along(): lax.ppermute(x, axis, [(i, (i + by) % devices) for i in range(devices)])  11.4 us
    dot_general x8, matrix products, dual_step(): lax.dot_general(block, moved.reshape(spheres, columns), (((0,), (0,)), ((...  10.7 us
    while x32, local copies, waits for them, and re-layouts  10.3 us
    dot_general x8, matrix products, dual_step(): lax.dot_general(flat_weighted, operator, (((1,), (1,)), ((), ())), prefer...  9.11 us
    dot_general x8, matrix products, primal_step(): jnp.dot(summed.reshape(spheres * groups, order), operator, preferred_elem...  8.88 us
    ppermute x1, starting transfers between devices, extended(): after = lax.ppermute(leading, axis, down)  8.79 us
  transfers between devices with their start and end apart: 4, of which 1 were waited for; matrix products, arithmetic and copies ran while one was open for 2% of the time, Pallas kernels for 0%

commit v1 on v0

v1 whole, which is shorter than its diff:
```python
import jax
import jax.numpy as jnp
from jax import lax
from jax.sharding import PartitionSpec as P


def passed_along(x, axis, by):
    devices = lax.axis_size(axis)
    return lax.ppermute(x, axis, [(i, (i + by) % devices) for i in range(devices)])


def butterfly_sum(v, axes):
    for axis in axes:
        devices = lax.axis_size(axis)
        bit = 1
        while bit < devices:
            v = v + lax.ppermute(v, axis, [(i, i ^ bit) for i in range(devices)])
            bit *= 2
    return v


def on_device(incident, scattering, translations, pair_sphere, pair_class, pair_weight, pair_mask):
    spheres = incident.shape[0]
    columns = incident.shape[1]
    order = translations.shape[1]
    groups = columns // order
    classes = translations.shape[0]
    slots = pair_sphere.shape[1]
    band = spheres // 2
    extent = spheres + 2 * band
    position = lax.axis_index("cells")
    cell_count = lax.axis_size("cells")

    source = incident.astype(jnp.bfloat16)
    from_prev_rows = passed_along(source[spheres - band :], "cells", 1)
    from_next_rows = passed_along(source[:band], "cells", -1)

    owner = pair_sphere // spheres
    within = pair_sphere % spheres
    offset = (owner - position) % cell_count
    column = jnp.where(
        offset == 0,
        band + within,
        jnp.where(offset == 1, band + spheres + within, within - (spheres - band)),
    )
    placed = (column[:, :, None] == jnp.arange(extent, dtype=jnp.int32)[None, None, :]).astype(
        jnp.bfloat16
    )
    strength = pair_weight.astype(jnp.float32) * pair_mask.astype(jnp.float32)
    chosen = pair_class[:, :, None] == jnp.arange(classes, dtype=jnp.int32)[None, None, :]
    coupling = jnp.where(chosen, strength[:, :, None], jnp.float32(0.0)).astype(jnp.bfloat16)
    blocks = jnp.einsum("smk,sme->kse", coupling, placed, preferred_element_type=jnp.float32)
    blocks_half = blocks.astype(jnp.bfloat16)

    gain = jnp.tile(scattering, (1, groups))
    weighted = (gain * incident).astype(jnp.bfloat16).reshape(spheres, groups, order)
    moved = jnp.einsum(
        "sdc,kfc->ksdf", weighted, translations, preferred_element_type=jnp.float32
    ).reshape(classes, spheres, columns)
    contrib = jnp.einsum(
        "kse,ksx->ex",
        blocks,
        moved,
        precision=lax.Precision.HIGHEST,
        preferred_element_type=jnp.float32,
    )
    from_next = passed_along(contrib[:band], "cells", -1)
    from_prev = passed_along(contrib[band + spheres :], "cells", 1)

    padded = jnp.concatenate([from_prev_rows, source, from_next_rows], axis=0)
    gathered = jnp.einsum(
        "kse,ex->ksx", blocks_half, padded, preferred_element_type=jnp.float32
    ).astype(jnp.bfloat16)
    coupled = jnp.einsum(
        "ksdc,kcf->sdf",
        gathered.reshape(classes, spheres, groups, order),
        translations,
        preferred_element_type=jnp.float32,
    ).reshape(spheres, columns)

    back = contrib[band : band + spheres]
    back = back.at[spheres - band :].add(from_next)
    back = back.at[:band].add(from_prev)

    scattered = gain * coupled
    image = incident - scattered
    dual_image = incident - back

    partial = jnp.stack(
        [
            jnp.sum(incident * incident),
            jnp.sum(incident * scattered),
            jnp.sum(incident * back),
            jnp.sum(scattered * back),
        ]
    )
    total = butterfly_sum(partial, ("cells", "dirs"))
    norm_old = total[0]
    cross_u = total[1]
    cross_v = total[2]
    cross_uv = total[3]
    curvature = norm_old - cross_u
    step_size = norm_old / curvature
    keep = -cross_u / curvature
    norm_new = keep * keep * norm_old + keep * step_size * (cross_u + cross_v) + step_size * step_size * cross_uv

    solution = step_size * incident
    residual = incident - step_size * image
    dual_residual = incident - step_size * dual_image
    direction = residual + norm_new / norm_old * incident
    return (solution, residual, dual_residual, direction)


def solution(mesh):
    placed = (
        P("cells", "dirs"),
        P("cells", None),
        P(),
        P("cells", None),
        P("cells", None),
        P("cells", None),
        P("cells", None),
    )
    return jax.shard_map(
        on_device,
        mesh=mesh,
        in_specs=placed,
        out_specs=(P("cells", "dirs"), P("cells", "dirs"), P("cells", "dirs"), P("cells", "dirs")),
        check_vma=False,
    )
```

time: 302 us -> 126 us (0.42)
  the two profiles are of different devices: /device:TPU:1 before, /device:TPU:2 now
where the time goes in v1:
time: 126 us; the launch traced here: 125 us
  starting transfers between devices  46.3 us (37%)
  waiting for transfers between devices  36.4 us (29%)
  other arithmetic  13.2 us (10%)
  local copies, waits for them, and re-layouts  11.8 us (9%)
  matrix products  10.7 us (8%)
  between operations  6.84 us (5%)
    ppermute x9, waiting for transfers between devices, butterfly_sum(): v = v + lax.ppermute(v, axis, [(i, i ^ bit) for i in range(devices)])  36.3 us
    ppermute x9, starting transfers between devices, butterfly_sum(): v = v + lax.ppermute(v, axis, [(i, i ^ bit) for i in range(devices)])  26.6 us
    ppermute x4, starting transfers between devices, passed_along(): lax.ppermute(x, axis, [(i, (i + by) % devices) for i in range(devices)])  19.7 us
    add x9, other arithmetic, butterfly_sum(): v = v + lax.ppermute(v, axis, [(i, i ^ bit) for i in range(devices)])  5.35 us
    reshape x1, local copies, waits for them, and re-layouts, on_device(): moved = jnp.einsum('sdc,kfc->ksdf', weighted, translations, preferred_ele...  5.24 us
    dot_general x1, matrix products, on_device(): jnp.einsum('kse,ksx->ex', blocks, moved, precision=lax.Precision.HIGHEST,...  3.74 us
    dot_general x1, matrix products, on_device(): jnp.einsum('sdc,kfc->ksdf', weighted, translations, preferred_element_typ...  2.71 us
    reshape x1, local copies, waits for them, and re-layouts, on_device(): gathered.reshape(classes, spheres, groups, order)  2.67 us
  transfers between devices with their start and end apart: 13, of which 10 were waited for; matrix products, arithmetic and copies ran while one was open for 17% of the time, Pallas kernels for 0%

profile of v1, /device:TPU:2, one launch (start us, length us, event | category | flops | bytes accessed | tf_op | source)
XLA Modules:
  0.0 125.3 jit_solution(1828448618770019105)
XLA Ops:
  0.6 0.9 tile.4
  1.6 0.2 tile.10
  1.8 1.2 multiply_convert_fusion
  3.0 1.9 %collective-permute-start = (bf16[32,1536]{1,0:T(8,128)(2,1)S(1)}, bf16[32,1536]{1,0:T(8,128)(2,1)}, u32[]{:S(2)}, u32[]{:S(2)}) collective-permute-start(bf16[32,1536]{1,0:T(8,128)(2,1)S(1)} %get-tuple-element.42), channel_id=1, source_target_pairs={{0,4},{4,8},{8,12},{12,16},{16,20},{20,24},{24,28},{28,32},{32,36}... | collective-permute-start | bytes 294920 | tf_op jit(solution)/shard_map/ppermute | solution.py:9
  4.9 13.3 %collective-permute-start.1 = (bf16[32,1536]{1,0:T(8,128)(2,1)S(1)}, bf16[32,1536]{1,0:T(8,128)(2,1)S(1)}, u32[]{:S(2)}, u32[]{:S(2)}) collective-permute-start(bf16[32,1536]{1,0:T(8,128)(2,1)S(1)} %get-tuple-element.43), channel_id=1, source_target_pairs={{0,508},{4,0},{8,4},{12,8},{16,12},{20,16},{24,20},{28,24},{32,28}... | collective-permute-start | bytes 294920 | tf_op jit(solution)/shard_map/ppermute | solution.py:9
  18.2 0.2 reshape.83
  18.5 2.7 %convolution_bitcast_fusion.1 = f32[8,64,8,192]{3,2,0,1:T(8,128)} fusion(bf16[8,192,192]{2,1,0:T(8,128)(2,1)S(1)} %copy-done, bf16[64,8,192,1]{2,1,0,3:T(8,128)(2,1)S(1)} %reshape.83), kind=kOutput, calls=%fused_computation.2 | convolution fusion | flops 301989888 | bytes 3932160 | tf_op jit(solution)/shard_map/sdc,kfc->ksdf/dot_general | solution.py:57
  21.2 5.2 %reshape.79 = f32[8,64,1536]{2,0,1:T(8,128)} reshape(f32[8,64,8,192]{3,2,0,1:T(8,128)} %convolution_bitcast_fusion.1) | data formatting | bytes 6291456 | tf_op jit(solution)/shard_map/reshape | solution.py:59
  26.4 0.1 copy.11
  26.5 0.1 copy.12
  26.6 0.1 copy.13
  26.7 0.5 fusion.22
  27.3 3.7 %convolution_bitcast_fusion = f32[128,1536]{1,0:T(8,128)S(1)} fusion(f32[8,64,128]{2,0,1:T(8,128)S(1)} %get-tuple-element.49, f32[8,64,1536]{2,0,1:T(8,128)} %reshape.79), kind=kOutput, calls=%fused_computation.1 | convolution fusion | flops 1207959552 | bytes 4194304 | tf_op jit(solution)/shard_map/kse,ksx->ex/dot_general | solution.py:60
  31.0 0.8 fusion.19
  31.8 2.6 %collective-permute-start.2 = (f32[32,1536]{1,0:T(8,128)}, f32[32,1536]{1,0:T(8,128)}, u32[]{:S(2)}, u32[]{:S(2)}) collective-permute-start(f32[32,1536]{1,0:T(8,128)} %get-tuple-element.35), channel_id=1, source_target_pairs={{0,508},{4,0},{8,4},{12,8},{16,12},{20,16},{24,20},{28,24},{32,28}... | collective-permute-start | bytes 589832 | tf_op jit(solution)/shard_map/ppermute | solution.py:9
  34.4 1.9 %collective-permute-start.3 = (f32[32,1536]{1,0:T(8,128)S(1)}, f32[32,1536]{1,0:T(8,128)}, u32[]{:S(2)}, u32[]{:S(2)}) collective-permute-start(f32[32,1536]{1,0:T(8,128)S(1)} %get-tuple-element.34), channel_id=1, source_target_pairs={{0,4},{4,8},{8,12},{12,16},{16,20},{20,24},{24,28},{28,32},{32,36}... | collective-permute-start | bytes 589832 | tf_op jit(solution)/shard_map/ppermute | solution.py:9
  36.4 0.6 copy-done.3
  37.1 1.5 %convolution_convert_fusion = bf16[8,64,1536]{2,1,0:T(8,128)(2,1)S(1)} fusion(bf16[32,1536]{1,0:T(8,128)(2,1)} %copy-done.3, bf16[64,1536]{1,0:T(8,128)(2,1)S(1)} %get-tuple-element.41, bf16[32,1536]{1,0:T(8,128)(2,1)} %collective-permute-done, bf16[8,64,128]{2,0,1:T(8,128)(2,1)S(1)} %get-tuple-element.48), kind=kOutput, calls=%fused_computation | convolution fusion | flops 203292672 | bytes 2097152 | tf_op jit(solution)/shard_map/kse,ex->ksx/dot_general | solution.py:71
  38.6 2.7 %reshape.76 = bf16[8,64,8,192]{3,2,1,0:T(8,128)(2,1)} reshape(bf16[8,64,1536]{2,1,0:T(8,128)(2,1)S(1)} %convolution_convert_fusion) | data formatting | bytes 3145728 | tf_op jit(solution)/shard_map/reshape | solution.py:76
  41.2 2.3 %convolution_bitcast_fusion.2 = f32[64,8,192]{2,1,0:T(8,128)S(1)} fusion(bf16[8,64,8,192]{3,2,1,0:T(8,128)(2,1)} %reshape.76, bf16[8,192,192]{2,1,0:T(8,128)(2,1)S(1)} %copy-done), kind=kOutput, calls=%fused_computation.3 | convolution fusion | flops 301989888 | bytes 2555904 | tf_op jit(solution)/shard_map/ksdc,kcf->sdf/dot_general | solution.py:74
  43.5 0.2 reshape.77
  43.7 1.0 fusion.9
  44.7 0.1 collective-permute-done.3
  44.8 1.0 fusion.8
  45.8 0.8 multiply_reduce_fusion.2
  46.6 2.7 %pad_maximum_fusion = f32[4]{0:T(128)S(1)} fusion(f32[1]{0:T(128)} %bitcast.11, f32[1]{0:T(128)} %bitcast.10, f32[1]{0:T(128)} %bitcast.6, f32[1]{0:T(128)} %bitcast), kind=kLoop, calls=%fused_computation.48 | loop fusion | flops 12 | bytes 32 | tf_op jit(solution)/shard_map/stack | solution.py:89
  49.3 1.9 %collective-permute-start.4 = (f32[4]{0:T(128)S(1)}, f32[4]{0:T(128)S(1)}, u32[]{:S(2)}, u32[]{:S(2)}) collective-permute-start(f32[4]{0:T(128)S(1)} %pad_maximum_fusion), channel_id=1, source_target_pairs={{0,4},{4,0},{8,12},{12,8},{16,20},{20,16},{24,28},{28,24},{32,36},... | collective-permute-start | bytes 56 | tf_op jit(solution)/shard_map/ppermute | solution.py:17
  51.2 1.1 collective-permute-done.4
  52.3 2.7 %fusion.26 = f32[4]{0:T(128)S(1)} fusion(f32[4]{0:T(128)S(1)} %collective-permute-done.4, f32[1]{0:T(128)} %bitcast.11, f32[1]{0:T(128)} %bitcast.10, f32[1]{0:T(128)} %bitcast.6, f32[1]{0:T(128)} %bitcast), kind=kLoop, calls=%fused_computation.55 | loop fusion | flops 16 | bytes 48 | tf_op jit(solution)/shard_map/add | solution.py:17
  54.9 1.9 %collective-permute-start.5 = (f32[4]{0:T(128)S(1)}, f32[4]{0:T(128)S(1)}, u32[]{:S(2)}, u32[]{:S(2)}) collective-permute-start(f32[4]{0:T(128)S(1)} %fusion.26), channel_id=1, source_target_pairs={{0,8},{4,12},{8,0},{12,4},{16,24},{20,28},{24,16},{28,20},{32,40},... | collective-permute-start | bytes 56 | tf_op jit(solution)/shard_map/ppermute | solution.py:17
  56.9 3.5 %collective-permute-done.5 = f32[4]{0:T(128)S(1)} collective-permute-done((f32[4]{0:T(128)S(1)}, f32[4]{0:T(128)S(1)}, u32[]{:S(2)}, u32[]{:S(2)}) %collective-permute-start.5) | collective-permute-done | bytes 48 | tf_op jit(solution)/shard_map/ppermute | solution.py:17
  60.4 2.7 %fusion.27 = f32[4]{0:T(128)S(1)} fusion(f32[4]{0:T(128)S(1)} %collective-permute-done.5, f32[4]{0:T(128)S(1)} %collective-permute-done.4, f32[1]{0:T(128)} %bitcast.11, f32[1]{0:T(128)} %bitcast.10, f32[1]{0:T(128)} %bitcast.6, f32[1]{0:T(128)} %bitcast), kind=kLoop, calls=%fused_computation.56 | loop fusion | flops 20 | bytes 64 | tf_op jit(solution)/shard_map/add | solution.py:17
  63.0 1.9 %collective-permute-start.6 = (f32[4]{0:T(128)S(1)}, f32[4]{0:T(128)S(1)}, u32[]{:S(2)}, u32[]{:S(2)}) collective-permute-start(f32[4]{0:T(128)S(1)} %fusion.27), channel_id=1, source_target_pairs={{0,16},{4,20},{8,24},{12,28},{16,0},{20,4},{24,8},{28,12},{32,48},... | collective-permute-start | bytes 56 | tf_op jit(solution)/shard_map/ppermute | solution.py:17
  65.0 4.4 %collective-permute-done.6 = f32[4]{0:T(128)S(1)} collective-permute-done((f32[4]{0:T(128)S(1)}, f32[4]{0:T(128)S(1)}, u32[]{:S(2)}, u32[]{:S(2)}) %collective-permute-start.6) | collective-permute-done | bytes 48 | tf_op jit(solution)/shard_map/ppermute | solution.py:17
  69.4 3.1 %collective-permute-start.7 = (f32[4]{0:T(128)S(1)}, f32[4]{0:T(128)S(1)}, u32[]{:S(2)}, u32[]{:S(2)}) collective-permute-start(f32[4]{0:T(128)S(1)} %add.83), channel_id=1, source_target_pairs={{0,32},{4,36},{8,40},{12,44},{16,48},{20,52},{24,56},{28,60},{32,0... | collective-permute-start | bytes 56 | tf_op jit(solution)/shard_map/ppermute | solution.py:17
  72.4 6.2 %collective-permute-done.7 = f32[4]{0:T(128)S(1)} collective-permute-done((f32[4]{0:T(128)S(1)}, f32[4]{0:T(128)S(1)}, u32[]{:S(2)}, u32[]{:S(2)}) %collective-permute-start.7) | collective-permute-done | bytes 48 | tf_op jit(solution)/shard_map/ppermute | solution.py:17
  78.7 7.0 %collective-permute-start.8 = (f32[4]{0:T(128)S(1)}, f32[4]{0:T(128)S(1)}, u32[]{:S(2)}, u32[]{:S(2)}) collective-permute-start(f32[4]{0:T(128)S(1)} %add.84), channel_id=1, source_target_pairs={{0,64},{4,68},{8,72},{12,76},{16,80},{20,84},{24,88},{28,92},{32,9... | collective-permute-start | bytes 56 | tf_op jit(solution)/shard_map/ppermute | solution.py:17
  85.7 7.1 %collective-permute-done.8 = f32[4]{0:T(128)S(1)} collective-permute-done((f32[4]{0:T(128)S(1)}, f32[4]{0:T(128)S(1)}, u32[]{:S(2)}, u32[]{:S(2)}) %collective-permute-start.8) | collective-permute-done | bytes 48 | tf_op jit(solution)/shard_map/ppermute | solution.py:17
  92.8 1.9 %collective-permute-start.9 = (f32[4]{0:T(128)S(1)}, f32[4]{0:T(128)S(1)}, u32[]{:S(2)}, u32[]{:S(2)}) collective-permute-start(f32[4]{0:T(128)S(1)} %add.85), channel_id=1, source_target_pairs={{0,128},{4,132},{8,136},{12,140},{16,144},{20,148},{24,152},{28,15... | collective-permute-start | bytes 56 | tf_op jit(solution)/shard_map/ppermute | solution.py:17
  94.8 3.5 %collective-permute-done.9 = f32[4]{0:T(128)S(1)} collective-permute-done((f32[4]{0:T(128)S(1)}, f32[4]{0:T(128)S(1)}, u32[]{:S(2)}, u32[]{:S(2)}) %collective-permute-start.9) | collective-permute-done | bytes 48 | tf_op jit(solution)/shard_map/ppermute | solution.py:17
  98.3 2.4 %collective-permute-start.10 = (f32[4]{0:T(128)S(1)}, f32[4]{0:T(128)S(1)}, u32[]{:S(2)}, u32[]{:S(2)}) collective-permute-start(f32[4]{0:T(128)S(1)} %add.86), channel_id=1, source_target_pairs={{0,256},{4,260},{8,264},{12,268},{16,272},{20,276},{24,280},{28,28... | collective-permute-start | bytes 56 | tf_op jit(solution)/shard_map/ppermute | solution.py:17
  100.7 4.5 %collective-permute-done.10 = f32[4]{0:T(128)S(1)} collective-permute-done((f32[4]{0:T(128)S(1)}, f32[4]{0:T(128)S(1)}, u32[]{:S(2)}, u32[]{:S(2)}) %collective-permute-start.10) | collective-permute-done | bytes 48 | tf_op jit(solution)/shard_map/ppermute | solution.py:17
  105.2 2.4 %collective-permute-start.11 = (f32[4]{0:T(128)S(1)}, f32[4]{0:T(128)S(1)}, u32[]{:S(2)}, u32[]{:S(2)}) collective-permute-start(f32[4]{0:T(128)S(1)} %add.87), channel_id=1, source_target_pairs={{0,1},{1,0},{2,3},{3,2},{4,5},{5,4},{6,7},{7,6},{8,9},{9,8},{10,11... | collective-permute-start | bytes 56 | tf_op jit(solution)/shard_map/ppermute | solution.py:17
  107.6 3.0 %collective-permute-done.11 = f32[4]{0:T(128)S(1)} collective-permute-done((f32[4]{0:T(128)S(1)}, f32[4]{0:T(128)S(1)}, u32[]{:S(2)}, u32[]{:S(2)}) %collective-permute-start.11) | collective-permute-done | bytes 48 | tf_op jit(solution)/shard_map/ppermute | solution.py:17
  110.6 4.0 %collective-permute-start.12 = (f32[4]{0:T(128)S(1)}, f32[4]{0:T(128)S(1)}, u32[]{:S(2)}, u32[]{:S(2)}) collective-permute-start(f32[4]{0:T(128)S(1)} %add.88), channel_id=1, source_target_pairs={{0,2},{1,3},{2,0},{3,1},{4,6},{5,7},{6,4},{7,5},{8,10},{9,11},{10,... | collective-permute-start | bytes 56 | tf_op jit(solution)/shard_map/ppermute | solution.py:17
  114.6 2.9 %collective-permute-done.12 = f32[4]{0:T(128)S(1)} collective-permute-done((f32[4]{0:T(128)S(1)}, f32[4]{0:T(128)S(1)}, u32[]{:S(2)}, u32[]{:S(2)}) %collective-permute-start.12) | collective-permute-done | bytes 48 | tf_op jit(solution)/shard_map/ppermute | solution.py:17
  117.5 0.6 fusion.21
  124.1 1.2 multiply_subtract_fusion
  (29 shorter events, 0.1 us)
Async XLA Ops:
  0.6 17.8 %copy-start = (bf16[8,192,192]{2,1,0:T(8,128)(2,1)S(1)}, bf16[8,192,192]{2,1,0:T(8,128)(2,1)}, u32[]{:S(2)}) copy-start(bf16[8,192,192]{2,1,0:T(8,128)(2,1)} %param.13) | copy-start | bytes 1769476
  3.0 33.4 %collective-permute-start = (bf16[32,1536]{1,0:T(8,128)(2,1)S(1)}, bf16[32,1536]{1,0:T(8,128)(2,1)}, u32[]{:S(2)}, u32[]{:S(2)}) collective-permute-start(bf16[32,1536]{1,0:T(8,128)(2,1)S(1)} %get-tuple-element.42), channel_id=1, source_target_pairs={{0,4},{4,8},{8,12},{12,16},{16,20},{20,24},{24,28},{28,32},{32,36}... | collective-permute-start | bytes 294920 | tf_op jit(solution)/shard_map/ppermute | solution.py:9
  4.9 31.5 %collective-permute-start.1 = (bf16[32,1536]{1,0:T(8,128)(2,1)S(1)}, bf16[32,1536]{1,0:T(8,128)(2,1)S(1)}, u32[]{:S(2)}, u32[]{:S(2)}) collective-permute-start(bf16[32,1536]{1,0:T(8,128)(2,1)S(1)} %get-tuple-element.43), channel_id=1, source_target_pairs={{0,508},{4,0},{8,4},{12,8},{16,12},{20,16},{24,20},{28,24},{32,28}... | collective-permute-start | bytes 294920 | tf_op jit(solution)/shard_map/ppermute | solution.py:9
  21.2 5.3 %copy-start.5 = (s32[64,16]{0,1:T(8,128)S(1)}, s32[64,16]{0,1:T(8,128)}, u32[]{:S(2)}) copy-start(s32[64,16]{0,1:T(8,128)} %param.14) | copy-start | bytes 12292
  21.2 5.4 %copy-start.4 = (s32[64,16]{0,1:T(8,128)S(1)}, s32[64,16]{0,1:T(8,128)}, u32[]{:S(2)}) copy-start(s32[64,16]{0,1:T(8,128)} %param.15) | copy-start | bytes 12292
  21.2 5.4 %copy-start.6 = (s32[64,16]{0,1:T(8,128)S(1)}, s32[64,16]{0,1:T(8,128)}, u32[]{:S(2)}) copy-start(s32[64,16]{0,1:T(8,128)} %param.17) | copy-start | bytes 12292
  21.2 5.4 %copy-start.7 = (bf16[64,16]{0,1:T(8,128)(2,1)S(1)}, bf16[64,16]{0,1:T(8,128)(2,1)}, u32[]{:S(2)}) copy-start(bf16[64,16]{0,1:T(8,128)(2,1)} %param.16) | copy-start | bytes 6148
  31.0 5.4 %copy-start.1 = (f32[128,1536]{1,0:T(8,128)}, f32[128,1536]{1,0:T(8,128)S(1)}, u32[]{:S(2)}) copy-start(f32[128,1536]{1,0:T(8,128)S(1)} %convolution_bitcast_fusion) | copy-start | bytes 2359300
  31.8 11.8 %collective-permute-start.2 = (f32[32,1536]{1,0:T(8,128)}, f32[32,1536]{1,0:T(8,128)}, u32[]{:S(2)}, u32[]{:S(2)}) collective-permute-start(f32[32,1536]{1,0:T(8,128)} %get-tuple-element.35), channel_id=1, source_target_pairs={{0,508},{4,0},{8,4},{12,8},{16,12},{20,16},{24,20},{28,24},{32,28}... | collective-permute-start | bytes 589832 | tf_op jit(solution)/shard_map/ppermute | solution.py:9
  34.4 10.4 %collective-permute-start.3 = (f32[32,1536]{1,0:T(8,128)S(1)}, f32[32,1536]{1,0:T(8,128)}, u32[]{:S(2)}, u32[]{:S(2)}) collective-permute-start(f32[32,1536]{1,0:T(8,128)S(1)} %get-tuple-element.34), channel_id=1, source_target_pairs={{0,4},{4,8},{8,12},{12,16},{16,20},{20,24},{24,28},{28,32},{32,36}... | collective-permute-start | bytes 589832 | tf_op jit(solution)/shard_map/ppermute | solution.py:9
  36.4 0.6 copy-start.3
  41.2 4.6 %copy-start.2 = (f32[64,1536]{1,0:T(8,128)S(1)}, f32[64,1536]{1,0:T(8,128)}, u32[]{:S(2)}) copy-start(f32[64,1536]{1,0:T(8,128)} %param.11) | copy-start | bytes 1179652
  49.3 3.0 %collective-permute-start.4 = (f32[4]{0:T(128)S(1)}, f32[4]{0:T(128)S(1)}, u32[]{:S(2)}, u32[]{:S(2)}) collective-permute-start(f32[4]{0:T(128)S(1)} %pad_maximum_fusion), channel_id=1, source_target_pairs={{0,4},{4,0},{8,12},{12,8},{16,20},{20,16},{24,28},{28,24},{32,36},... | collective-permute-start | bytes 56 | tf_op jit(solution)/shard_map/ppermute | solution.py:17
  54.9 5.4 %collective-permute-start.5 = (f32[4]{0:T(128)S(1)}, f32[4]{0:T(128)S(1)}, u32[]{:S(2)}, u32[]{:S(2)}) collective-permute-start(f32[4]{0:T(128)S(1)} %fusion.26), channel_id=1, source_target_pairs={{0,8},{4,12},{8,0},{12,4},{16,24},{20,28},{24,16},{28,20},{32,40},... | collective-permute-start | bytes 56 | tf_op jit(solution)/shard_map/ppermute | solution.py:17
  63.0 6.3 %collective-permute-start.6 = (f32[4]{0:T(128)S(1)}, f32[4]{0:T(128)S(1)}, u32[]{:S(2)}, u32[]{:S(2)}) collective-permute-start(f32[4]{0:T(128)S(1)} %fusion.27), channel_id=1, source_target_pairs={{0,16},{4,20},{8,24},{12,28},{16,0},{20,4},{24,8},{28,12},{32,48},... | collective-permute-start | bytes 56 | tf_op jit(solution)/shard_map/ppermute | solution.py:17
  69.4 9.3 %collective-permute-start.7 = (f32[4]{0:T(128)S(1)}, f32[4]{0:T(128)S(1)}, u32[]{:S(2)}, u32[]{:S(2)}) collective-permute-start(f32[4]{0:T(128)S(1)} %add.83), channel_id=1, source_target_pairs={{0,32},{4,36},{8,40},{12,44},{16,48},{20,52},{24,56},{28,60},{32,0... | collective-permute-start | bytes 56 | tf_op jit(solution)/shard_map/ppermute | solution.py:17
  78.7 14.1 %collective-permute-start.8 = (f32[4]{0:T(128)S(1)}, f32[4]{0:T(128)S(1)}, u32[]{:S(2)}, u32[]{:S(2)}) collective-permute-start(f32[4]{0:T(128)S(1)} %add.84), channel_id=1, source_target_pairs={{0,64},{4,68},{8,72},{12,76},{16,80},{20,84},{24,88},{28,92},{32,9... | collective-permute-start | bytes 56 | tf_op jit(solution)/shard_map/ppermute | solution.py:17
  92.8 5.4 %collective-permute-start.9 = (f32[4]{0:T(128)S(1)}, f32[4]{0:T(128)S(1)}, u32[]{:S(2)}, u32[]{:S(2)}) collective-permute-start(f32[4]{0:T(128)S(1)} %add.85), channel_id=1, source_target_pairs={{0,128},{4,132},{8,136},{12,140},{16,144},{20,148},{24,152},{28,15... | collective-permute-start | bytes 56 | tf_op jit(solution)/shard_map/ppermute | solution.py:17
  98.3 6.9 %collective-permute-start.10 = (f32[4]{0:T(128)S(1)}, f32[4]{0:T(128)S(1)}, u32[]{:S(2)}, u32[]{:S(2)}) collective-permute-start(f32[4]{0:T(128)S(1)} %add.86), channel_id=1, source_target_pairs={{0,256},{4,260},{8,264},{12,268},{16,272},{20,276},{24,280},{28,28... | collective-permute-start | bytes 56 | tf_op jit(solution)/shard_map/ppermute | solution.py:17
  105.2 5.4 %collective-permute-start.11 = (f32[4]{0:T(128)S(1)}, f32[4]{0:T(128)S(1)}, u32[]{:S(2)}, u32[]{:S(2)}) collective-permute-start(f32[4]{0:T(128)S(1)} %add.87), channel_id=1, source_target_pairs={{0,1},{1,0},{2,3},{3,2},{4,5},{5,4},{6,7},{7,6},{8,9},{9,8},{10,11... | collective-permute-start | bytes 56 | tf_op jit(solution)/shard_map/ppermute | solution.py:17
  110.6 6.9 %collective-permute-start.12 = (f32[4]{0:T(128)S(1)}, f32[4]{0:T(128)S(1)}, u32[]{:S(2)}, u32[]{:S(2)}) collective-permute-start(f32[4]{0:T(128)S(1)} %add.88), channel_id=1, source_target_pairs={{0,2},{1,3},{2,0},{3,1},{4,6},{5,7},{6,4},{7,5},{8,10},{9,11},{10,... | collective-permute-start | bytes 56 | tf_op jit(solution)/shard_map/ppermute | solution.py:17

commit v2 on v1

--- a/solution.py
+++ b/solution.py
@@ -54,16 +54,14 @@
 
     gain = jnp.tile(scattering, (1, groups))
     weighted = (gain * incident).astype(jnp.bfloat16).reshape(spheres, groups, order)
-    moved = jnp.einsum(
-        "sdc,kfc->ksdf", weighted, translations, preferred_element_type=jnp.float32
-    ).reshape(classes, spheres, columns)
+    moved = jnp.einsum("sdc,kfc->sdkf", weighted, translations, preferred_element_type=jnp.float32)
     contrib = jnp.einsum(
-        "kse,ksx->ex",
+        "kse,sdkf->edf",
         blocks,
         moved,
         precision=lax.Precision.HIGHEST,
         preferred_element_type=jnp.float32,
-    )
+    ).reshape(extent, columns)
     from_next = passed_along(contrib[:band], "cells", -1)
     from_prev = passed_along(contrib[band + spheres :], "cells", 1)
 
@@ -71,12 +69,14 @@
     gathered = jnp.einsum(
         "kse,ex->ksx", blocks_half, padded, preferred_element_type=jnp.float32
     ).astype(jnp.bfloat16)
-    coupled = jnp.einsum(
-        "ksdc,kcf->sdf",
-        gathered.reshape(classes, spheres, groups, order),
-        translations,
-        preferred_element_type=jnp.float32,
-    ).reshape(spheres, columns)
+    coupled = jnp.zeros((spheres * groups, order), jnp.float32)
+    for klass in range(classes):
+        coupled = coupled + jnp.dot(
+            gathered[klass].reshape(spheres * groups, order),
+            translations[klass],
+            preferred_element_type=jnp.float32,
+        )
+    coupled = coupled.reshape(spheres, columns)
 
     back = contrib[band : band + spheres]
     back = back.at[spheres - band :].add(from_next)
@@ -94,6 +94,7 @@
             jnp.sum(scattered * back),
         ]
     )
+    partial = lax.optimization_barrier(partial)
     total = butterfly_sum(partial, ("cells", "dirs"))
     norm_old = total[0]
     cross_u = total[1]

time: 126 us -> 134 us (1.063)
  the two profiles are of different devices: /device:TPU:2 before, /device:TPU:4 now
where the time goes in v2:
time: 134 us; the launch traced here: 133 us
  waiting for transfers between devices  43.6 us (33%)
  starting transfers between devices  43.5 us (32%)
  local copies, waits for them, and re-layouts  15 us (11%)
  matrix products  14.6 us (11%)
  other arithmetic  9.32 us (7%)
  between operations  6.87 us (5%)
    ppermute x9, waiting for transfers between devices, butterfly_sum(): v = v + lax.ppermute(v, axis, [(i, i ^ bit) for i in range(devices)])  43.6 us
    ppermute x4, starting transfers between devices, passed_along(): lax.ppermute(x, axis, [(i, (i + by) % devices) for i in range(devices)])  24.2 us
    ppermute x9, starting transfers between devices, butterfly_sum(): v = v + lax.ppermute(v, axis, [(i, i ^ bit) for i in range(devices)])  19.2 us
    dot_general x1, matrix products, on_device(): jnp.einsum('kse,sdkf->edf', blocks, moved, precision=lax.Precision.HIGHES...  8.26 us
    another operation x8, local copies, waits for them, and re-layouts, on_device(): gathered[klass].reshape(spheres * groups, order)  4.42 us
    dot_general x8, matrix products, on_device(): jnp.dot(gathered[klass].reshape(spheres * groups, order), translations[kl...  2.96 us
  transfers between devices with their start and end apart: 13, of which 9 were waited for; matrix products, arithmetic and copies ran while one was open for 22% of the time, Pallas kernels for 0%

profile of v2, /device:TPU:4, one launch (start us, length us, event | category | flops | bytes accessed | tf_op | source)
XLA Modules:
  0.0 132.9 jit_solution(14546411901603307319)
XLA Ops:
  0.6 0.9 tile.4
  1.8 1.2 multiply_convert_fusion
  3.0 0.7 fusion.44
  3.7 13.3 %collective-permute-start.1 = (bf16[32,1536]{1,0:T(8,128)(2,1)}, bf16[32,1536]{1,0:T(8,128)(2,1)}, u32[]{:S(2)}, u32[]{:S(2)}) collective-permute-start(bf16[32,1536]{1,0:T(8,128)(2,1)} %get-tuple-element.52), channel_id=1, source_target_pairs={{0,508},{4,0},{8,4},{12,8},{16,12},{20,16},{24,20},{28,24},{32,28}... | collective-permute-start | bytes 294920 | tf_op jit(solution)/shard_map/ppermute | solution.py:9
  17.0 1.9 %collective-permute-start = (bf16[32,1536]{1,0:T(8,128)(2,1)}, bf16[32,1536]{1,0:T(8,128)(2,1)}, u32[]{:S(2)}, u32[]{:S(2)}) collective-permute-start(bf16[32,1536]{1,0:T(8,128)(2,1)} %get-tuple-element.51), channel_id=1, source_target_pairs={{0,4},{4,8},{8,12},{12,16},{16,20},{20,24},{24,28},{28,32},{32,36}... | collective-permute-start | bytes 294920 | tf_op jit(solution)/shard_map/ppermute | solution.py:9
  19.2 0.7 convert_multiply_fusion
  20.0 0.8 copy.21
  20.8 0.7 select_select_fusion
  21.6 0.7 fusion.5
  22.3 1.0 bitcast_convert_fusion
  23.3 8.3 %fusion.2 = f32[128,8,192]{0,2,1:T(8,128)S(1)} fusion(f32[64,8,8,192]{3,0,2,1:T(8,128)S(1)} %fusion.5, f32[64,128,8]{1,2,0:T(8,128)S(1)} %get-tuple-element.58), kind=kOutput, calls=%fused_computation.3 | convolution fusion | flops 1207959552 | bytes 4194304 | tf_op jit(solution)/shard_map/kse,sdkf->edf/dot_general | solution.py:58
  31.6 1.3 %fusion.43 = (f32[32,8,192]{0,2,1:T(8,128)S(1)}, f32[32,8,192]{0,2,1:T(8,128)}, f32[32,8,192]{0,2,1:T(8,128)S(1)}) fusion(f32[128,8,192]{0,2,1:T(8,128)S(1)} %fusion.2), kind=kLoop, calls=%fused_computation.77 | loop fusion | bytes 1179648 | tf_op jit(solution)/shard_map/slice | solution.py:66
  32.9 2.1 %copy.26 = f32[32,1536]{1,0:T(8,128)} copy(f32[32,1536]{0,1:T(8,128)} %bitcast.61) | data formatting | bytes 393216 | tf_op jit(solution)/shard_map/slice | solution.py:65
  34.9 7.0 %collective-permute-start.2 = (f32[32,1536]{1,0:T(8,128)}, f32[32,1536]{1,0:T(8,128)}, u32[]{:S(2)}, u32[]{:S(2)}) collective-permute-start(f32[32,1536]{1,0:T(8,128)} %copy.26), channel_id=1, source_target_pairs={{0,508},{4,0},{8,4},{12,8},{16,12},{20,16},{24,20},{28,24},{32,28}... | collective-permute-start | bytes 589832 | tf_op jit(solution)/shard_map/ppermute | solution.py:9
  41.9 0.9 copy.29
  42.8 2.1 %collective-permute-start.3 = (f32[32,1536]{1,0:T(8,128)}, f32[32,1536]{1,0:T(8,128)}, u32[]{:S(2)}, u32[]{:S(2)}) collective-permute-start(f32[32,1536]{1,0:T(8,128)} %copy.29), channel_id=1, source_target_pairs={{0,4},{4,8},{8,12},{12,16},{16,20},{20,24},{24,28},{28,32},{32,36}... | collective-permute-start | bytes 589832 | tf_op jit(solution)/shard_map/ppermute | solution.py:9
  44.9 0.3 slice.164
  45.5 0.9 copy.27
  46.4 1.7 %convolution_convert_fusion = bf16[8,64,1536]{2,1,0:T(8,128)(2,1)S(1)} fusion(bf16[32,1536]{1,0:T(8,128)(2,1)} %collective-permute-done.1, bf16[64,1536]{1,0:T(8,128)(2,1)} %copy-done.2, bf16[32,1536]{1,0:T(8,128)(2,1)} %collective-permute-done, bf16[8,64,128]{2,0,1:T(8,128)(2,1)} %get-tuple-element.57), kind=kOutput, calls=%fused_computation.2 | convolution fusion | flops 203292672 | bytes 2097152 | tf_op jit(solution)/shard_map/kse,ex->ksx/dot_general | solution.py:69
  48.0 0.8 fusion.42
  49.4 1.2 reshape_squeeze.25
  50.5 0.9 reshape_squeeze.26
  52.4 1.2 reshape_squeeze.31
  53.8 1.2 convolution_add_fusion.5
  56.8 1.0 add_dynamic-update-slice_fusion
  57.8 1.0 fusion.15
  58.8 0.8 multiply_reduce_fusion.2
  59.6 2.7 %pad_maximum_fusion = f32[4]{0:T(128)S(1)} fusion(f32[1]{0:T(128)} %bitcast.21, f32[1]{0:T(128)} %bitcast.20, f32[1]{0:T(128)} %bitcast.11, f32[1]{0:T(128)} %bitcast), kind=kLoop, calls=%fused_computation.73 | loop fusion | flops 12 | bytes 32 | tf_op jit(solution)/shard_map/stack | solution.py:89
  62.3 1.9 %collective-permute-start.4 = (f32[4]{0:T(128)S(1)}, f32[4]{0:T(128)S(1)}, u32[]{:S(2)}, u32[]{:S(2)}) collective-permute-start(f32[4]{0:T(128)S(1)} %pad_maximum_fusion), channel_id=1, source_target_pairs={{0,4},{4,0},{8,12},{12,8},{16,20},{20,16},{24,28},{28,24},{32,36},... | collective-permute-start | bytes 56 | tf_op jit(solution)/shard_map/ppermute | solution.py:17
  64.2 1.1 collective-permute-done.4
  65.3 1.9 %collective-permute-start.5 = (f32[4]{0:T(128)S(1)}, f32[4]{0:T(128)S(1)}, u32[]{:S(2)}, u32[]{:S(2)}) collective-permute-start(f32[4]{0:T(128)S(1)} %add.109), channel_id=1, source_target_pairs={{0,8},{4,12},{8,0},{12,4},{16,24},{20,28},{24,16},{28,20},{32,40},... | collective-permute-start | bytes 56 | tf_op jit(solution)/shard_map/ppermute | solution.py:17
  67.2 3.5 %collective-permute-done.5 = f32[4]{0:T(128)S(1)} collective-permute-done((f32[4]{0:T(128)S(1)}, f32[4]{0:T(128)S(1)}, u32[]{:S(2)}, u32[]{:S(2)}) %collective-permute-start.5) | collective-permute-done | bytes 48 | tf_op jit(solution)/shard_map/ppermute | solution.py:17
  70.7 1.9 %collective-permute-start.6 = (f32[4]{0:T(128)S(1)}, f32[4]{0:T(128)S(1)}, u32[]{:S(2)}, u32[]{:S(2)}) collective-permute-start(f32[4]{0:T(128)S(1)} %add.110), channel_id=1, source_target_pairs={{0,16},{4,20},{8,24},{12,28},{16,0},{20,4},{24,8},{28,12},{32,48},... | collective-permute-start | bytes 56 | tf_op jit(solution)/shard_map/ppermute | solution.py:17
  72.6 4.4 %collective-permute-done.6 = f32[4]{0:T(128)S(1)} collective-permute-done((f32[4]{0:T(128)S(1)}, f32[4]{0:T(128)S(1)}, u32[]{:S(2)}, u32[]{:S(2)}) %collective-permute-start.6) | collective-permute-done | bytes 48 | tf_op jit(solution)/shard_map/ppermute | solution.py:17
  77.0 1.9 %collective-permute-start.7 = (f32[4]{0:T(128)S(1)}, f32[4]{0:T(128)S(1)}, u32[]{:S(2)}, u32[]{:S(2)}) collective-permute-start(f32[4]{0:T(128)S(1)} %add.111), channel_id=1, source_target_pairs={{0,32},{4,36},{8,40},{12,44},{16,48},{20,52},{24,56},{28,60},{32,0... | collective-permute-start | bytes 56 | tf_op jit(solution)/shard_map/ppermute | solution.py:17
  79.0 7.4 %collective-permute-done.7 = f32[4]{0:T(128)S(1)} collective-permute-done((f32[4]{0:T(128)S(1)}, f32[4]{0:T(128)S(1)}, u32[]{:S(2)}, u32[]{:S(2)}) %collective-permute-start.7) | collective-permute-done | bytes 48 | tf_op jit(solution)/shard_map/ppermute | solution.py:17
  86.4 2.3 %collective-permute-start.8 = (f32[4]{0:T(128)S(1)}, f32[4]{0:T(128)S(1)}, u32[]{:S(2)}, u32[]{:S(2)}) collective-permute-start(f32[4]{0:T(128)S(1)} %add.112), channel_id=1, source_target_pairs={{0,64},{4,68},{8,72},{12,76},{16,80},{20,84},{24,88},{28,92},{32,9... | collective-permute-start | bytes 56 | tf_op jit(solution)/shard_map/ppermute | solution.py:17
  88.6 11.9 %collective-permute-done.8 = f32[4]{0:T(128)S(1)} collective-permute-done((f32[4]{0:T(128)S(1)}, f32[4]{0:T(128)S(1)}, u32[]{:S(2)}, u32[]{:S(2)}) %collective-permute-start.8) | collective-permute-done | bytes 48 | tf_op jit(solution)/shard_map/ppermute | solution.py:17
  100.5 1.9 %collective-permute-start.9 = (f32[4]{0:T(128)S(1)}, f32[4]{0:T(128)S(1)}, u32[]{:S(2)}, u32[]{:S(2)}) collective-permute-start(f32[4]{0:T(128)S(1)} %add.113), channel_id=1, source_target_pairs={{0,128},{4,132},{8,136},{12,140},{16,144},{20,148},{24,152},{28,15... | collective-permute-start | bytes 56 | tf_op jit(solution)/shard_map/ppermute | solution.py:17
  102.4 3.5 %collective-permute-done.9 = f32[4]{0:T(128)S(1)} collective-permute-done((f32[4]{0:T(128)S(1)}, f32[4]{0:T(128)S(1)}, u32[]{:S(2)}, u32[]{:S(2)}) %collective-permute-start.9) | collective-permute-done | bytes 48 | tf_op jit(solution)/shard_map/ppermute | solution.py:17
  105.9 1.9 %collective-permute-start.10 = (f32[4]{0:T(128)S(1)}, f32[4]{0:T(128)S(1)}, u32[]{:S(2)}, u32[]{:S(2)}) collective-permute-start(f32[4]{0:T(128)S(1)} %add.114), channel_id=1, source_target_pairs={{0,256},{4,260},{8,264},{12,268},{16,272},{20,276},{24,280},{28,28... | collective-permute-start | bytes 56 | tf_op jit(solution)/shard_map/ppermute | solution.py:17
  107.9 5.0 %collective-permute-done.10 = f32[4]{0:T(128)S(1)} collective-permute-done((f32[4]{0:T(128)S(1)}, f32[4]{0:T(128)S(1)}, u32[]{:S(2)}, u32[]{:S(2)}) %collective-permute-start.10) | collective-permute-done | bytes 48 | tf_op jit(solution)/shard_map/ppermute | solution.py:17
  112.9 3.1 %collective-permute-start.11 = (f32[4]{0:T(128)S(1)}, f32[4]{0:T(128)S(1)}, u32[]{:S(2)}, u32[]{:S(2)}) collective-permute-start(f32[4]{0:T(128)S(1)} %add.115), channel_id=1, source_target_pairs={{0,1},{1,0},{2,3},{3,2},{4,5},{5,4},{6,7},{7,6},{8,9},{9,8},{10,11... | collective-permute-start | bytes 56 | tf_op jit(solution)/shard_map/ppermute | solution.py:17
  116.0 2.3 %collective-permute-done.11 = f32[4]{0:T(128)S(1)} collective-permute-done((f32[4]{0:T(128)S(1)}, f32[4]{0:T(128)S(1)}, u32[]{:S(2)}, u32[]{:S(2)}) %collective-permute-start.11) | collective-permute-done | bytes 48 | tf_op jit(solution)/shard_map/ppermute | solution.py:17
  118.3 2.4 %collective-permute-start.12 = (f32[4]{0:T(128)S(1)}, f32[4]{0:T(128)S(1)}, u32[]{:S(2)}, u32[]{:S(2)}) collective-permute-start(f32[4]{0:T(128)S(1)} %add.116), channel_id=1, source_target_pairs={{0,2},{1,3},{2,0},{3,1},{4,6},{5,7},{6,4},{7,5},{8,10},{9,11},{10,... | collective-permute-start | bytes 56 | tf_op jit(solution)/shard_map/ppermute | solution.py:17
  120.7 4.5 %collective-permute-done.12 = f32[4]{0:T(128)S(1)} collective-permute-done((f32[4]{0:T(128)S(1)}, f32[4]{0:T(128)S(1)}, u32[]{:S(2)}, u32[]{:S(2)}) %collective-permute-start.12) | collective-permute-done | bytes 48 | tf_op jit(solution)/shard_map/ppermute | solution.py:17
  125.2 0.6 fusion.45
  131.7 1.2 multiply_subtract_fusion
  (38 shorter events, 4.2 us)
Async XLA Ops:
  0.6 20.9 %copy-start.1 = (bf16[8,192,192]{2,1,0:T(8,128)(2,1)S(1)}, bf16[8,192,192]{2,1,0:T(8,128)(2,1)}, u32[]{:S(2)}) copy-start(bf16[8,192,192]{2,1,0:T(8,128)(2,1)} %param.13) | copy-start | bytes 1769476
  3.0 20.3 %copy-start.2 = (bf16[64,1536]{1,0:T(8,128)(2,1)}, bf16[64,1536]{1,0:T(8,128)(2,1)S(1)}, u32[]{:S(2)}) copy-start(bf16[64,1536]{1,0:T(8,128)(2,1)S(1)} %get-tuple-element.50) | copy-start | bytes 589828
  3.7 42.7 %collective-permute-start.1 = (bf16[32,1536]{1,0:T(8,128)(2,1)}, bf16[32,1536]{1,0:T(8,128)(2,1)}, u32[]{:S(2)}, u32[]{:S(2)}) collective-permute-start(bf16[32,1536]{1,0:T(8,128)(2,1)} %get-tuple-element.52), channel_id=1, source_target_pairs={{0,508},{4,0},{8,4},{12,8},{16,12},{20,16},{24,20},{28,24},{32,28}... | collective-permute-start | bytes 294920 | tf_op jit(solution)/shard_map/ppermute | solution.py:9
  17.0 29.4 %collective-permute-start = (bf16[32,1536]{1,0:T(8,128)(2,1)}, bf16[32,1536]{1,0:T(8,128)(2,1)}, u32[]{:S(2)}, u32[]{:S(2)}) collective-permute-start(bf16[32,1536]{1,0:T(8,128)(2,1)} %get-tuple-element.51), channel_id=1, source_target_pairs={{0,4},{4,8},{8,12},{12,16},{16,20},{20,24},{24,28},{28,32},{32,36}... | collective-permute-start | bytes 294920 | tf_op jit(solution)/shard_map/ppermute | solution.py:9
  34.9 21.8 %collective-permute-start.2 = (f32[32,1536]{1,0:T(8,128)}, f32[32,1536]{1,0:T(8,128)}, u32[]{:S(2)}, u32[]{:S(2)}) collective-permute-start(f32[32,1536]{1,0:T(8,128)} %copy.26), channel_id=1, source_target_pairs={{0,508},{4,0},{8,4},{12,8},{16,12},{20,16},{24,20},{28,24},{32,28}... | collective-permute-start | bytes 589832 | tf_op jit(solution)/shard_map/ppermute | solution.py:9
  42.8 15.0 %collective-permute-start.3 = (f32[32,1536]{1,0:T(8,128)}, f32[32,1536]{1,0:T(8,128)}, u32[]{:S(2)}, u32[]{:S(2)}) collective-permute-start(f32[32,1536]{1,0:T(8,128)} %copy.29), channel_id=1, source_target_pairs={{0,4},{4,8},{8,12},{12,16},{16,20},{20,24},{24,28},{28,32},{32,36}... | collective-permute-start | bytes 589832 | tf_op jit(solution)/shard_map/ppermute | solution.py:9
  55.1 3.7 %copy-start = (f32[64,1536]{1,0:T(8,128)S(1)}, f32[64,1536]{1,0:T(8,128)}, u32[]{:S(2)}) copy-start(f32[64,1536]{1,0:T(8,128)} %param.11) | copy-start | bytes 1179652
  62.3 3.0 %collective-permute-start.4 = (f32[4]{0:T(128)S(1)}, f32[4]{0:T(128)S(1)}, u32[]{:S(2)}, u32[]{:S(2)}) collective-permute-start(f32[4]{0:T(128)S(1)} %pad_maximum_fusion), channel_id=1, source_target_pairs={{0,4},{4,0},{8,12},{12,8},{16,20},{20,16},{24,28},{28,24},{32,36},... | collective-permute-start | bytes 56 | tf_op jit(solution)/shard_map/ppermute | solution.py:17
  65.3 5.4 %collective-permute-start.5 = (f32[4]{0:T(128)S(1)}, f32[4]{0:T(128)S(1)}, u32[]{:S(2)}, u32[]{:S(2)}) collective-permute-start(f32[4]{0:T(128)S(1)} %add.109), channel_id=1, source_target_pairs={{0,8},{4,12},{8,0},{12,4},{16,24},{20,28},{24,16},{28,20},{32,40},... | collective-permute-start | bytes 56 | tf_op jit(solution)/shard_map/ppermute | solution.py:17
  70.7 6.3 %collective-permute-start.6 = (f32[4]{0:T(128)S(1)}, f32[4]{0:T(128)S(1)}, u32[]{:S(2)}, u32[]{:S(2)}) collective-permute-start(f32[4]{0:T(128)S(1)} %add.110), channel_id=1, source_target_pairs={{0,16},{4,20},{8,24},{12,28},{16,0},{20,4},{24,8},{28,12},{32,48},... | collective-permute-start | bytes 56 | tf_op jit(solution)/shard_map/ppermute | solution.py:17
  77.0 9.3 %collective-permute-start.7 = (f32[4]{0:T(128)S(1)}, f32[4]{0:T(128)S(1)}, u32[]{:S(2)}, u32[]{:S(2)}) collective-permute-start(f32[4]{0:T(128)S(1)} %add.111), channel_id=1, source_target_pairs={{0,32},{4,36},{8,40},{12,44},{16,48},{20,52},{24,56},{28,60},{32,0... | collective-permute-start | bytes 56 | tf_op jit(solution)/shard_map/ppermute | solution.py:17
  86.4 14.1 %collective-permute-start.8 = (f32[4]{0:T(128)S(1)}, f32[4]{0:T(128)S(1)}, u32[]{:S(2)}, u32[]{:S(2)}) collective-permute-start(f32[4]{0:T(128)S(1)} %add.112), channel_id=1, source_target_pairs={{0,64},{4,68},{8,72},{12,76},{16,80},{20,84},{24,88},{28,92},{32,9... | collective-permute-start | bytes 56 | tf_op jit(solution)/shard_map/ppermute | solution.py:17
  100.5 5.4 %collective-permute-start.9 = (f32[4]{0:T(128)S(1)}, f32[4]{0:T(128)S(1)}, u32[]{:S(2)}, u32[]{:S(2)}) collective-permute-start(f32[4]{0:T(128)S(1)} %add.113), channel_id=1, source_target_pairs={{0,128},{4,132},{8,136},{12,140},{16,144},{20,148},{24,152},{28,15... | collective-permute-start | bytes 56 | tf_op jit(solution)/shard_map/ppermute | solution.py:17
  105.9 6.9 %collective-permute-start.10 = (f32[4]{0:T(128)S(1)}, f32[4]{0:T(128)S(1)}, u32[]{:S(2)}, u32[]{:S(2)}) collective-permute-start(f32[4]{0:T(128)S(1)} %add.114), channel_id=1, source_target_pairs={{0,256},{4,260},{8,264},{12,268},{16,272},{20,276},{24,280},{28,28... | collective-permute-start | bytes 56 | tf_op jit(solution)/shard_map/ppermute | solution.py:17
  112.9 5.4 %collective-permute-start.11 = (f32[4]{0:T(128)S(1)}, f32[4]{0:T(128)S(1)}, u32[]{:S(2)}, u32[]{:S(2)}) collective-permute-start(f32[4]{0:T(128)S(1)} %add.115), channel_id=1, source_target_pairs={{0,1},{1,0},{2,3},{3,2},{4,5},{5,4},{6,7},{7,6},{8,9},{9,8},{10,11... | collective-permute-start | bytes 56 | tf_op jit(solution)/shard_map/ppermute | solution.py:17
  118.3 6.9 %collective-permute-start.12 = (f32[4]{0:T(128)S(1)}, f32[4]{0:T(128)S(1)}, u32[]{:S(2)}, u32[]{:S(2)}) collective-permute-start(f32[4]{0:T(128)S(1)} %add.116), channel_id=1, source_target_pairs={{0,2},{1,3},{2,0},{3,1},{4,6},{5,7},{6,4},{7,5},{8,10},{9,11},{10,... | collective-permute-start | bytes 56 | tf_op jit(solution)/shard_map/ppermute | solution.py:17

commit v3 on v1

--- a/solution.py
+++ b/solution.py
@@ -1,22 +1,26 @@
 import jax
 import jax.numpy as jnp
 from jax import lax
-from jax.sharding import PartitionSpec as P
+from jax.sharding import Mesh, PartitionSpec as P
 
 
-def passed_along(x, axis, by):
-    devices = lax.axis_size(axis)
-    return lax.ppermute(x, axis, [(i, (i + by) % devices) for i in range(devices)])
+def passed_along(x, axes, by):
+    devices = 1
+    for axis in axes:
+        devices *= lax.axis_size(axis)
+    return lax.ppermute(x, axes, [(i, (i + by) % devices) for i in range(devices)])
 
 
-def butterfly_sum(v, axes):
+CELLS = ("y", "z", "core")
+DIRS = "x"
+
+
+def exchange_sum(v, axes):
+    members = 1
     for axis in axes:
-        devices = lax.axis_size(axis)
-        bit = 1
-        while bit < devices:
-            v = v + lax.ppermute(v, axis, [(i, i ^ bit) for i in range(devices)])
-            bit *= 2
-    return v
+        members *= lax.axis_size(axis)
+    spread = jnp.broadcast_to(v[None, :], (members,) + v.shape)
+    return jnp.sum(lax.all_to_all(spread, axes, 0, 0, tiled=True), axis=0)
 
 
 def on_device(incident, scattering, translations, pair_sphere, pair_class, pair_weight, pair_mask):
@@ -28,12 +32,12 @@
     slots = pair_sphere.shape[1]
     band = spheres // 2
     extent = spheres + 2 * band
-    position = lax.axis_index("cells")
-    cell_count = lax.axis_size("cells")
+    position = lax.axis_index(CELLS)
+    cell_count = lax.axis_size("y") * lax.axis_size("z") * lax.axis_size("core")
 
     source = incident.astype(jnp.bfloat16)
-    from_prev_rows = passed_along(source[spheres - band :], "cells", 1)
-    from_next_rows = passed_along(source[:band], "cells", -1)
+    from_prev_rows = passed_along(source[spheres - band :], CELLS, 1)
+    from_next_rows = passed_along(source[:band], CELLS, -1)
 
     owner = pair_sphere // spheres
     within = pair_sphere % spheres
@@ -64,8 +68,8 @@
         precision=lax.Precision.HIGHEST,
         preferred_element_type=jnp.float32,
     )
-    from_next = passed_along(contrib[:band], "cells", -1)
-    from_prev = passed_along(contrib[band + spheres :], "cells", 1)
+    from_next = passed_along(contrib[:band], CELLS, -1)
+    from_prev = passed_along(contrib[band + spheres :], CELLS, 1)
 
     padded = jnp.concatenate([from_prev_rows, source, from_next_rows], axis=0)
     gathered = jnp.einsum(
@@ -94,7 +98,8 @@
             jnp.sum(scattered * back),
         ]
     )
-    total = butterfly_sum(partial, ("cells", "dirs"))
+    partial = lax.optimization_barrier(partial)
+    total = exchange_sum(exchange_sum(partial, ("z", "core")), ("y", DIRS))
     norm_old = total[0]
     cross_u = total[1]
     cross_v = total[2]
@@ -111,20 +116,28 @@
     return (solution, residual, dual_residual, direction)
 
 
+def physical_mesh(mesh):
+    devices = mesh.devices
+    cores = len({d.core_on_chip for d in devices.flat})
+    rows = len({d.coords[1] for d in devices.flat})
+    depth = devices.shape[0] // (rows * cores)
+    return Mesh(devices.reshape(rows, depth, cores, devices.shape[1]), CELLS + (DIRS,))
+
+
 def solution(mesh):
     placed = (
-        P("cells", "dirs"),
-        P("cells", None),
+        P(CELLS, DIRS),
+        P(CELLS, None),
         P(),
-        P("cells", None),
-        P("cells", None),
-        P("cells", None),
-        P("cells", None),
+        P(CELLS, None),
+        P(CELLS, None),
+        P(CELLS, None),
+        P(CELLS, None),
     )
     return jax.shard_map(
         on_device,
-        mesh=mesh,
+        mesh=physical_mesh(mesh),
         in_specs=placed,
-        out_specs=(P("cells", "dirs"), P("cells", "dirs"), P("cells", "dirs"), P("cells", "dirs")),
+        out_specs=(P(CELLS, DIRS), P(CELLS, DIRS), P(CELLS, DIRS), P(CELLS, DIRS)),
         check_vma=False,
     )

time: 126 us -> 91 us (0.72)
  the two profiles are of different devices: /device:TPU:2 before, /device:TPU:1 now
where the time goes in v3:
time: 91 us; the launch traced here: 90.3 us
  blocking collectives  31.9 us (35%)
  starting transfers between devices  20.5 us (23%)
  local copies, waits for them, and re-layouts  11.8 us (13%)
  matrix products  10.6 us (12%)
  other arithmetic  8.68 us (10%)
  between operations  6.8 us (7%)
    all_to_all x2, blocking collectives, exchange_sum(): return jnp.sum(lax.all_to_all(spread, axes, 0, 0, tiled=True), axis=0)  31.9 us
    ppermute x4, starting transfers between devices, passed_along(): lax.ppermute(x, axes, [(i, (i + by) % devices) for i in range(devices)])  20.5 us
    reshape x1, local copies, waits for them, and re-layouts, on_device(): moved = jnp.einsum('sdc,kfc->ksdf', weighted, translations, preferred_ele...  5.22 us
    dot_general x1, matrix products, on_device(): jnp.einsum('kse,ksx->ex', blocks, moved, precision=lax.Precision.HIGHEST,...  3.69 us
    reshape x1, local copies, waits for them, and re-layouts, on_device(): gathered.reshape(classes, spheres, groups, order)  2.71 us
    dot_general x1, matrix products, on_device(): jnp.einsum('sdc,kfc->ksdf', weighted, translations, preferred_element_typ...  2.68 us
    another operation x1, other arithmetic, on_device(): jnp.stack([jnp.sum(incident * incident), jnp.sum(incident * scattered), j...  2.66 us
    dot_general x1, matrix products, on_device(): jnp.einsum('ksdc,kcf->sdf', gathered.reshape(classes, spheres, groups, or...  2.25 us
  transfers between devices with their start and end apart: 4, of which 0 were waited for; matrix products, arithmetic and copies ran while one was open for 24% of the time, Pallas kernels for 0%

profile of v3, /device:TPU:1, one launch (start us, length us, event | category | flops | bytes accessed | tf_op | source)
XLA Modules:
  0.0 90.3 jit_solution(4391597036915219606)
XLA Ops:
  0.6 0.0 copy-start
  0.6 0.0 copy-start.4
  0.7 0.0 copy-start.6
  0.7 0.0 copy-start.5
  0.7 0.9 %tile.4 = f32[64,8,192]{2,1,0:T(8,128)S(1)} broadcast(f32[64,192]{1,0:T(8,128)} %param.12), dimensions={0,2} | broadcast | bytes 442368 | tf_op jit(solution)/shard_map/tile | solution.py:59
  1.6 0.2 tile.10
  1.8 1.2 %multiply_convert_fusion = (bf16[64,1536]{1,0:T(8,128)(2,1)S(1)}, bf16[64,1536]{1,0:T(8,128)(2,1)S(1)}) fusion(f32[64,1536]{1,0:T(8,128)S(1)} %tile.10, f32[64,1536]{1,0:T(8,128)} %param.11), kind=kLoop, calls=%fused_computation.18 | loop fusion | flops 294912 | bytes 1179648 | tf_op jit(solution)/shard_map/convert_element_type | solution.py:60
  3.0 4.9 %collective-permute-start = (bf16[32,1536]{1,0:T(8,128)(2,1)S(1)}, bf16[32,1536]{1,0:T(8,128)(2,1)}, u32[]{:S(2)}, u32[]{:S(2)}) collective-permute-start(bf16[32,1536]{1,0:T(8,128)(2,1)S(1)} %get-tuple-element.42), channel_id=1, source_target_pairs={{0,4},{4,8},{8,12},{12,16},{16,20},{20,24},{24,28},{28,32},{32,36}... | collective-permute-start | bytes 294920 | tf_op jit(solution)/shard_map/ppermute | solution.py:11
  8.0 5.8 %collective-permute-start.1 = (bf16[32,1536]{1,0:T(8,128)(2,1)S(1)}, bf16[32,1536]{1,0:T(8,128)(2,1)S(1)}, u32[]{:S(2)}, u32[]{:S(2)}) collective-permute-start(bf16[32,1536]{1,0:T(8,128)(2,1)S(1)} %get-tuple-element.43), channel_id=1, source_target_pairs={{0,508},{4,0},{8,4},{12,8},{16,12},{20,16},{24,20},{28,24},{32,28}... | collective-permute-start | bytes 294920 | tf_op jit(solution)/shard_map/ppermute | solution.py:11
  13.7 0.7 select_select_fusion
  14.5 0.1 copy.25
  14.5 0.0 copy-done.4
  14.5 0.1 copy.26
  14.6 0.0 copy-done.6
  14.6 0.0 copy-done.5
  14.7 0.1 copy.27
  14.8 0.2 reshape.95
  15.0 0.0 copy-done
  15.0 2.7 %convolution_bitcast_fusion.1 = f32[8,64,8,192]{3,2,0,1:T(8,128)} fusion(bf16[8,192,192]{2,1,0:T(8,128)(2,1)S(1)} %copy-done, bf16[64,8,192,1]{2,1,0,3:T(8,128)(2,1)S(1)} %reshape.95), kind=kOutput, calls=%fused_computation.2 | convolution fusion | flops 301989888 | bytes 3932160 | tf_op jit(solution)/shard_map/sdc,kfc->ksdf/dot_general | solution.py:61
  17.7 5.2 %reshape.91 = f32[8,64,1536]{2,0,1:T(8,128)} reshape(f32[8,64,8,192]{3,2,0,1:T(8,128)} %convolution_bitcast_fusion.1) | data formatting | bytes 6291456 | tf_op jit(solution)/shard_map/reshape | solution.py:63
  22.9 0.5 fusion.22
  23.4 3.7 %convolution_bitcast_fusion = f32[128,1536]{1,0:T(8,128)S(1)} fusion(f32[8,64,128]{2,0,1:T(8,128)S(1)} %get-tuple-element.49, f32[8,64,1536]{2,0,1:T(8,128)} %reshape.91), kind=kOutput, calls=%fused_computation.1 | convolution fusion | flops 1207959552 | bytes 4194304 | tf_op jit(solution)/shard_map/kse,ksx->ex/dot_general | solution.py:64
  27.1 0.0 copy-start.1
  27.1 0.8 fusion.19
  27.9 7.9 %collective-permute-start.2 = (f32[32,1536]{1,0:T(8,128)}, f32[32,1536]{1,0:T(8,128)}, u32[]{:S(2)}, u32[]{:S(2)}) collective-permute-start(f32[32,1536]{1,0:T(8,128)} %get-tuple-element.35), channel_id=1, source_target_pairs={{0,508},{4,0},{8,4},{12,8},{16,12},{20,16},{24,20},{28,24},{32,28}... | collective-permute-start | bytes 589832 | tf_op jit(solution)/shard_map/ppermute | solution.py:11
  35.8 1.9 %collective-permute-start.3 = (f32[32,1536]{1,0:T(8,128)S(1)}, f32[32,1536]{1,0:T(8,128)}, u32[]{:S(2)}, u32[]{:S(2)}) collective-permute-start(f32[32,1536]{1,0:T(8,128)S(1)} %get-tuple-element.34), channel_id=1, source_target_pairs={{0,4},{4,8},{8,12},{12,16},{16,20},{20,24},{24,28},{28,32},{32,36}... | collective-permute-start | bytes 589832 | tf_op jit(solution)/shard_map/ppermute | solution.py:11
  37.8 0.0 collective-permute-done
  37.8 0.0 collective-permute-done.1
  37.8 0.0 copy-done.1
  37.8 0.0 copy-start.3
  37.9 0.6 copy-done.3
  38.5 1.5 %convolution_convert_fusion = bf16[8,64,1536]{2,1,0:T(8,128)(2,1)S(1)} fusion(bf16[32,1536]{1,0:T(8,128)(2,1)} %copy-done.3, bf16[64,1536]{1,0:T(8,128)(2,1)S(1)} %get-tuple-element.41, bf16[32,1536]{1,0:T(8,128)(2,1)} %collective-permute-done, bf16[8,64,128]{2,0,1:T(8,128)(2,1)S(1)} %get-tuple-element.48), kind=kOutput, calls=%fused_computation | convolution fusion | flops 203292672 | bytes 2097152 | tf_op jit(solution)/shard_map/kse,ex->ksx/dot_general | solution.py:75
  40.0 2.7 %reshape.88 = bf16[8,64,8,192]{3,2,1,0:T(8,128)(2,1)} reshape(bf16[8,64,1536]{2,1,0:T(8,128)(2,1)S(1)} %convolution_convert_fusion) | data formatting | bytes 3145728 | tf_op jit(solution)/shard_map/reshape | solution.py:80
  42.7 0.0 copy-start.2
  42.7 2.3 %convolution_bitcast_fusion.2 = f32[64,8,192]{2,1,0:T(8,128)S(1)} fusion(bf16[8,64,8,192]{3,2,1,0:T(8,128)(2,1)} %reshape.88, bf16[8,192,192]{2,1,0:T(8,128)(2,1)S(1)} %copy-done), kind=kOutput, calls=%fused_computation.3 | convolution fusion | flops 301989888 | bytes 2555904 | tf_op jit(solution)/shard_map/ksdc,kcf->sdf/dot_general | solution.py:78
  45.0 0.2 reshape.89
  45.1 0.0 collective-permute-done.2
  45.2 1.0 %fusion.9 = f32[64,1536]{1,0:T(8,128)S(1)} fusion(f32[64,1536]{1,0:T(8,128)S(1)} %slice.79, f32[32,1536]{1,0:T(8,128)} %collective-permute-done.2, f32[128,1536]{1,0:T(8,128)} %copy-done.1), kind=kLoop, calls=%fused_computation.28 | loop fusion | flops 49152 | bytes 589824 | tf_op jit(solution)/shard_map/scatter-add | solution.py:86
  46.2 0.0 collective-permute-done.3
  46.2 1.0 %fusion.8 = f32[64,1536]{1,0:T(8,128)S(1)} fusion(f32[64,1536]{1,0:T(8,128)S(1)} %fusion.9, f32[32,1536]{1,0:T(8,128)} %collective-permute-done.3), kind=kLoop, calls=%fused_computation.26 | loop fusion | flops 49152 | bytes 589824 | tf_op jit(solution)/shard_map/scatter-add | solution.py:87
  47.2 0.0 copy-done.2
  47.2 0.8 multiply_reduce_fusion.2
  48.0 2.7 %pad_maximum_fusion = f32[4]{0:T(128)S(1)} fusion(f32[1]{0:T(128)} %bitcast.11, f32[1]{0:T(128)} %bitcast.10, f32[1]{0:T(128)} %bitcast.6, f32[1]{0:T(128)} %bitcast), kind=kLoop, calls=%fused_computation.48 | loop fusion | flops 12 | bytes 32 | tf_op jit(solution)/shard_map/stack | solution.py:93
  50.7 18.9 %all_to_all.12 = f32[32,1,4]{2,1,0:T(1,128)S(1)} all-to-all(f32[32,1,4]{2,1,0:T(1,128)S(1)} %broadcast_in_dim.18), channel_id=1, replica_groups=mesh['y'=4,'z'=16,'core'=2,'x'=4] {'z','core'}, dimensions={0} | all-to-all | bytes 1024 | tf_op jit(solution)/shard_map/all_to_all | solution.py:23
  69.6 0.1 reduce_sum.58
  69.6 13.0 %all_to_all.13 = f32[16,1,4]{2,1,0:T(1,128)S(1)} all-to-all(f32[16,1,4]{2,1,0:T(1,128)S(1)} %broadcast_in_dim.19), channel_id=1, replica_groups=mesh['y'=4,'z'=16,'core'=2,'x'=4] {'y','x'}, dimensions={0} | all-to-all | bytes 512 | tf_op jit(solution)/shard_map/all_to_all | solution.py:23
  82.6 0.6 fusion.21
  89.1 1.2 %multiply_subtract_fusion = (f32[64,1536]{1,0:T(8,128)}, f32[64,1536]{1,0:T(8,128)}, f32[64,1536]{1,0:T(8,128)}, f32[64,1536]{1,0:T(8,128)}) fusion(f32[64,1536]{1,0:T(8,128)S(1)} %copy-done.2, f32[64,1536]{1,0:T(8,128)S(1)} %fusion.8, f32[]{:T(128)S(6)} %div.25, f32[]{:T(128)S(6)} %div.27, f32[64,1536]{1,0:T(8,128)S(1)} %tile.10, f32[64,1536]{1,0:T(8,128)S(1)} %reshape.89), kind=kLoop, calls=%fused_computation.14 | loop fusion | flops 983040 | bytes 3145736 | tf_op jit(solution)/shard_map/sub | solution.py:114
  (6 shorter events, 0.1 us)
Async XLA Ops:
  0.6 14.4 %copy-start = (bf16[8,192,192]{2,1,0:T(8,128)(2,1)S(1)}, bf16[8,192,192]{2,1,0:T(8,128)(2,1)}, u32[]{:S(2)}) copy-start(bf16[8,192,192]{2,1,0:T(8,128)(2,1)} %param.13) | copy-start | bytes 1769476
  0.6 13.9 %copy-start.4 = (s32[64,16]{0,1:T(8,128)S(1)}, s32[64,16]{0,1:T(8,128)}, u32[]{:S(2)}) copy-start(s32[64,16]{0,1:T(8,128)} %param.15) | copy-start | bytes 12292
  0.7 14.0 %copy-start.6 = (bf16[64,16]{0,1:T(8,128)(2,1)S(1)}, bf16[64,16]{0,1:T(8,128)(2,1)}, u32[]{:S(2)}) copy-start(bf16[64,16]{0,1:T(8,128)(2,1)} %param.16) | copy-start | bytes 6148
  0.7 14.0 %copy-start.5 = (s32[64,16]{0,1:T(8,128)S(1)}, s32[64,16]{0,1:T(8,128)}, u32[]{:S(2)}) copy-start(s32[64,16]{0,1:T(8,128)} %param.17) | copy-start | bytes 12292
  3.0 34.8 %collective-permute-start = (bf16[32,1536]{1,0:T(8,128)(2,1)S(1)}, bf16[32,1536]{1,0:T(8,128)(2,1)}, u32[]{:S(2)}, u32[]{:S(2)}) collective-permute-start(bf16[32,1536]{1,0:T(8,128)(2,1)S(1)} %get-tuple-element.42), channel_id=1, source_target_pairs={{0,4},{4,8},{8,12},{12,16},{16,20},{20,24},{24,28},{28,32},{32,36}... | collective-permute-start | bytes 294920 | tf_op jit(solution)/shard_map/ppermute | solution.py:11
  8.0 29.9 %collective-permute-start.1 = (bf16[32,1536]{1,0:T(8,128)(2,1)S(1)}, bf16[32,1536]{1,0:T(8,128)(2,1)S(1)}, u32[]{:S(2)}, u32[]{:S(2)}) collective-permute-start(bf16[32,1536]{1,0:T(8,128)(2,1)S(1)} %get-tuple-element.43), channel_id=1, source_target_pairs={{0,508},{4,0},{8,4},{12,8},{16,12},{20,16},{24,20},{28,24},{32,28}... | collective-permute-start | bytes 294920 | tf_op jit(solution)/shard_map/ppermute | solution.py:11
  27.1 10.7 %copy-start.1 = (f32[128,1536]{1,0:T(8,128)}, f32[128,1536]{1,0:T(8,128)S(1)}, u32[]{:S(2)}) copy-start(f32[128,1536]{1,0:T(8,128)S(1)} %convolution_bitcast_fusion) | copy-start | bytes 2359300
  27.9 17.2 %collective-permute-start.2 = (f32[32,1536]{1,0:T(8,128)}, f32[32,1536]{1,0:T(8,128)}, u32[]{:S(2)}, u32[]{:S(2)}) collective-permute-start(f32[32,1536]{1,0:T(8,128)} %get-tuple-element.35), channel_id=1, source_target_pairs={{0,508},{4,0},{8,4},{12,8},{16,12},{20,16},{24,20},{28,24},{32,28}... | collective-permute-start | bytes 589832 | tf_op jit(solution)/shard_map/ppermute | solution.py:11
  35.8 10.4 %collective-permute-start.3 = (f32[32,1536]{1,0:T(8,128)S(1)}, f32[32,1536]{1,0:T(8,128)}, u32[]{:S(2)}, u32[]{:S(2)}) collective-permute-start(f32[32,1536]{1,0:T(8,128)S(1)} %get-tuple-element.34), channel_id=1, source_target_pairs={{0,4},{4,8},{8,12},{12,16},{16,20},{20,24},{24,28},{28,32},{32,36}... | collective-permute-start | bytes 589832 | tf_op jit(solution)/shard_map/ppermute | solution.py:11
  37.8 0.6 copy-start.3
  42.7 4.5 %copy-start.2 = (f32[64,1536]{1,0:T(8,128)S(1)}, f32[64,1536]{1,0:T(8,128)}, u32[]{:S(2)}) copy-start(f32[64,1536]{1,0:T(8,128)} %param.11) | copy-start | bytes 1179652

commit v4 on v3

--- a/solution.py
+++ b/solution.py
@@ -36,8 +36,6 @@
     cell_count = lax.axis_size("y") * lax.axis_size("z") * lax.axis_size("core")
 
     source = incident.astype(jnp.bfloat16)
-    from_prev_rows = passed_along(source[spheres - band :], CELLS, 1)
-    from_next_rows = passed_along(source[:band], CELLS, -1)
 
     owner = pair_sphere // spheres
     within = pair_sphere % spheres
@@ -68,13 +66,18 @@
         precision=lax.Precision.HIGHEST,
         preferred_element_type=jnp.float32,
     )
-    from_next = passed_along(contrib[:band], CELLS, -1)
-    from_prev = passed_along(contrib[band + spheres :], CELLS, 1)
+    to_next = jnp.concatenate([incident[spheres - band :], contrib[band + spheres :]], axis=0)
+    to_prev = jnp.concatenate([incident[:band], contrib[:band]], axis=0)
+    from_prev = passed_along(to_next, CELLS, 1)
+    from_next = passed_along(to_prev, CELLS, -1)
 
-    padded = jnp.concatenate([from_prev_rows, source, from_next_rows], axis=0)
-    gathered = jnp.einsum(
-        "kse,ex->ksx", blocks_half, padded, preferred_element_type=jnp.float32
-    ).astype(jnp.bfloat16)
+    own_part = jnp.einsum(
+        "kse,ex->ksx", blocks_half[:, :, band : band + spheres], source, preferred_element_type=jnp.float32
+    )
+    halo = jnp.concatenate([from_prev[:band], from_next[:band]], axis=0).astype(jnp.bfloat16)
+    halo_blocks = jnp.concatenate([blocks_half[:, :, :band], blocks_half[:, :, band + spheres :]], axis=2)
+    halo_part = jnp.einsum("kse,ex->ksx", halo_blocks, halo, preferred_element_type=jnp.float32)
+    gathered = (own_part + halo_part).astype(jnp.bfloat16)
     coupled = jnp.einsum(
         "ksdc,kcf->sdf",
         gathered.reshape(classes, spheres, groups, order),
@@ -83,8 +86,8 @@
     ).reshape(spheres, columns)
 
     back = contrib[band : band + spheres]
-    back = back.at[spheres - band :].add(from_next)
-    back = back.at[:band].add(from_prev)
+    back = back.at[spheres - band :].add(from_next[band:])
+    back = back.at[:band].add(from_prev[band:])
 
     scattered = gain * coupled
     image = incident - scattered
@@ -100,10 +103,11 @@
     )
     partial = lax.optimization_barrier(partial)
     total = exchange_sum(exchange_sum(partial, ("z", "core")), ("y", DIRS))
-    norm_old = total[0]
-    cross_u = total[1]
-    cross_v = total[2]
-    cross_uv = total[3]
+    rows = lax.optimization_barrier(jnp.broadcast_to(total[:, None], (4, columns)))
+    norm_old = rows[0:1]
+    cross_u = rows[1:2]
+    cross_v = rows[2:3]
+    cross_uv = rows[3:4]
     curvature = norm_old - cross_u
     step_size = norm_old / curvature
     keep = -cross_u / curvature

time: 91 us -> 90 us (0.989)
  waiting for transfers between devices: 0.01 us -> 11.5 us
  starting transfers between devices: 20.5 us -> 10.8 us
  between operations: 6.8 us -> 0.83 us
  blocking collectives: 31.9 us -> 35.8 us
  other arithmetic: 8.68 us -> 7.61 us
    ppermute x4 -> x2, waiting for transfers between devices: 0.01 us -> 11.5 us  [passed_along(): lax.ppermute(x, axes, [(i, (i + by) % devices) for i in range(devices)])]
    ppermute x4 -> x2, starting transfers between devices: 20.5 us -> 10.8 us  [passed_along(): lax.ppermute(x, axes, [(i, (i + by) % devices) for i in range(devices)])]
    all_to_all x2, blocking collectives: 31.9 us -> 35.8 us  [exchange_sum(): return jnp.sum(lax.all_to_all(spread, axes, 0, 0, tiled=True), axis=0)]
    scatter-add x2, other arithmetic: 2.02 us -> 0.08 us  [the longest x1 0.04 us: on_device(): back = back.at[:band].add(from_prev[band:])]
  transfers between devices with their start and end apart: 4 -> 2, of which waited for: 0 -> 2; matrix products, arithmetic and copies ran while one was open for 24% -> 1% of each run, Pallas kernels for 0% -> 0%
where the time goes in v4:
time: 90 us; the launch traced here: 89.4 us
  blocking collectives  35.8 us (40%)
  local copies, waits for them, and re-layouts  12.5 us (14%)
  waiting for transfers between devices  11.5 us (13%)
  starting transfers between devices  10.8 us (12%)
  matrix products  10.2 us (11%)
  other arithmetic  7.61 us (8%)
    all_to_all x2, blocking collectives, exchange_sum(): return jnp.sum(lax.all_to_all(spread, axes, 0, 0, tiled=True), axis=0)  35.8 us
    ppermute x2, waiting for transfers between devices, passed_along(): lax.ppermute(x, axes, [(i, (i + by) % devices) for i in range(devices)])  11.5 us
    ppermute x2, starting transfers between devices, passed_along(): lax.ppermute(x, axes, [(i, (i + by) % devices) for i in range(devices)])  10.8 us
    reshape x1, local copies, waits for them, and re-layouts, on_device(): moved = jnp.einsum('sdc,kfc->ksdf', weighted, translations, preferred_ele...  5.22 us
    dot_general x1, matrix products, on_device(): jnp.einsum('kse,ksx->ex', blocks, moved, precision=lax.Precision.HIGHEST,...  3.69 us
    reshape x1, local copies, waits for them, and re-layouts, on_device(): gathered.reshape(classes, spheres, groups, order)  2.71 us
    dot_general x1, matrix products, on_device(): jnp.einsum('sdc,kfc->ksdf', weighted, translations, preferred_element_typ...  2.67 us
    another operation x1, other arithmetic, on_device(): jnp.stack([jnp.sum(incident * incident), jnp.sum(incident * scattered), j...  2.66 us
  transfers between devices with their start and end apart: 2, of which 2 were waited for; matrix products, arithmetic and copies ran while one was open for 1% of the time, Pallas kernels for 0%

profile of v4, /device:TPU:1, one launch (start us, length us, event | category | flops | bytes accessed | tf_op | source)
XLA Modules:
  0.0 89.4 jit_solution(15666883948598714915)
XLA Ops:
  0.6 0.0 copy-start
  0.7 0.8 select_select_fusion
  1.4 0.1 copy.27
  1.5 0.8 copy.28
  2.3 0.7 convert_multiply_fusion
  3.0 0.1 copy.29
  3.1 0.9 tile.4
  4.0 0.2 tile.10
  4.2 1.1 %fusion.28 = (f32[32,1536]{1,0:T(8,128)S(1)}, f32[32,1536]{1,0:T(8,128)S(1)}) fusion(f32[64,1536]{1,0:T(8,128)} %param.11), kind=kLoop, calls=%fused_computation.68 | loop fusion | bytes 786432 | tf_op jit(solution)/shard_map/slice | solution.py:69
  5.2 1.0 %multiply_convert_fusion = bf16[64,1536]{1,0:T(8,128)(2,1)S(1)} fusion(f32[64,1536]{1,0:T(8,128)S(1)} %tile.10, f32[64,1536]{1,0:T(8,128)} %param.11), kind=kLoop, calls=%fused_computation.17 | loop fusion | flops 196608 | bytes 983040 | tf_op jit(solution)/shard_map/convert_element_type | solution.py:58
  6.3 0.2 reshape.94
  6.5 0.0 copy-done
  6.5 2.7 %convolution_bitcast_fusion.1 = f32[8,64,8,192]{3,2,0,1:T(8,128)} fusion(bf16[8,192,192]{2,1,0:T(8,128)(2,1)S(1)} %copy-done, bf16[64,8,192,1]{2,1,0,3:T(8,128)(2,1)S(1)} %reshape.94), kind=kOutput, calls=%fused_computation.3 | convolution fusion | flops 301989888 | bytes 3932160 | tf_op jit(solution)/shard_map/sdc,kfc->ksdf/dot_general | solution.py:59
  9.2 5.2 %reshape.90 = f32[8,64,1536]{2,0,1:T(8,128)} reshape(f32[8,64,8,192]{3,2,0,1:T(8,128)} %convolution_bitcast_fusion.1) | data formatting | bytes 6291456 | tf_op jit(solution)/shard_map/reshape | solution.py:61
  14.4 0.5 fusion.30
  14.9 3.7 %convolution_bitcast_fusion = f32[128,1536]{1,0:T(8,128)S(1)} fusion(f32[8,64,128]{2,0,1:T(8,128)S(1)} %get-tuple-element.47, f32[8,64,1536]{2,0,1:T(8,128)} %reshape.90), kind=kOutput, calls=%fused_computation.2 | convolution fusion | flops 1207959552 | bytes 4194304 | tf_op jit(solution)/shard_map/kse,ksx->ex/dot_general | solution.py:62
  18.6 0.0 copy-start.1
  18.7 8.9 %collective-permute-start.1 = (f32[64,1536]{1,0:T(8,128)S(1)}, f32[64,1536]{1,0:T(8,128)S(1)}, u32[]{:S(2)}, u32[]{:S(2)}) collective-permute-start(f32[64,1536]{1,0:T(8,128)S(1)} %pad_maximum_fusion.1), channel_id=1, source_target_pairs={{0,508},{4,0},{8,4},{12,8},{16,12},{20,16},{24,20},{28,24},{32,28}... | collective-permute-start | bytes 1179656 | tf_op jit(solution)/shard_map/ppermute | solution.py:11
  27.7 0.1 slice.107
  27.8 0.1 fusion.29
  27.9 1.3 %collective-permute-done.1 = f32[64,1536]{1,0:T(8,128)S(1)} collective-permute-done((f32[64,1536]{1,0:T(8,128)S(1)}, f32[64,1536]{1,0:T(8,128)S(1)}, u32[]{:S(2)}, u32[]{:S(2)}) %collective-permute-start.1) | collective-permute-done | bytes 393248 | tf_op jit(solution)/shard_map/ppermute | solution.py:11
  29.3 1.9 %collective-permute-start = (f32[64,1536]{1,0:T(8,128)S(1)}, f32[64,1536]{1,0:T(8,128)S(1)}, u32[]{:S(2)}, u32[]{:S(2)}) collective-permute-start(f32[64,1536]{1,0:T(8,128)S(1)} %pad_maximum_fusion), channel_id=1, source_target_pairs={{0,4},{4,8},{8,12},{12,16},{16,20},{20,24},{24,28},{28,32},{32,36}... | collective-permute-start | bytes 1179656 | tf_op jit(solution)/shard_map/ppermute | solution.py:11
  31.2 0.1 pad_maximum_fusion.2
  31.4 0.0 copy-done.1
  31.4 0.6 fusion.9
  31.9 10.2 %collective-permute-done = f32[64,1536]{1,0:T(8,128)S(1)} collective-permute-done((f32[64,1536]{1,0:T(8,128)S(1)}, f32[64,1536]{1,0:T(8,128)S(1)}, u32[]{:S(2)}, u32[]{:S(2)}) %collective-permute-start) | collective-permute-done | bytes 393248 | tf_op jit(solution)/shard_map/ppermute | solution.py:11
  42.1 0.0 copy-start.2
  42.1 0.7 copy-done.2
  42.9 0.5 fusion
  43.4 2.7 %reshape.91 = bf16[8,64,8,192]{3,2,1,0:T(8,128)(2,1)} reshape(bf16[8,64,1536]{2,1,0:T(8,128)(2,1)S(1)} %fusion) | data formatting | bytes 3145728 | tf_op jit(solution)/shard_map/reshape | solution.py:83
  46.1 0.0 copy-start.3
  46.1 2.3 %convolution_bitcast_fusion.2 = f32[64,8,192]{2,1,0:T(8,128)S(1)} fusion(bf16[8,64,8,192]{3,2,1,0:T(8,128)(2,1)} %reshape.91, bf16[8,192,192]{2,1,0:T(8,128)(2,1)S(1)} %copy-done), kind=kOutput, calls=%fused_computation.4 | convolution fusion | flops 301989888 | bytes 2555904 | tf_op jit(solution)/shard_map/ksdc,kcf->sdf/dot_general | solution.py:81
  48.4 0.2 reshape.92
  48.6 0.0 copy-done.3
  48.6 0.8 multiply_reduce_fusion.2
  49.4 2.7 %pad_maximum_fusion.3 = f32[4]{0:T(128)S(1)} fusion(f32[1]{0:T(128)} %bitcast.12, f32[1]{0:T(128)} %bitcast.11, f32[1]{0:T(128)} %bitcast.10, f32[1]{0:T(128)} %bitcast), kind=kLoop, calls=%fused_computation.65 | loop fusion | flops 12 | bytes 32 | tf_op jit(solution)/shard_map/stack | solution.py:96
  52.1 24.0 %all_to_all.12 = f32[32,1,4]{2,1,0:T(1,128)S(1)} all-to-all(f32[32,1,4]{2,1,0:T(1,128)S(1)} %broadcast_in_dim.20), channel_id=1, replica_groups=mesh['y'=4,'z'=16,'core'=2,'x'=4] {'z','core'}, dimensions={0} | all-to-all | bytes 1024 | tf_op jit(solution)/shard_map/all_to_all | solution.py:23
  76.1 0.1 reduce_sum.58
  76.2 11.8 %all_to_all.13 = f32[16,1,4]{2,1,0:T(1,128)S(1)} all-to-all(f32[16,1,4]{2,1,0:T(1,128)S(1)} %broadcast_in_dim.21), channel_id=1, replica_groups=mesh['y'=4,'z'=16,'core'=2,'x'=4] {'y','x'}, dimensions={0} | all-to-all | bytes 512 | tf_op jit(solution)/shard_map/all_to_all | solution.py:23
  88.0 0.1 broadcast_in_dim.22
  88.1 0.1 fusion.24
  88.2 1.2 %multiply_subtract_fusion = (f32[64,1536]{1,0:T(8,128)}, f32[64,1536]{1,0:T(8,128)}, f32[64,1536]{1,0:T(8,128)}, f32[64,1536]{1,0:T(8,128)}) fusion(f32[64,1536]{1,0:T(8,128)S(1)} %copy-done.1, f32[64,1536]{1,0:T(8,128)S(1)} %fusion.5, f32[1536]{0:T(1024)S(1)} %get-tuple-element.33, f32[1536]{0:T(1024)S(1)} %get-tuple-element.32, f32[64,1536]{1,0:T(8,128)S(1)} %tile.10, ...), kind=kLoop, calls=%fused_computation.12 | loop fusion | flops 983040 | bytes 3158016 | tf_op jit(solution)/shard_map/sub | solution.py:118
  (11 shorter events, 0.3 us)
Async XLA Ops:
  0.6 5.9 %copy-start = (bf16[8,192,192]{2,1,0:T(8,128)(2,1)S(1)}, bf16[8,192,192]{2,1,0:T(8,128)(2,1)}, u32[]{:S(2)}) copy-start(bf16[8,192,192]{2,1,0:T(8,128)(2,1)} %param.13) | copy-start | bytes 1769476
  18.6 12.7 %copy-start.1 = (f32[64,1536]{1,0:T(8,128)S(1)}, f32[64,1536]{1,0:T(8,128)}, u32[]{:S(2)}) copy-start(f32[64,1536]{1,0:T(8,128)} %param.11) | copy-start | bytes 1179652
  18.7 10.5 %collective-permute-start.1 = (f32[64,1536]{1,0:T(8,128)S(1)}, f32[64,1536]{1,0:T(8,128)S(1)}, u32[]{:S(2)}, u32[]{:S(2)}) collective-permute-start(f32[64,1536]{1,0:T(8,128)S(1)} %pad_maximum_fusion.1), channel_id=1, source_target_pairs={{0,508},{4,0},{8,4},{12,8},{16,12},{20,16},{24,20},{28,24},{32,28}... | collective-permute-start | bytes 1179656 | tf_op jit(solution)/shard_map/ppermute | solution.py:11
  29.3 12.8 %collective-permute-start = (f32[64,1536]{1,0:T(8,128)S(1)}, f32[64,1536]{1,0:T(8,128)S(1)}, u32[]{:S(2)}, u32[]{:S(2)}) collective-permute-start(f32[64,1536]{1,0:T(8,128)S(1)} %pad_maximum_fusion), channel_id=1, source_target_pairs={{0,4},{4,8},{8,12},{12,16},{16,20},{20,24},{24,28},{28,32},{32,36}... | collective-permute-start | bytes 1179656 | tf_op jit(solution)/shard_map/ppermute | solution.py:11
  42.1 0.7 copy-start.2
  46.1 2.4 %copy-start.3 = (f32[64,1536]{1,0:T(8,128)S(1)}, f32[64,1536]{1,0:T(8,128)}, u32[]{:S(2)}) copy-start(f32[64,1536]{1,0:T(8,128)} %copy-done.2) | copy-start | bytes 1179652

commit v5 on v3

--- a/solution.py
+++ b/solution.py
@@ -100,10 +100,11 @@
     )
     partial = lax.optimization_barrier(partial)
     total = exchange_sum(exchange_sum(partial, ("z", "core")), ("y", DIRS))
-    norm_old = total[0]
-    cross_u = total[1]
-    cross_v = total[2]
-    cross_uv = total[3]
+    rows = lax.optimization_barrier(jnp.broadcast_to(total[:, None], (4, columns)))
+    norm_old = rows[0:1]
+    cross_u = rows[1:2]
+    cross_v = rows[2:3]
+    cross_uv = rows[3:4]
     curvature = norm_old - cross_u
     step_size = norm_old / curvature
     keep = -cross_u / curvature

time: 91 us -> 84.6 us (0.930)
  between operations: 6.8 us -> 0.89 us
  transfers between devices with their start and end apart: 4 -> 4, of which waited for: 0 -> 0; matrix products, arithmetic and copies ran while one was open for 24% -> 26% of each run, Pallas kernels for 0% -> 0%
where the time goes in v5:
time: 84.6 us; the launch traced here: 84 us
  blocking collectives  31.9 us (38%)
  starting transfers between devices  20.5 us (24%)
  local copies, waits for them, and re-layouts  11.3 us (13%)
  matrix products  10.7 us (13%)
  other arithmetic  8.73 us (10%)
  between operations  0.89 us (1%)
    all_to_all x2, blocking collectives, exchange_sum(): return jnp.sum(lax.all_to_all(spread, axes, 0, 0, tiled=True), axis=0)  31.9 us
    ppermute x4, starting transfers between devices, passed_along(): lax.ppermute(x, axes, [(i, (i + by) % devices) for i in range(devices)])  20.5 us
    reshape x1, local copies, waits for them, and re-layouts, on_device(): moved = jnp.einsum('sdc,kfc->ksdf', weighted, translations, preferred_ele...  5.22 us
    dot_general x1, matrix products, on_device(): jnp.einsum('kse,ksx->ex', blocks, moved, precision=lax.Precision.HIGHEST,...  3.74 us
    reshape x1, local copies, waits for them, and re-layouts, on_device(): gathered.reshape(classes, spheres, groups, order)  2.71 us
    dot_general x1, matrix products, on_device(): jnp.einsum('sdc,kfc->ksdf', weighted, translations, preferred_element_typ...  2.67 us
    another operation x1, other arithmetic, on_device(): jnp.stack([jnp.sum(incident * incident), jnp.sum(incident * scattered), j...  2.66 us
    dot_general x1, matrix products, on_device(): jnp.einsum('ksdc,kcf->sdf', gathered.reshape(classes, spheres, groups, or...  2.26 us
  transfers between devices with their start and end apart: 4, of which 0 were waited for; matrix products, arithmetic and copies ran while one was open for 26% of the time, Pallas kernels for 0%

profile of v5, /device:TPU:1, one launch (start us, length us, event | category | flops | bytes accessed | tf_op | source)
XLA Modules:
  0.0 84.0 jit_solution(5781838875227060928)
XLA Ops:
  0.6 0.0 copy-start
  0.6 0.0 copy-start.4
  0.7 0.0 copy-start.6
  0.7 0.0 copy-start.5
  0.7 0.9 %tile.4 = f32[64,8,192]{2,1,0:T(8,128)S(1)} broadcast(f32[64,192]{1,0:T(8,128)} %param.12), dimensions={0,2} | broadcast | bytes 442368 | tf_op jit(solution)/shard_map/tile | solution.py:59
  1.6 0.2 tile.10
  1.8 1.2 %multiply_convert_fusion = (bf16[64,1536]{1,0:T(8,128)(2,1)S(1)}, bf16[64,1536]{1,0:T(8,128)(2,1)S(1)}) fusion(f32[64,1536]{1,0:T(8,128)S(1)} %tile.10, f32[64,1536]{1,0:T(8,128)} %param.11), kind=kLoop, calls=%fused_computation.18 | loop fusion | flops 294912 | bytes 1179648 | tf_op jit(solution)/shard_map/convert_element_type | solution.py:60
  3.0 4.9 %collective-permute-start = (bf16[32,1536]{1,0:T(8,128)(2,1)S(1)}, bf16[32,1536]{1,0:T(8,128)(2,1)}, u32[]{:S(2)}, u32[]{:S(2)}) collective-permute-start(bf16[32,1536]{1,0:T(8,128)(2,1)S(1)} %get-tuple-element.44), channel_id=1, source_target_pairs={{0,4},{4,8},{8,12},{12,16},{16,20},{20,24},{24,28},{28,32},{32,36}... | collective-permute-start | bytes 294920 | tf_op jit(solution)/shard_map/ppermute | solution.py:11
  8.0 5.8 %collective-permute-start.1 = (bf16[32,1536]{1,0:T(8,128)(2,1)S(1)}, bf16[32,1536]{1,0:T(8,128)(2,1)S(1)}, u32[]{:S(2)}, u32[]{:S(2)}) collective-permute-start(bf16[32,1536]{1,0:T(8,128)(2,1)S(1)} %get-tuple-element.45), channel_id=1, source_target_pairs={{0,508},{4,0},{8,4},{12,8},{16,12},{20,16},{24,20},{28,24},{32,28}... | collective-permute-start | bytes 294920 | tf_op jit(solution)/shard_map/ppermute | solution.py:11
  13.7 0.7 select_select_fusion
  14.5 0.1 copy.25
  14.5 0.0 copy-done.4
  14.5 0.1 copy.26
  14.6 0.0 copy-done.6
  14.6 0.0 copy-done.5
  14.7 0.1 copy.27
  14.8 0.2 reshape.96
  15.0 0.0 copy-done
  15.0 2.7 %convolution_bitcast_fusion.1 = f32[8,64,8,192]{3,2,0,1:T(8,128)} fusion(bf16[8,192,192]{2,1,0:T(8,128)(2,1)S(1)} %copy-done, bf16[64,8,192,1]{2,1,0,3:T(8,128)(2,1)S(1)} %reshape.96), kind=kOutput, calls=%fused_computation.2 | convolution fusion | flops 301989888 | bytes 3932160 | tf_op jit(solution)/shard_map/sdc,kfc->ksdf/dot_general | solution.py:61
  17.7 5.2 %reshape.92 = f32[8,64,1536]{2,0,1:T(8,128)} reshape(f32[8,64,8,192]{3,2,0,1:T(8,128)} %convolution_bitcast_fusion.1) | data formatting | bytes 6291456 | tf_op jit(solution)/shard_map/reshape | solution.py:63
  22.9 0.5 fusion.27
  23.4 3.7 %convolution_bitcast_fusion = f32[128,1536]{1,0:T(8,128)S(1)} fusion(f32[8,64,128]{2,0,1:T(8,128)S(1)} %get-tuple-element.47, f32[8,64,1536]{2,0,1:T(8,128)} %reshape.92), kind=kOutput, calls=%fused_computation.1 | convolution fusion | flops 1207959552 | bytes 4194304 | tf_op jit(solution)/shard_map/kse,ksx->ex/dot_general | solution.py:64
  27.2 0.0 copy-start.1
  27.2 0.8 fusion.25
  28.0 7.9 %collective-permute-start.2 = (f32[32,1536]{1,0:T(8,128)}, f32[32,1536]{1,0:T(8,128)}, u32[]{:S(2)}, u32[]{:S(2)}) collective-permute-start(f32[32,1536]{1,0:T(8,128)} %get-tuple-element.37), channel_id=1, source_target_pairs={{0,508},{4,0},{8,4},{12,8},{16,12},{20,16},{24,20},{28,24},{32,28}... | collective-permute-start | bytes 589832 | tf_op jit(solution)/shard_map/ppermute | solution.py:11
  35.9 1.9 %collective-permute-start.3 = (f32[32,1536]{1,0:T(8,128)S(1)}, f32[32,1536]{1,0:T(8,128)}, u32[]{:S(2)}, u32[]{:S(2)}) collective-permute-start(f32[32,1536]{1,0:T(8,128)S(1)} %get-tuple-element.36), channel_id=1, source_target_pairs={{0,4},{4,8},{8,12},{12,16},{16,20},{20,24},{24,28},{28,32},{32,36}... | collective-permute-start | bytes 589832 | tf_op jit(solution)/shard_map/ppermute | solution.py:11
  37.8 0.0 collective-permute-done
  37.9 0.0 collective-permute-done.1
  37.9 0.0 copy-done.1
  37.9 0.0 copy-start.3
  37.9 0.6 copy-done.3
  38.5 1.5 %convolution_convert_fusion = bf16[8,64,1536]{2,1,0:T(8,128)(2,1)S(1)} fusion(bf16[32,1536]{1,0:T(8,128)(2,1)} %copy-done.3, bf16[64,1536]{1,0:T(8,128)(2,1)S(1)} %get-tuple-element.43, bf16[32,1536]{1,0:T(8,128)(2,1)} %collective-permute-done, bf16[8,64,128]{2,0,1:T(8,128)(2,1)S(1)} %get-tuple-element.46), kind=kOutput, calls=%fused_computation | convolution fusion | flops 203292672 | bytes 2097152 | tf_op jit(solution)/shard_map/kse,ex->ksx/dot_general | solution.py:75
  40.0 2.7 %reshape.89 = bf16[8,64,8,192]{3,2,1,0:T(8,128)(2,1)} reshape(bf16[8,64,1536]{2,1,0:T(8,128)(2,1)S(1)} %convolution_convert_fusion) | data formatting | bytes 3145728 | tf_op jit(solution)/shard_map/reshape | solution.py:80
  42.7 2.3 %convolution_bitcast_fusion.2 = f32[64,8,192]{2,1,0:T(8,128)S(1)} fusion(bf16[8,64,8,192]{3,2,1,0:T(8,128)(2,1)} %reshape.89, bf16[8,192,192]{2,1,0:T(8,128)(2,1)S(1)} %copy-done), kind=kOutput, calls=%fused_computation.3 | convolution fusion | flops 301989888 | bytes 2555904 | tf_op jit(solution)/shard_map/ksdc,kcf->sdf/dot_general | solution.py:78
  45.0 0.2 reshape.90
  45.2 0.0 collective-permute-done.2
  45.2 1.0 %fusion.9 = f32[64,1536]{1,0:T(8,128)S(1)} fusion(f32[64,1536]{1,0:T(8,128)S(1)} %slice.79, f32[32,1536]{1,0:T(8,128)} %collective-permute-done.2, f32[128,1536]{1,0:T(8,128)} %copy-done.1), kind=kLoop, calls=%fused_computation.28 | loop fusion | flops 49152 | bytes 589824 | tf_op jit(solution)/shard_map/scatter-add | solution.py:86
  46.2 0.0 collective-permute-done.3
  46.2 1.0 %fusion.8 = f32[64,1536]{1,0:T(8,128)S(1)} fusion(f32[64,1536]{1,0:T(8,128)S(1)} %fusion.9, f32[32,1536]{1,0:T(8,128)} %collective-permute-done.3), kind=kLoop, calls=%fused_computation.26 | loop fusion | flops 49152 | bytes 589824 | tf_op jit(solution)/shard_map/scatter-add | solution.py:87
  47.2 0.0 copy-done.2
  47.2 0.8 multiply_reduce_fusion.2
  48.0 2.7 %pad_maximum_fusion = f32[4]{0:T(128)S(1)} fusion(f32[1]{0:T(128)} %bitcast.11, f32[1]{0:T(128)} %bitcast.10, f32[1]{0:T(128)} %bitcast.6, f32[1]{0:T(128)} %bitcast), kind=kLoop, calls=%fused_computation.57 | loop fusion | flops 12 | bytes 32 | tf_op jit(solution)/shard_map/stack | solution.py:93
  50.7 18.9 %all_to_all.12 = f32[32,1,4]{2,1,0:T(1,128)S(1)} all-to-all(f32[32,1,4]{2,1,0:T(1,128)S(1)} %broadcast_in_dim.20), channel_id=1, replica_groups=mesh['y'=4,'z'=16,'core'=2,'x'=4] {'z','core'}, dimensions={0} | all-to-all | bytes 1024 | tf_op jit(solution)/shard_map/all_to_all | solution.py:23
  69.6 0.1 reduce_sum.58
  69.6 13.0 %all_to_all.13 = f32[16,1,4]{2,1,0:T(1,128)S(1)} all-to-all(f32[16,1,4]{2,1,0:T(1,128)S(1)} %broadcast_in_dim.21), channel_id=1, replica_groups=mesh['y'=4,'z'=16,'core'=2,'x'=4] {'y','x'}, dimensions={0} | all-to-all | bytes 512 | tf_op jit(solution)/shard_map/all_to_all | solution.py:23
  82.7 0.1 broadcast_in_dim.22
  82.7 0.1 fusion.21
  82.8 1.2 %multiply_subtract_fusion = (f32[64,1536]{1,0:T(8,128)}, f32[64,1536]{1,0:T(8,128)}, f32[64,1536]{1,0:T(8,128)}, f32[64,1536]{1,0:T(8,128)}) fusion(f32[64,1536]{1,0:T(8,128)S(1)} %copy-done.2, f32[64,1536]{1,0:T(8,128)S(1)} %fusion.8, f32[1536]{0:T(1024)S(1)} %get-tuple-element.33, f32[1536]{0:T(1024)S(1)} %get-tuple-element.32, f32[64,1536]{1,0:T(8,128)S(1)} %tile.10, ...), kind=kLoop, calls=%fused_computation.14 | loop fusion | flops 983040 | bytes 3158016 | tf_op jit(solution)/shard_map/sub | solution.py:115
  (7 shorter events, 0.1 us)
Async XLA Ops:
  0.6 14.4 %copy-start = (bf16[8,192,192]{2,1,0:T(8,128)(2,1)S(1)}, bf16[8,192,192]{2,1,0:T(8,128)(2,1)}, u32[]{:S(2)}) copy-start(bf16[8,192,192]{2,1,0:T(8,128)(2,1)} %param.13) | copy-start | bytes 1769476
  0.6 13.9 %copy-start.4 = (s32[64,16]{0,1:T(8,128)S(1)}, s32[64,16]{0,1:T(8,128)}, u32[]{:S(2)}) copy-start(s32[64,16]{0,1:T(8,128)} %param.15) | copy-start | bytes 12292
  0.7 14.0 %copy-start.6 = (bf16[64,16]{0,1:T(8,128)(2,1)S(1)}, bf16[64,16]{0,1:T(8,128)(2,1)}, u32[]{:S(2)}) copy-start(bf16[64,16]{0,1:T(8,128)(2,1)} %param.16) | copy-start | bytes 6148
  0.7 14.0 %copy-start.5 = (s32[64,16]{0,1:T(8,128)S(1)}, s32[64,16]{0,1:T(8,128)}, u32[]{:S(2)}) copy-start(s32[64,16]{0,1:T(8,128)} %param.17) | copy-start | bytes 12292
  3.0 34.8 %collective-permute-start = (bf16[32,1536]{1,0:T(8,128)(2,1)S(1)}, bf16[32,1536]{1,0:T(8,128)(2,1)}, u32[]{:S(2)}, u32[]{:S(2)}) collective-permute-start(bf16[32,1536]{1,0:T(8,128)(2,1)S(1)} %get-tuple-element.44), channel_id=1, source_target_pairs={{0,4},{4,8},{8,12},{12,16},{16,20},{20,24},{24,28},{28,32},{32,36}... | collective-permute-start | bytes 294920 | tf_op jit(solution)/shard_map/ppermute | solution.py:11
  8.0 29.9 %collective-permute-start.1 = (bf16[32,1536]{1,0:T(8,128)(2,1)S(1)}, bf16[32,1536]{1,0:T(8,128)(2,1)S(1)}, u32[]{:S(2)}, u32[]{:S(2)}) collective-permute-start(bf16[32,1536]{1,0:T(8,128)(2,1)S(1)} %get-tuple-element.45), channel_id=1, source_target_pairs={{0,508},{4,0},{8,4},{12,8},{16,12},{20,16},{24,20},{28,24},{32,28}... | collective-permute-start | bytes 294920 | tf_op jit(solution)/shard_map/ppermute | solution.py:11
  27.2 10.7 %copy-start.1 = (f32[128,1536]{1,0:T(8,128)}, f32[128,1536]{1,0:T(8,128)S(1)}, u32[]{:S(2)}) copy-start(f32[128,1536]{1,0:T(8,128)S(1)} %convolution_bitcast_fusion) | copy-start | bytes 2359300
  28.0 17.2 %collective-permute-start.2 = (f32[32,1536]{1,0:T(8,128)}, f32[32,1536]{1,0:T(8,128)}, u32[]{:S(2)}, u32[]{:S(2)}) collective-permute-start(f32[32,1536]{1,0:T(8,128)} %get-tuple-element.37), channel_id=1, source_target_pairs={{0,508},{4,0},{8,4},{12,8},{16,12},{20,16},{24,20},{28,24},{32,28}... | collective-permute-start | bytes 589832 | tf_op jit(solution)/shard_map/ppermute | solution.py:11
  35.9 10.4 %collective-permute-start.3 = (f32[32,1536]{1,0:T(8,128)S(1)}, f32[32,1536]{1,0:T(8,128)}, u32[]{:S(2)}, u32[]{:S(2)}) collective-permute-start(f32[32,1536]{1,0:T(8,128)S(1)} %get-tuple-element.36), channel_id=1, source_target_pairs={{0,4},{4,8},{8,12},{12,16},{16,20},{20,24},{24,28},{28,32},{32,36}... | collective-permute-start | bytes 589832 | tf_op jit(solution)/shard_map/ppermute | solution.py:11
  37.9 0.6 copy-start.3
  42.7 4.5 %copy-start.2 = (f32[64,1536]{1,0:T(8,128)S(1)}, f32[64,1536]{1,0:T(8,128)}, u32[]{:S(2)}) copy-start(f32[64,1536]{1,0:T(8,128)} %param.11) | copy-start | bytes 1179652

commit v6 on v5

--- a/solution.py
+++ b/solution.py
@@ -82,22 +82,18 @@
         preferred_element_type=jnp.float32,
     ).reshape(spheres, columns)
 
-    back = contrib[band : band + spheres]
-    back = back.at[spheres - band :].add(from_next)
-    back = back.at[:band].add(from_prev)
+    back = jnp.concatenate(
+        [contrib[band : band + band] + from_prev, contrib[band + band : band + spheres] + from_next], axis=0
+    )
 
     scattered = gain * coupled
     image = incident - scattered
     dual_image = incident - back
 
-    partial = jnp.stack(
-        [
-            jnp.sum(incident * incident),
-            jnp.sum(incident * scattered),
-            jnp.sum(incident * back),
-            jnp.sum(scattered * back),
-        ]
+    partial = jnp.sum(
+        jnp.stack([incident * incident, incident * scattered, incident * back, scattered * back]), axis=1
     )
+    partial = jnp.sum(lax.optimization_barrier(partial), axis=1)
     partial = lax.optimization_barrier(partial)
     total = exchange_sum(exchange_sum(partial, ("z", "core")), ("y", DIRS))
     rows = lax.optimization_barrier(jnp.broadcast_to(total[:, None], (4, columns)))

time: 84.6 us -> 93.8 us (1.11)
  waiting for transfers between devices: 0.01 us -> 6.93 us
  local copies, waits for them, and re-layouts: 11.3 us -> 15.8 us
  other arithmetic: 8.73 us -> 6.71 us
  blocking collectives: 31.9 us -> 30 us
  starting transfers between devices: 20.5 us -> 22 us
    ppermute x4, waiting for transfers between devices: 0.01 us -> 6.93 us  [passed_along(): lax.ppermute(x, axes, [(i, (i + by) % devices) for i in range(devices)])]
    scatter-add x2 -> x0, other arithmetic: 2.02 us -> none  [the longest x1 1.05 us: on_device(): back = back.at[spheres - band:].add(from_next)]
    mul x0 -> x1, local copies, waits for them, and re-layouts: none -> 1.96 us  [on_device(): scattered = gain * coupled]
    all_to_all x2, blocking collectives: 31.9 us -> 30 us  [exchange_sum(): return jnp.sum(lax.all_to_all(spread, axes, 0, 0, tiled=True), axis=0)]
    another operation x1 -> x2, other arithmetic: 2.66 us -> 1.13 us  [on_device(): jnp.stack([incident * incident, incident * scattered, incident * back, sc...]
    ppermute x4, starting transfers between devices: 20.5 us -> 22 us  [passed_along(): lax.ppermute(x, axes, [(i, (i + by) % devices) for i in range(devices)])]
    reshape x1, local copies, waits for them, and re-layouts: 0.17 us -> 1.21 us  [on_device(): coupled = jnp.einsum('ksdc,kcf->sdf', gathered.reshape(classes, spheres,...]
    unnamed x15 -> x13, local copies, waits for them, and re-layouts: 0.75 us -> 1.69 us
  transfers between devices with their start and end apart: 4 -> 4, of which waited for: 0 -> 1; matrix products, arithmetic and copies ran while one was open for 26% -> 8% of each run, Pallas kernels for 0% -> 0%
where the time goes in v6:
time: 93.8 us; the launch traced here: 93 us
  blocking collectives  30 us (32%)
  starting transfers between devices  22 us (23%)
  local copies, waits for them, and re-layouts  15.8 us (17%)
  matrix products  10.7 us (11%)
  waiting for transfers between devices  6.93 us (7%)
  other arithmetic  6.71 us (7%)
    all_to_all x2, blocking collectives, exchange_sum(): return jnp.sum(lax.all_to_all(spread, axes, 0, 0, tiled=True), axis=0)  30 us
    ppermute x4, starting transfers between devices, passed_along(): lax.ppermute(x, axes, [(i, (i + by) % devices) for i in range(devices)])  22 us
    ppermute x4, waiting for transfers between devices, passed_along(): lax.ppermute(x, axes, [(i, (i + by) % devices) for i in range(devices)])  6.93 us
    reshape x1, local copies, waits for them, and re-layouts, on_device(): moved = jnp.einsum('sdc,kfc->ksdf', weighted, translations, preferred_ele...  5.26 us
    dot_general x1, matrix products, on_device(): jnp.einsum('kse,ksx->ex', blocks, moved, precision=lax.Precision.HIGHEST,...  3.69 us
    reshape x1, local copies, waits for them, and re-layouts, on_device(): gathered.reshape(classes, spheres, groups, order)  3.34 us
    dot_general x1, matrix products, on_device(): jnp.einsum('sdc,kfc->ksdf', weighted, translations, preferred_element_typ...  2.68 us
    mul x1, local copies, waits for them, and re-layouts, on_device(): scattered = gain * coupled  1.96 us
  transfers between devices with their start and end apart: 4, of which 1 were waited for; matrix products, arithmetic and copies ran while one was open for 8% of the time, Pallas kernels for 0%

profile of v6, /device:TPU:1, one launch (start us, length us, event | category | flops | bytes accessed | tf_op | source)
XLA Modules:
  0.0 93.0 jit_solution(5541448814243419624)
XLA Ops:
  0.6 0.0 copy-start
  0.6 1.1 %convert_element_type.26 = bf16[64,1536]{1,0:T(8,128)(2,1)S(1)} convert(f32[64,1536]{1,0:T(8,128)} %param.7) | non-fusion elementwise | flops 98304 | bytes 589824 | tf_op jit(solution)/shard_map/convert_element_type | solution.py:38
  1.8 4.9 %collective-permute-start = (bf16[32,1536]{1,0:T(8,128)(2,1)S(1)}, bf16[32,1536]{1,0:T(8,128)(2,1)S(1)}, u32[]{:S(2)}, u32[]{:S(2)}) collective-permute-start(bf16[32,1536]{1,0:T(8,128)(2,1)S(1)} %get-tuple-element.18), channel_id=1, source_target_pairs={{0,4},{4,8},{8,12},{12,16},{16,20},{20,24},{24,28},{28,32},{32,36}... | collective-permute-start | bytes 294920 | tf_op jit(solution)/shard_map/ppermute | solution.py:11
  6.7 5.8 %collective-permute-start.1 = (bf16[32,1536]{1,0:T(8,128)(2,1)S(1)}, bf16[32,1536]{1,0:T(8,128)(2,1)S(1)}, u32[]{:S(2)}, u32[]{:S(2)}) collective-permute-start(bf16[32,1536]{1,0:T(8,128)(2,1)S(1)} %get-tuple-element.19), channel_id=1, source_target_pairs={{0,508},{4,0},{8,4},{12,8},{16,12},{20,16},{24,20},{28,24},{32,28}... | collective-permute-start | bytes 294920 | tf_op jit(solution)/shard_map/ppermute | solution.py:11
  12.5 0.7 convert_multiply_fusion
  13.2 0.1 copy.27
  13.3 0.7 select_select_fusion
  14.0 0.1 copy.25
  14.1 0.8 copy.26
  14.9 1.0 %fusion.24 = (bf16[8,64,128]{2,0,1:T(8,128)(2,1)S(1)}, f32[8,64,128]{2,0,1:T(8,128)}) fusion(bf16[64,16]{1,0:T(8,128)(2,1)S(1)} %copy.27, s32[64,16]{1,0:T(8,128)S(1)} %copy.26, s32[64,16]{1,0:T(8,128)S(1)} %copy.25), kind=kOutput, calls=%fused_computation.61 | convolution fusion | flops 2310144 | bytes 403456 | tf_op jit(solution)/shard_map/smk,sme->kse/dot_general | solution.py:56
  15.9 0.9 tile.4
  16.8 0.9 tile.10
  17.7 0.0 collective-permute-done
  17.7 0.0 collective-permute-done.1
  17.7 1.7 %convolution_convert_fusion = bf16[8,64,1536]{2,1,0:T(8,128)(2,1)} fusion(bf16[32,1536]{1,0:T(8,128)(2,1)S(1)} %collective-permute-done.1, bf16[64,1536]{1,0:T(8,128)(2,1)S(1)} %convert_element_type.26, bf16[32,1536]{1,0:T(8,128)(2,1)S(1)} %collective-permute-done, bf16[8,64,128]{2,0,1:T(8,128)(2,1)S(1)} %get-tuple-element.20), kind=kOutput, calls=%fused_computation | convolution fusion | flops 203292672 | bytes 2097152 | tf_op jit(solution)/shard_map/kse,ex->ksx/dot_general | solution.py:75
  19.4 0.0 copy-start.4
  19.4 3.3 %reshape.90 = bf16[8,64,8,192]{3,2,1,0:T(8,128)(2,1)S(1)} reshape(bf16[8,64,1536]{2,1,0:T(8,128)(2,1)} %convolution_convert_fusion) | data formatting | bytes 3145728 | tf_op jit(solution)/shard_map/reshape | solution.py:80
  22.8 0.0 copy-done
  22.8 0.0 copy-done.4
  22.8 0.0 copy-start.1
  22.8 1.6 %broadcast_multiply_fusion = (f32[64,8,192]{2,1,0:T(8,128)}, f32[64,8,192]{2,1,0:T(8,128)}) fusion(f32[64,192]{1,0:T(8,128)S(1)} %copy-done.4, bf16[8,64,8,192]{3,2,1,0:T(8,128)(2,1)S(1)} %reshape.90, bf16[8,192,192]{2,1,0:T(8,128)(2,1)S(1)} %copy-done), kind=kOutput, calls=%fused_computation.27 | convolution fusion | flops 302088192 | bytes 2998272 | tf_op jit(solution)/shard_map/ksdc,kcf->sdf/dot_general | solution.py:78
  24.4 1.2 %reshape.91 = f32[64,1536]{1,0:T(8,128)S(1)} reshape(f32[64,8,192]{2,1,0:T(8,128)} %get-tuple-element.23) | data formatting | bytes 786432 | tf_op jit(solution)/shard_map/reshape | solution.py:83
  25.6 0.0 copy-done.1
  25.6 1.1 %multiply_bitcast_fusion.1 = (f32[1,64,1536]{2,1,0:T(8,128)S(1)}, bf16[64,1536]{1,0:T(8,128)(2,1)S(1)}) fusion(f32[64,1536]{1,0:T(8,128)S(1)} %copy-done.1, f32[64,1536]{1,0:T(8,128)} %tile.10, f32[64,1536]{1,0:T(8,128)S(1)} %reshape.91), kind=kLoop, calls=%fused_computation.21 | loop fusion | flops 393216 | bytes 1769472 | tf_op jit(solution)/shard_map/stack | solution.py:94
  26.7 0.2 reshape.97
  26.9 2.7 %convolution_bitcast_fusion.1 = f32[8,64,8,192]{3,2,0,1:T(8,128)} fusion(bf16[8,192,192]{2,1,0:T(8,128)(2,1)S(1)} %copy-done, bf16[64,8,192,1]{2,1,0,3:T(8,128)(2,1)S(1)} %reshape.97), kind=kOutput, calls=%fused_computation.2 | convolution fusion | flops 301989888 | bytes 3932160 | tf_op jit(solution)/shard_map/sdc,kfc->ksdf/dot_general | solution.py:61
  29.6 0.0 copy-start.5
  29.6 5.3 %reshape.93 = f32[8,64,1536]{2,0,1:T(8,128)} reshape(f32[8,64,8,192]{3,2,0,1:T(8,128)} %convolution_bitcast_fusion.1) | data formatting | bytes 6291456 | tf_op jit(solution)/shard_map/reshape | solution.py:63
  34.9 0.0 copy-done.5
  34.9 3.7 %convolution_bitcast_fusion = f32[128,1536]{1,0:T(8,128)S(1)} fusion(f32[8,64,128]{2,0,1:T(8,128)S(1)} %copy-done.5, f32[8,64,1536]{2,0,1:T(8,128)} %reshape.93), kind=kOutput, calls=%fused_computation.1 | convolution fusion | flops 1207959552 | bytes 4194304 | tf_op jit(solution)/shard_map/kse,ksx->ex/dot_general | solution.py:64
  38.6 1.9 %collective-permute-start.2 = (f32[32,1536]{1,0:T(8,128)S(1)}, f32[32,1536]{1,0:T(8,128)S(1)}, u32[]{:S(2)}, u32[]{:S(2)}) collective-permute-start(f32[32,1536]{1,0:T(8,128)S(1)} %slice.43), channel_id=1, source_target_pairs={{0,4},{4,8},{8,12},{12,16},{16,20},{20,24},{24,28},{28,32},{32,36}... | collective-permute-start | bytes 589832 | tf_op jit(solution)/shard_map/ppermute | solution.py:11
  40.5 6.9 %collective-permute-done.2 = f32[32,1536]{1,0:T(8,128)S(1)} collective-permute-done((f32[32,1536]{1,0:T(8,128)S(1)}, f32[32,1536]{1,0:T(8,128)S(1)}, u32[]{:S(2)}, u32[]{:S(2)}) %collective-permute-start.2) | collective-permute-done | bytes 196640 | tf_op jit(solution)/shard_map/ppermute | solution.py:11
  47.5 9.4 %collective-permute-start.3 = (f32[32,1536]{1,0:T(8,128)S(1)}, f32[32,1536]{1,0:T(8,128)S(1)}, u32[]{:S(2)}, u32[]{:S(2)}) collective-permute-start(f32[32,1536]{1,0:T(8,128)S(1)} %get-tuple-element.11), channel_id=1, source_target_pairs={{0,508},{4,0},{8,4},{12,8},{16,12},{20,16},{24,20},{28,24},{32,28}... | collective-permute-start | bytes 589832 | tf_op jit(solution)/shard_map/ppermute | solution.py:11
  56.9 2.0 %mul.105 = f32[1,64,1536]{2,1,0:T(8,128)} reshape(f32[64,8,192]{2,1,0:T(8,128)} %get-tuple-element.22) | data formatting | bytes 786432 | tf_op jit(solution)/shard_map/mul | solution.py:89
  58.8 0.0 copy-start.3
  58.8 0.0 collective-permute-done.3
  58.9 0.0 copy-start.2
  58.9 0.1 multiply_bitcast_fusion.2
  59.0 0.9 copy-done.3
  59.9 0.7 maximum_reduce_fusion
  60.6 0.9 reduce_sum.37
  61.5 17.1 %all_to_all.12 = f32[32,1,4]{2,1,0:T(1,128)S(1)} all-to-all(f32[32,1,4]{2,1,0:T(1,128)S(1)} %broadcast_in_dim.20), channel_id=1, replica_groups=mesh['y'=4,'z'=16,'core'=2,'x'=4] {'z','core'}, dimensions={0} | all-to-all | bytes 1024 | tf_op jit(solution)/shard_map/all_to_all | solution.py:23
  78.6 0.1 reduce_sum.38
  78.6 12.9 %all_to_all.13 = f32[16,1,4]{2,1,0:T(1,128)S(1)} all-to-all(f32[16,1,4]{2,1,0:T(1,128)S(1)} %broadcast_in_dim.21), channel_id=1, replica_groups=mesh['y'=4,'z'=16,'core'=2,'x'=4] {'y','x'}, dimensions={0} | all-to-all | bytes 512 | tf_op jit(solution)/shard_map/all_to_all | solution.py:23
  91.6 0.1 broadcast_in_dim.22
  91.7 0.1 fusion.19
  91.8 0.0 copy-done.2
  91.8 1.2 %multiply_subtract_fusion = (f32[64,1536]{1,0:T(8,128)}, f32[64,1536]{1,0:T(8,128)}, f32[64,1536]{1,0:T(8,128)}, f32[64,1536]{1,0:T(8,128)}) fusion(f32[64,1536]{1,0:T(8,128)S(1)} %copy-done.1, f32[32,1536]{1,0:T(8,128)S(1)} %slice_add_fusion, f32[32,1536]{1,0:T(8,128)S(1)} %get-tuple-element.10, f32[1536]{0:T(1024)S(1)} %get-tuple-element.5, ...), kind=kLoop, calls=%fused_computation.17 | loop fusion | flops 1081344 | bytes 3158016 | tf_op jit(solution)/shard_map/sub | solution.py:111
  (8 shorter events, 0.2 us)
Async XLA Ops:
  0.6 22.2 %copy-start = (bf16[8,192,192]{2,1,0:T(8,128)(2,1)S(1)}, bf16[8,192,192]{2,1,0:T(8,128)(2,1)}, u32[]{:S(2)}) copy-start(bf16[8,192,192]{2,1,0:T(8,128)(2,1)} %param.9) | copy-start | bytes 1769476
  1.8 16.0 %collective-permute-start = (bf16[32,1536]{1,0:T(8,128)(2,1)S(1)}, bf16[32,1536]{1,0:T(8,128)(2,1)S(1)}, u32[]{:S(2)}, u32[]{:S(2)}) collective-permute-start(bf16[32,1536]{1,0:T(8,128)(2,1)S(1)} %get-tuple-element.18), channel_id=1, source_target_pairs={{0,4},{4,8},{8,12},{12,16},{16,20},{20,24},{24,28},{28,32},{32,36}... | collective-permute-start | bytes 294920 | tf_op jit(solution)/shard_map/ppermute | solution.py:11
  6.7 11.0 %collective-permute-start.1 = (bf16[32,1536]{1,0:T(8,128)(2,1)S(1)}, bf16[32,1536]{1,0:T(8,128)(2,1)S(1)}, u32[]{:S(2)}, u32[]{:S(2)}) collective-permute-start(bf16[32,1536]{1,0:T(8,128)(2,1)S(1)} %get-tuple-element.19), channel_id=1, source_target_pairs={{0,508},{4,0},{8,4},{12,8},{16,12},{20,16},{24,20},{28,24},{32,28}... | collective-permute-start | bytes 294920 | tf_op jit(solution)/shard_map/ppermute | solution.py:11
  19.4 3.4 %copy-start.4 = (f32[64,192]{1,0:T(8,128)S(1)}, f32[64,192]{1,0:T(8,128)}, u32[]{:S(2)}) copy-start(f32[64,192]{1,0:T(8,128)} %param.8) | copy-start | bytes 147460
  22.8 2.8 %copy-start.1 = (f32[64,1536]{1,0:T(8,128)S(1)}, f32[64,1536]{1,0:T(8,128)}, u32[]{:S(2)}) copy-start(f32[64,1536]{1,0:T(8,128)} %param.7) | copy-start | bytes 1179652
  29.6 5.3 %copy-start.5 = (f32[8,64,128]{2,0,1:T(8,128)S(1)}, f32[8,64,128]{2,0,1:T(8,128)}, u32[]{:S(2)}) copy-start(f32[8,64,128]{2,0,1:T(8,128)} %get-tuple-element.21) | copy-start | bytes 786436
  38.6 8.8 %collective-permute-start.2 = (f32[32,1536]{1,0:T(8,128)S(1)}, f32[32,1536]{1,0:T(8,128)S(1)}, u32[]{:S(2)}, u32[]{:S(2)}) collective-permute-start(f32[32,1536]{1,0:T(8,128)S(1)} %slice.43), channel_id=1, source_target_pairs={{0,4},{4,8},{8,12},{12,16},{16,20},{20,24},{24,28},{28,32},{32,36}... | collective-permute-start | bytes 589832 | tf_op jit(solution)/shard_map/ppermute | solution.py:11
  47.5 11.4 %collective-permute-start.3 = (f32[32,1536]{1,0:T(8,128)S(1)}, f32[32,1536]{1,0:T(8,128)S(1)}, u32[]{:S(2)}, u32[]{:S(2)}) collective-permute-start(f32[32,1536]{1,0:T(8,128)S(1)} %get-tuple-element.11), channel_id=1, source_target_pairs={{0,508},{4,0},{8,4},{12,8},{16,12},{20,16},{24,20},{28,24},{32,28}... | collective-permute-start | bytes 589832 | tf_op jit(solution)/shard_map/ppermute | solution.py:11
  58.8 1.0 %copy-start.3 = (f32[1,64,1536]{2,1,0:T(8,128)S(1)}, f32[1,64,1536]{2,1,0:T(8,128)}, u32[]{:S(2)}) copy-start(f32[1,64,1536]{2,1,0:T(8,128)} %mul.105) | copy-start | bytes 1179652
  58.9 32.9 %copy-start.2 = (f32[64,1536]{1,0:T(8,128)S(1)}, f32[64,1536]{1,0:T(8,128)}, u32[]{:S(2)}) copy-start(f32[64,1536]{1,0:T(8,128)} %tile.10) | copy-start | bytes 1179652

commit v7 on v6

--- a/solution.py
+++ b/solution.py
@@ -72,6 +72,7 @@
     from_prev = passed_along(contrib[band + spheres :], CELLS, 1)
 
     padded = jnp.concatenate([from_prev_rows, source, from_next_rows], axis=0)
+    padded, blocks_half, unused = lax.optimization_barrier((padded, blocks_half, contrib))
     gathered = jnp.einsum(
         "kse,ex->ksx", blocks_half, padded, preferred_element_type=jnp.float32
     ).astype(jnp.bfloat16)
@@ -82,9 +83,9 @@
         preferred_element_type=jnp.float32,
     ).reshape(spheres, columns)
 
-    back = jnp.concatenate(
-        [contrib[band : band + band] + from_prev, contrib[band + band : band + spheres] + from_next], axis=0
-    )
+    back = contrib[band : band + spheres]
+    back = back.at[spheres - band :].add(from_next)
+    back = back.at[:band].add(from_prev)
 
     scattered = gain * coupled
     image = incident - scattered

time: 93.8 us -> 82.6 us (0.88)
  waiting for transfers between devices: 6.93 us -> 0.01 us
  local copies, waits for them, and re-layouts: 15.8 us -> 11.7 us
  blocking collectives: 30 us -> 33.5 us
  other arithmetic: 6.71 us -> 4.95 us
  starting transfers between devices: 22 us -> 20.5 us
    ppermute x4, waiting for transfers between devices: 6.93 us -> 0.01 us  [passed_along(): lax.ppermute(x, axes, [(i, (i + by) % devices) for i in range(devices)])]
    all_to_all x2, blocking collectives: 30 us -> 33.5 us  [exchange_sum(): return jnp.sum(lax.all_to_all(spread, axes, 0, 0, tiled=True), axis=0)]
    mul x1 -> x0, local copies, waits for them, and re-layouts: 1.96 us -> none  [on_device(): scattered = gain * coupled]
    scatter-add x0 -> x2, other arithmetic: none -> 1.92 us  [the longest x1 0.97 us: on_device(): back = back.at[:band].add(from_prev)]
    unnamed x13 -> x17, local copies, waits for them, and re-layouts: 1.69 us -> 0.12 us
    dot_general x1, matrix products: 1.59 us -> 3.12 us  [on_device(): jnp.einsum('ksdc,kcf->sdf', gathered.reshape(classes, spheres, groups, or...]
    ppermute x4, starting transfers between devices: 22 us -> 20.5 us  [passed_along(): lax.ppermute(x, axes, [(i, (i + by) % devices) for i in range(devices)])]
    dot_general x1, matrix products: 1.71 us -> 0.55 us  [on_device(): jnp.einsum('kse,ex->ksx', blocks_half, padded, preferred_element_type=jnp...]
  transfers between devices with their start and end apart: 4 -> 4, of which waited for: 1 -> 0; matrix products, arithmetic and copies ran while one was open for 8% -> 27% of each run, Pallas kernels for 0% -> 0%
where the time goes in v7:
time: 82.6 us; the launch traced here: 82.1 us
  blocking collectives  33.5 us (41%)
  starting transfers between devices  20.5 us (25%)
  local copies, waits for them, and re-layouts  11.7 us (14%)
  matrix products  10.6 us (13%)
  other arithmetic  4.95 us (6%)
  between operations  0.91 us (1%)
    all_to_all x2, blocking collectives, exchange_sum(): return jnp.sum(lax.all_to_all(spread, axes, 0, 0, tiled=True), axis=0)  33.5 us
    ppermute x4, starting transfers between devices, passed_along(): lax.ppermute(x, axes, [(i, (i + by) % devices) for i in range(devices)])  20.5 us
    reshape x1, local copies, waits for them, and re-layouts, on_device(): moved = jnp.einsum('sdc,kfc->ksdf', weighted, translations, preferred_ele...  5.19 us
    dot_general x1, matrix products, on_device(): jnp.einsum('kse,ksx->ex', blocks, moved, precision=lax.Precision.HIGHEST,...  3.69 us
    dot_general x1, matrix products, on_device(): jnp.einsum('ksdc,kcf->sdf', gathered.reshape(classes, spheres, groups, or...  3.12 us
    reshape x1, local copies, waits for them, and re-layouts, on_device(): gathered.reshape(classes, spheres, groups, order)  2.69 us
    dot_general x1, matrix products, on_device(): jnp.einsum('sdc,kfc->ksdf', weighted, translations, preferred_element_typ...  2.68 us
  transfers between devices with their start and end apart: 4, of which 0 were waited for; matrix products, arithmetic and copies ran while one was open for 27% of the time, Pallas kernels for 0%

profile of v7, /device:TPU:1, one launch (start us, length us, event | category | flops | bytes accessed | tf_op | source)
XLA Modules:
  0.0 82.1 jit_solution(15577895153246316879)
XLA Ops:
  0.6 0.0 copy-start
  0.6 0.0 copy-start.5
  0.7 0.0 copy-start.7
  0.7 0.0 copy-start.4
  0.7 0.0 copy-start.6
  0.7 0.9 %tile.4 = f32[64,8,192]{2,1,0:T(8,128)S(1)} broadcast(f32[64,192]{1,0:T(8,128)} %param.12), dimensions={0,2} | broadcast | bytes 442368 | tf_op jit(solution)/shard_map/tile | solution.py:59
  1.6 0.2 tile.10
  1.8 1.2 %fusion.22 = (bf16[64,1536]{1,0:T(8,128)(2,1)S(1)}, bf16[64,1536]{1,0:T(8,128)(2,1)S(1)}) fusion(f32[64,1536]{1,0:T(8,128)} %param.11, f32[64,1536]{1,0:T(8,128)S(1)} %tile.10), kind=kLoop, calls=%fused_computation.57 | loop fusion | flops 294912 | bytes 1179648 | tf_op jit(solution)/shard_map/convert_element_type | solution.py:38
  3.0 8.8 %collective-permute-start.1 = (bf16[32,1536]{1,0:T(8,128)(2,1)S(1)}, bf16[32,1536]{1,0:T(8,128)(2,1)S(1)}, u32[]{:S(2)}, u32[]{:S(2)}) collective-permute-start(bf16[32,1536]{1,0:T(8,128)(2,1)S(1)} %get-tuple-element.49), channel_id=1, source_target_pairs={{0,508},{4,0},{8,4},{12,8},{16,12},{20,16},{24,20},{28,24},{32,28}... | collective-permute-start | bytes 294920 | tf_op jit(solution)/shard_map/ppermute | solution.py:11
  11.8 1.9 %collective-permute-start = (bf16[32,1536]{1,0:T(8,128)(2,1)S(1)}, bf16[32,1536]{1,0:T(8,128)(2,1)S(1)}, u32[]{:S(2)}, u32[]{:S(2)}) collective-permute-start(bf16[32,1536]{1,0:T(8,128)(2,1)S(1)} %get-tuple-element.48), channel_id=1, source_target_pairs={{0,4},{4,8},{8,12},{12,16},{16,20},{20,24},{24,28},{28,32},{32,36}... | collective-permute-start | bytes 294920 | tf_op jit(solution)/shard_map/ppermute | solution.py:11
  13.7 0.0 copy-done.5
  13.8 0.0 copy-done.7
  13.8 0.1 copy.27
  13.9 0.0 copy-done.4
  13.9 0.1 copy.26
  14.0 0.0 copy-done.6
  14.0 0.1 copy.25
  14.1 0.2 reshape.93
  14.3 0.0 copy-done
  14.3 2.7 %convolution_bitcast_fusion.1 = f32[8,64,8,192]{3,2,0,1:T(8,128)} fusion(bf16[8,192,192]{2,1,0:T(8,128)(2,1)S(1)} %copy-done, bf16[64,8,192,1]{2,1,0,3:T(8,128)(2,1)S(1)} %reshape.93), kind=kOutput, calls=%fused_computation.2 | convolution fusion | flops 301989888 | bytes 3932160 | tf_op jit(solution)/shard_map/sdc,kfc->ksdf/dot_general | solution.py:61
  17.0 5.2 %reshape.90 = f32[8,64,1536]{2,0,1:T(8,128)} reshape(f32[8,64,8,192]{3,2,0,1:T(8,128)} %convolution_bitcast_fusion.1) | data formatting | bytes 6291456 | tf_op jit(solution)/shard_map/reshape | solution.py:63
  22.2 0.5 fusion.24
  22.7 3.7 %convolution_bitcast_fusion = f32[128,1536]{1,0:T(8,128)S(1)} fusion(f32[8,64,128]{2,0,1:T(8,128)S(1)} %get-tuple-element.51, f32[8,64,1536]{2,0,1:T(8,128)} %reshape.90), kind=kOutput, calls=%fused_computation.1 | convolution fusion | flops 1207959552 | bytes 4194304 | tf_op jit(solution)/shard_map/kse,ksx->ex/dot_general | solution.py:64
  26.4 0.0 copy-start.1
  26.4 0.8 %fusion.21 = (f32[32,1536]{1,0:T(8,128)}, f32[32,1536]{1,0:T(8,128)}) fusion(f32[128,1536]{1,0:T(8,128)S(1)} %convolution_bitcast_fusion), kind=kLoop, calls=%fused_computation.56 | loop fusion | bytes 786432 | tf_op jit(solution)/shard_map/slice | solution.py:72
  27.3 7.9 %collective-permute-start.2 = (f32[32,1536]{1,0:T(8,128)}, f32[32,1536]{1,0:T(8,128)}, u32[]{:S(2)}, u32[]{:S(2)}) collective-permute-start(f32[32,1536]{1,0:T(8,128)} %get-tuple-element.40), channel_id=1, source_target_pairs={{0,508},{4,0},{8,4},{12,8},{16,12},{20,16},{24,20},{28,24},{32,28}... | collective-permute-start | bytes 589832 | tf_op jit(solution)/shard_map/ppermute | solution.py:11
  35.2 1.9 %collective-permute-start.3 = (f32[32,1536]{1,0:T(8,128)}, f32[32,1536]{1,0:T(8,128)}, u32[]{:S(2)}, u32[]{:S(2)}) collective-permute-start(f32[32,1536]{1,0:T(8,128)} %get-tuple-element.39), channel_id=1, source_target_pairs={{0,4},{4,8},{8,12},{12,16},{16,20},{20,24},{24,28},{28,32},{32,36}... | collective-permute-start | bytes 589832 | tf_op jit(solution)/shard_map/ppermute | solution.py:11
  37.1 0.0 collective-permute-done.1
  37.1 0.0 collective-permute-done
  37.2 0.5 convolution_convert_fusion
  37.7 2.7 %reshape.91 = bf16[8,64,8,192]{3,2,1,0:T(8,128)(2,1)} reshape(bf16[8,64,1536]{2,1,0:T(8,128)(2,1)S(1)} %convolution_convert_fusion) | data formatting | bytes 3145728 | tf_op jit(solution)/shard_map/reshape | solution.py:81
  40.4 3.1 %convolution_bitcast_fusion.2 = f32[64,8,192]{2,1,0:T(8,128)} fusion(bf16[8,64,8,192]{3,2,1,0:T(8,128)(2,1)} %reshape.91, bf16[8,192,192]{2,1,0:T(8,128)(2,1)S(1)} %copy-done), kind=kOutput, calls=%fused_computation.4 | convolution fusion | flops 301989888 | bytes 2555904 | tf_op jit(solution)/shard_map/ksdc,kcf->sdf/dot_general | solution.py:79
  43.6 1.2 %reshape.92 = f32[64,1536]{1,0:T(8,128)S(1)} reshape(f32[64,8,192]{2,1,0:T(8,128)} %convolution_bitcast_fusion.2) | data formatting | bytes 786432 | tf_op jit(solution)/shard_map/reshape | solution.py:84
  44.8 0.0 collective-permute-done.2
  44.8 0.0 copy-done.2
  44.8 0.0 slice-done
  44.8 1.0 %fusion.6 = f32[64,1536]{1,0:T(8,128)S(1)} fusion(f32[64,1536]{1,0:T(8,128)S(1)} %slice-done, f32[32,1536]{1,0:T(8,128)} %collective-permute-done.2, f32[128,1536]{1,0:T(8,128)S(1)} %copy-done.2), kind=kLoop, calls=%fused_computation.26 | loop fusion | flops 49152 | bytes 589824 | tf_op jit(solution)/shard_map/scatter-add | solution.py:87
  45.7 0.0 collective-permute-done.3
  45.8 1.0 %fusion.5 = f32[64,1536]{1,0:T(8,128)S(1)} fusion(f32[64,1536]{1,0:T(8,128)S(1)} %fusion.6, f32[32,1536]{1,0:T(8,128)} %collective-permute-done.3), kind=kLoop, calls=%fused_computation.24 | loop fusion | flops 49152 | bytes 589824 | tf_op jit(solution)/shard_map/scatter-add | solution.py:88
  46.7 0.2 multiply_bitcast_fusion.2
  46.9 0.1 maximum_reduce_fusion
  47.1 0.1 reduce_sum.37
  47.2 19.6 %all_to_all.12 = f32[32,1,4]{2,1,0:T(1,128)S(1)} all-to-all(f32[32,1,4]{2,1,0:T(1,128)S(1)} %broadcast_in_dim.20), channel_id=1, replica_groups=mesh['y'=4,'z'=16,'core'=2,'x'=4] {'z','core'}, dimensions={0} | all-to-all | bytes 1024 | tf_op jit(solution)/shard_map/all_to_all | solution.py:23
  66.8 0.1 reduce_sum.38
  66.9 13.8 %all_to_all.13 = f32[16,1,4]{2,1,0:T(1,128)S(1)} all-to-all(f32[16,1,4]{2,1,0:T(1,128)S(1)} %broadcast_in_dim.21), channel_id=1, replica_groups=mesh['y'=4,'z'=16,'core'=2,'x'=4] {'y','x'}, dimensions={0} | all-to-all | bytes 512 | tf_op jit(solution)/shard_map/all_to_all | solution.py:23
  80.8 0.1 broadcast_in_dim.22
  80.8 0.1 fusion.18
  80.9 1.2 %multiply_subtract_fusion = (f32[64,1536]{1,0:T(8,128)}, f32[64,1536]{1,0:T(8,128)}, f32[64,1536]{1,0:T(8,128)}, f32[64,1536]{1,0:T(8,128)}) fusion(f32[64,1536]{1,0:T(8,128)S(1)} %copy-done.3, f32[64,1536]{1,0:T(8,128)S(1)} %fusion.5, f32[1536]{0:T(1024)S(1)} %get-tuple-element.33, f32[1536]{0:T(1024)S(1)} %get-tuple-element.32, f32[64,1536]{1,0:T(8,128)S(1)} %tile.10, ...), kind=kLoop, calls=%fused_computation.12 | loop fusion | flops 983040 | bytes 3158016 | tf_op jit(solution)/shard_map/sub | solution.py:112
  (12 shorter events, 0.1 us)
Async XLA Ops:
  0.6 13.7 %copy-start = (bf16[8,192,192]{2,1,0:T(8,128)(2,1)S(1)}, bf16[8,192,192]{2,1,0:T(8,128)(2,1)}, u32[]{:S(2)}) copy-start(bf16[8,192,192]{2,1,0:T(8,128)(2,1)} %param.13) | copy-start | bytes 1769476
  0.6 13.1 %copy-start.5 = (s32[64,16]{0,1:T(8,128)S(1)}, s32[64,16]{0,1:T(8,128)}, u32[]{:S(2)}) copy-start(s32[64,16]{0,1:T(8,128)} %param.17) | copy-start | bytes 12292
  0.7 13.1 %copy-start.7 = (bf16[64,16]{0,1:T(8,128)(2,1)S(1)}, bf16[64,16]{0,1:T(8,128)(2,1)}, u32[]{:S(2)}) copy-start(bf16[64,16]{0,1:T(8,128)(2,1)} %param.16) | copy-start | bytes 6148
  0.7 13.2 %copy-start.4 = (s32[64,16]{0,1:T(8,128)S(1)}, s32[64,16]{0,1:T(8,128)}, u32[]{:S(2)}) copy-start(s32[64,16]{0,1:T(8,128)} %param.15) | copy-start | bytes 12292
  0.7 13.3 %copy-start.6 = (s32[64,16]{0,1:T(8,128)S(1)}, s32[64,16]{0,1:T(8,128)}, u32[]{:S(2)}) copy-start(s32[64,16]{0,1:T(8,128)} %param.14) | copy-start | bytes 12292
  3.0 34.1 %collective-permute-start.1 = (bf16[32,1536]{1,0:T(8,128)(2,1)S(1)}, bf16[32,1536]{1,0:T(8,128)(2,1)S(1)}, u32[]{:S(2)}, u32[]{:S(2)}) collective-permute-start(bf16[32,1536]{1,0:T(8,128)(2,1)S(1)} %get-tuple-element.49), channel_id=1, source_target_pairs={{0,508},{4,0},{8,4},{12,8},{16,12},{20,16},{24,20},{28,24},{32,28}... | collective-permute-start | bytes 294920 | tf_op jit(solution)/shard_map/ppermute | solution.py:11
  11.8 25.3 %collective-permute-start = (bf16[32,1536]{1,0:T(8,128)(2,1)S(1)}, bf16[32,1536]{1,0:T(8,128)(2,1)S(1)}, u32[]{:S(2)}, u32[]{:S(2)}) collective-permute-start(bf16[32,1536]{1,0:T(8,128)(2,1)S(1)} %get-tuple-element.48), channel_id=1, source_target_pairs={{0,4},{4,8},{8,12},{12,16},{16,20},{20,24},{24,28},{28,32},{32,36}... | collective-permute-start | bytes 294920 | tf_op jit(solution)/shard_map/ppermute | solution.py:11
  26.4 11.3 %copy-start.1 = (f32[128,1536]{1,0:T(8,128)}, f32[128,1536]{1,0:T(8,128)S(1)}, u32[]{:S(2)}) copy-start(f32[128,1536]{1,0:T(8,128)S(1)} %convolution_bitcast_fusion) | copy-start | bytes 2359300
  27.3 17.5 %collective-permute-start.2 = (f32[32,1536]{1,0:T(8,128)}, f32[32,1536]{1,0:T(8,128)}, u32[]{:S(2)}, u32[]{:S(2)}) collective-permute-start(f32[32,1536]{1,0:T(8,128)} %get-tuple-element.40), channel_id=1, source_target_pairs={{0,508},{4,0},{8,4},{12,8},{16,12},{20,16},{24,20},{28,24},{32,28}... | collective-permute-start | bytes 589832 | tf_op jit(solution)/shard_map/ppermute | solution.py:11
  35.2 10.6 %collective-permute-start.3 = (f32[32,1536]{1,0:T(8,128)}, f32[32,1536]{1,0:T(8,128)}, u32[]{:S(2)}, u32[]{:S(2)}) collective-permute-start(f32[32,1536]{1,0:T(8,128)} %get-tuple-element.39), channel_id=1, source_target_pairs={{0,4},{4,8},{8,12},{12,16},{16,20},{20,24},{24,28},{28,32},{32,36}... | collective-permute-start | bytes 589832 | tf_op jit(solution)/shard_map/ppermute | solution.py:11
  40.4 4.4 %copy-start.2 = (f32[128,1536]{1,0:T(8,128)S(1)}, f32[128,1536]{1,0:T(8,128)}, u32[]{:S(2)}) copy-start(f32[128,1536]{1,0:T(8,128)} %copy-done.1) | copy-start | bytes 2359300
  40.4 4.4 %slice-start = ((f32[128,1536]{1,0:T(8,128)}), f32[64,1536]{1,0:T(8,128)S(1)}, s32[]{:S(2)}) async-start(f32[128,1536]{1,0:T(8,128)} %copy-done.1), calls=%async_computation.2 | async-start | bytes 786432 | tf_op jit(solution)/shard_map/slice | solution.py:86
  40.4 6.3 %copy-start.3 = (f32[64,1536]{1,0:T(8,128)S(1)}, f32[64,1536]{1,0:T(8,128)}, u32[]{:S(2)}) copy-start(f32[64,1536]{1,0:T(8,128)} %param.11) | copy-start | bytes 1179652

commit v8 on v7

--- a/solution.py
+++ b/solution.py
@@ -36,8 +36,6 @@
     cell_count = lax.axis_size("y") * lax.axis_size("z") * lax.axis_size("core")
 
     source = incident.astype(jnp.bfloat16)
-    from_prev_rows = passed_along(source[spheres - band :], CELLS, 1)
-    from_next_rows = passed_along(source[:band], CELLS, -1)
 
     owner = pair_sphere // spheres
     within = pair_sphere % spheres
@@ -68,14 +66,19 @@
         precision=lax.Precision.HIGHEST,
         preferred_element_type=jnp.float32,
     )
-    from_next = passed_along(contrib[:band], CELLS, -1)
-    from_prev = passed_along(contrib[band + spheres :], CELLS, 1)
+    sends = lax.optimization_barrier((source[spheres - band :], source[:band], contrib[:band], contrib[band + spheres :]))
+    from_prev_rows = passed_along(sends[0], CELLS, 1)
+    from_next_rows = passed_along(sends[1], CELLS, -1)
+    from_next = passed_along(sends[2], CELLS, -1)
+    from_prev = passed_along(sends[3], CELLS, 1)
 
-    padded = jnp.concatenate([from_prev_rows, source, from_next_rows], axis=0)
-    padded, blocks_half, unused = lax.optimization_barrier((padded, blocks_half, contrib))
-    gathered = jnp.einsum(
-        "kse,ex->ksx", blocks_half, padded, preferred_element_type=jnp.float32
-    ).astype(jnp.bfloat16)
+    own_part = jnp.einsum(
+        "kse,ex->ksx", blocks_half[:, :, band : band + spheres], source, preferred_element_type=jnp.float32
+    )
+    halo = jnp.concatenate([from_prev_rows, from_next_rows], axis=0)
+    halo_blocks = jnp.concatenate([blocks_half[:, :, :band], blocks_half[:, :, band + spheres :]], axis=2)
+    halo_part = jnp.einsum("kse,ex->ksx", halo_blocks, halo, preferred_element_type=jnp.float32)
+    gathered = (own_part + halo_part).astype(jnp.bfloat16)
     coupled = jnp.einsum(
         "ksdc,kcf->sdf",
         gathered.reshape(classes, spheres, groups, order),

time: 82.6 us -> 84.1 us (1.018)
  blocking collectives: 33.5 us -> 31.9 us
  other arithmetic: 4.95 us -> 6.5 us
  local copies, waits for them, and re-layouts: 11.7 us -> 12.6 us
    all_to_all x2, blocking collectives: 33.5 us -> 31.9 us  [exchange_sum(): return jnp.sum(lax.all_to_all(spread, axes, 0, 0, tiled=True), axis=0)]
  transfers between devices with their start and end apart: 4 -> 4, of which waited for: 0 -> 0; matrix products, arithmetic and copies ran while one was open for 27% -> 11% of each run, Pallas kernels for 0% -> 0%
where the time goes in v8:
time: 84.1 us; the launch traced here: 83.4 us
  blocking collectives  31.9 us (38%)
  starting transfers between devices  20.5 us (24%)
  local copies, waits for them, and re-layouts  12.6 us (15%)
  matrix products  11.1 us (13%)
  other arithmetic  6.5 us (8%)
  between operations  0.85 us (1%)
    all_to_all x2, blocking collectives, exchange_sum(): return jnp.sum(lax.all_to_all(spread, axes, 0, 0, tiled=True), axis=0)  31.9 us
    ppermute x4, starting transfers between devices, passed_along(): lax.ppermute(x, axes, [(i, (i + by) % devices) for i in range(devices)])  20.5 us
    reshape x1, local copies, waits for them, and re-layouts, on_device(): moved = jnp.einsum('sdc,kfc->ksdf', weighted, translations, preferred_ele...  5.22 us
    dot_general x1, matrix products, on_device(): jnp.einsum('kse,ksx->ex', blocks, moved, precision=lax.Precision.HIGHEST,...  3.69 us
    dot_general x1, matrix products, on_device(): jnp.einsum('ksdc,kcf->sdf', gathered.reshape(classes, spheres, groups, or...  3.14 us
    reshape x1, local copies, waits for them, and re-layouts, on_device(): gathered.reshape(classes, spheres, groups, order)  2.71 us
    dot_general x1, matrix products, on_device(): jnp.einsum('sdc,kfc->ksdf', weighted, translations, preferred_element_typ...  2.68 us
  transfers between devices with their start and end apart: 4, of which 0 were waited for; matrix products, arithmetic and copies ran while one was open for 11% of the time, Pallas kernels for 0%

profile of v8, /device:TPU:1, one launch (start us, length us, event | category | flops | bytes accessed | tf_op | source)
XLA Modules:
  0.0 83.4 jit_solution(14195401015291601047)
XLA Ops:
  0.6 0.0 copy-start
  0.7 0.8 select_select_fusion
  1.4 0.1 copy.27
  1.5 0.8 copy.28
  2.3 0.7 convert_multiply_fusion
  3.0 0.1 copy.29
  3.1 0.9 %tile.4 = f32[64,8,192]{2,1,0:T(8,128)S(1)} broadcast(f32[64,192]{1,0:T(8,128)} %param.12), dimensions={0,2} | broadcast | bytes 442368 | tf_op jit(solution)/shard_map/tile | solution.py:57
  4.0 0.2 tile.10
  4.2 1.2 %fusion.28 = (bf16[64,1536]{1,0:T(8,128)(2,1)S(1)}, bf16[64,1536]{1,0:T(8,128)(2,1)S(1)}) fusion(f32[64,1536]{1,0:T(8,128)} %param.11, f32[64,1536]{1,0:T(8,128)S(1)} %tile.10), kind=kLoop, calls=%fused_computation.64 | loop fusion | flops 294912 | bytes 1179648 | tf_op jit(solution)/shard_map/convert_element_type | solution.py:38
  5.4 0.2 reshape.94
  5.6 0.0 copy-done
  5.6 2.7 %convolution_bitcast_fusion.1 = f32[8,64,8,192]{3,2,0,1:T(8,128)} fusion(bf16[8,192,192]{2,1,0:T(8,128)(2,1)S(1)} %copy-done, bf16[64,8,192,1]{2,1,0,3:T(8,128)(2,1)S(1)} %reshape.94), kind=kOutput, calls=%fused_computation.3 | convolution fusion | flops 301989888 | bytes 3932160 | tf_op jit(solution)/shard_map/sdc,kfc->ksdf/dot_general | solution.py:59
  8.3 5.2 %reshape.90 = f32[8,64,1536]{2,0,1:T(8,128)} reshape(f32[8,64,8,192]{3,2,0,1:T(8,128)} %convolution_bitcast_fusion.1) | data formatting | bytes 6291456 | tf_op jit(solution)/shard_map/reshape | solution.py:61
  13.5 0.5 fusion.31
  14.0 3.7 %convolution_bitcast_fusion = f32[128,1536]{1,0:T(8,128)S(1)} fusion(f32[8,64,128]{2,0,1:T(8,128)S(1)} %get-tuple-element.57, f32[8,64,1536]{2,0,1:T(8,128)} %reshape.90), kind=kOutput, calls=%fused_computation.2 | convolution fusion | flops 1207959552 | bytes 4194304 | tf_op jit(solution)/shard_map/kse,ksx->ex/dot_general | solution.py:62
  17.7 0.0 copy-start.1
  17.7 0.8 %fusion.27 = (f32[32,1536]{1,0:T(8,128)}, f32[32,1536]{1,0:T(8,128)}) fusion(f32[128,1536]{1,0:T(8,128)S(1)} %convolution_bitcast_fusion), kind=kLoop, calls=%fused_computation.63 | loop fusion | bytes 786432 | tf_op jit(solution)/shard_map/slice | solution.py:69
  18.6 4.9 %collective-permute-start = (bf16[32,1536]{1,0:T(8,128)(2,1)S(1)}, bf16[32,1536]{1,0:T(8,128)(2,1)S(1)}, u32[]{:S(2)}, u32[]{:S(2)}) collective-permute-start(bf16[32,1536]{1,0:T(8,128)(2,1)S(1)} %get-tuple-element.32), channel_id=1, source_target_pairs={{0,4},{4,8},{8,12},{12,16},{16,20},{20,24},{24,28},{28,32},{32,36}... | collective-permute-start | bytes 294920 | tf_op jit(solution)/shard_map/ppermute | solution.py:11
  23.5 5.8 %collective-permute-start.1 = (bf16[32,1536]{1,0:T(8,128)(2,1)S(1)}, bf16[32,1536]{1,0:T(8,128)(2,1)S(1)}, u32[]{:S(2)}, u32[]{:S(2)}) collective-permute-start(bf16[32,1536]{1,0:T(8,128)(2,1)S(1)} %get-tuple-element.33), channel_id=1, source_target_pairs={{0,508},{4,0},{8,4},{12,8},{16,12},{20,16},{24,20},{28,24},{32,28}... | collective-permute-start | bytes 294920 | tf_op jit(solution)/shard_map/ppermute | solution.py:11
  29.3 7.9 %collective-permute-start.2 = (f32[32,1536]{1,0:T(8,128)}, f32[32,1536]{1,0:T(8,128)}, u32[]{:S(2)}, u32[]{:S(2)}) collective-permute-start(f32[32,1536]{1,0:T(8,128)} %get-tuple-element.34), channel_id=1, source_target_pairs={{0,508},{4,0},{8,4},{12,8},{16,12},{20,16},{24,20},{28,24},{32,28}... | collective-permute-start | bytes 589832 | tf_op jit(solution)/shard_map/ppermute | solution.py:11
  37.2 1.9 %collective-permute-start.3 = (f32[32,1536]{1,0:T(8,128)}, f32[32,1536]{1,0:T(8,128)}, u32[]{:S(2)}, u32[]{:S(2)}) collective-permute-start(f32[32,1536]{1,0:T(8,128)} %get-tuple-element.35), channel_id=1, source_target_pairs={{0,4},{4,8},{8,12},{12,16},{16,20},{20,24},{24,28},{28,32},{32,36}... | collective-permute-start | bytes 589832 | tf_op jit(solution)/shard_map/ppermute | solution.py:11
  39.2 0.1 fusion.30
  39.3 0.1 slice.89
  39.4 0.5 fusion.9
  39.9 0.0 copy-done.1
  39.9 0.1 pad_maximum_fusion
  40.1 0.0 collective-permute-done
  40.1 0.0 collective-permute-done.1
  40.1 0.5 fusion
  40.6 2.7 %reshape.91 = bf16[8,64,8,192]{3,2,1,0:T(8,128)(2,1)} reshape(bf16[8,64,1536]{2,1,0:T(8,128)(2,1)S(1)} %fusion) | data formatting | bytes 3145728 | tf_op jit(solution)/shard_map/reshape | solution.py:84
  43.3 3.1 %convolution_bitcast_fusion.2 = f32[64,8,192]{2,1,0:T(8,128)} fusion(bf16[8,64,8,192]{3,2,1,0:T(8,128)(2,1)} %reshape.91, bf16[8,192,192]{2,1,0:T(8,128)(2,1)S(1)} %copy-done), kind=kOutput, calls=%fused_computation.5 | convolution fusion | flops 301989888 | bytes 2555904 | tf_op jit(solution)/shard_map/ksdc,kcf->sdf/dot_general | solution.py:82
  46.5 1.2 %reshape.92 = f32[64,1536]{1,0:T(8,128)S(1)} reshape(f32[64,8,192]{2,1,0:T(8,128)} %convolution_bitcast_fusion.2) | data formatting | bytes 786432 | tf_op jit(solution)/shard_map/reshape | solution.py:87
  47.7 0.0 collective-permute-done.2
  47.7 0.0 copy-done.2
  47.7 0.0 slice-done
  47.7 1.0 %fusion.6 = f32[64,1536]{1,0:T(8,128)S(1)} fusion(f32[64,1536]{1,0:T(8,128)S(1)} %slice-done, f32[32,1536]{1,0:T(8,128)} %collective-permute-done.2, f32[128,1536]{1,0:T(8,128)S(1)} %copy-done.2), kind=kLoop, calls=%fused_computation.25 | loop fusion | flops 49152 | bytes 589824 | tf_op jit(solution)/shard_map/scatter-add | solution.py:90
  48.7 0.0 collective-permute-done.3
  48.7 1.0 %fusion.5 = f32[64,1536]{1,0:T(8,128)S(1)} fusion(f32[64,1536]{1,0:T(8,128)S(1)} %fusion.6, f32[32,1536]{1,0:T(8,128)} %collective-permute-done.3), kind=kLoop, calls=%fused_computation.23 | loop fusion | flops 49152 | bytes 589824 | tf_op jit(solution)/shard_map/scatter-add | solution.py:91
  49.7 0.0 copy-done.3
  49.7 0.2 multiply_bitcast_fusion.2
  49.9 0.1 maximum_reduce_fusion
  50.0 0.1 reduce_sum.37
  50.1 18.9 %all_to_all.12 = f32[32,1,4]{2,1,0:T(1,128)S(1)} all-to-all(f32[32,1,4]{2,1,0:T(1,128)S(1)} %broadcast_in_dim.20), channel_id=1, replica_groups=mesh['y'=4,'z'=16,'core'=2,'x'=4] {'z','core'}, dimensions={0} | all-to-all | bytes 1024 | tf_op jit(solution)/shard_map/all_to_all | solution.py:23
  69.0 0.1 reduce_sum.38
  69.1 13.0 %all_to_all.13 = f32[16,1,4]{2,1,0:T(1,128)S(1)} all-to-all(f32[16,1,4]{2,1,0:T(1,128)S(1)} %broadcast_in_dim.21), channel_id=1, replica_groups=mesh['y'=4,'z'=16,'core'=2,'x'=4] {'y','x'}, dimensions={0} | all-to-all | bytes 512 | tf_op jit(solution)/shard_map/all_to_all | solution.py:23
  82.1 0.1 broadcast_in_dim.22
  82.2 0.1 fusion.23
  82.2 1.2 %multiply_subtract_fusion = (f32[64,1536]{1,0:T(8,128)}, f32[64,1536]{1,0:T(8,128)}, f32[64,1536]{1,0:T(8,128)}, f32[64,1536]{1,0:T(8,128)}) fusion(f32[64,1536]{1,0:T(8,128)S(1)} %copy-done.3, f32[64,1536]{1,0:T(8,128)S(1)} %fusion.5, f32[1536]{0:T(1024)S(1)} %get-tuple-element.37, f32[1536]{0:T(1024)S(1)} %get-tuple-element.36, f32[64,1536]{1,0:T(8,128)S(1)} %tile.10, ...), kind=kLoop, calls=%fused_computation.11 | loop fusion | flops 983040 | bytes 3158016 | tf_op jit(solution)/shard_map/sub | solution.py:115
  (7 shorter events, 0.1 us)
Async XLA Ops:
  0.6 5.0 %copy-start = (bf16[8,192,192]{2,1,0:T(8,128)(2,1)S(1)}, bf16[8,192,192]{2,1,0:T(8,128)(2,1)}, u32[]{:S(2)}) copy-start(bf16[8,192,192]{2,1,0:T(8,128)(2,1)} %param.13) | copy-start | bytes 1769476
  17.7 22.2 %copy-start.1 = (f32[128,1536]{1,0:T(8,128)}, f32[128,1536]{1,0:T(8,128)S(1)}, u32[]{:S(2)}) copy-start(f32[128,1536]{1,0:T(8,128)S(1)} %convolution_bitcast_fusion) | copy-start | bytes 2359300
  18.6 21.5 %collective-permute-start = (bf16[32,1536]{1,0:T(8,128)(2,1)S(1)}, bf16[32,1536]{1,0:T(8,128)(2,1)S(1)}, u32[]{:S(2)}, u32[]{:S(2)}) collective-permute-start(bf16[32,1536]{1,0:T(8,128)(2,1)S(1)} %get-tuple-element.32), channel_id=1, source_target_pairs={{0,4},{4,8},{8,12},{12,16},{16,20},{20,24},{24,28},{28,32},{32,36}... | collective-permute-start | bytes 294920 | tf_op jit(solution)/shard_map/ppermute | solution.py:11
  23.5 16.5 %collective-permute-start.1 = (bf16[32,1536]{1,0:T(8,128)(2,1)S(1)}, bf16[32,1536]{1,0:T(8,128)(2,1)S(1)}, u32[]{:S(2)}, u32[]{:S(2)}) collective-permute-start(bf16[32,1536]{1,0:T(8,128)(2,1)S(1)} %get-tuple-element.33), channel_id=1, source_target_pairs={{0,508},{4,0},{8,4},{12,8},{16,12},{20,16},{24,20},{28,24},{32,28}... | collective-permute-start | bytes 294920 | tf_op jit(solution)/shard_map/ppermute | solution.py:11
  29.3 18.4 %collective-permute-start.2 = (f32[32,1536]{1,0:T(8,128)}, f32[32,1536]{1,0:T(8,128)}, u32[]{:S(2)}, u32[]{:S(2)}) collective-permute-start(f32[32,1536]{1,0:T(8,128)} %get-tuple-element.34), channel_id=1, source_target_pairs={{0,508},{4,0},{8,4},{12,8},{16,12},{20,16},{24,20},{28,24},{32,28}... | collective-permute-start | bytes 589832 | tf_op jit(solution)/shard_map/ppermute | solution.py:11
  37.2 11.4 %collective-permute-start.3 = (f32[32,1536]{1,0:T(8,128)}, f32[32,1536]{1,0:T(8,128)}, u32[]{:S(2)}, u32[]{:S(2)}) collective-permute-start(f32[32,1536]{1,0:T(8,128)} %get-tuple-element.35), channel_id=1, source_target_pairs={{0,4},{4,8},{8,12},{12,16},{16,20},{20,24},{24,28},{28,32},{32,36}... | collective-permute-start | bytes 589832 | tf_op jit(solution)/shard_map/ppermute | solution.py:11
  43.3 4.4 %copy-start.2 = (f32[128,1536]{1,0:T(8,128)S(1)}, f32[128,1536]{1,0:T(8,128)}, u32[]{:S(2)}) copy-start(f32[128,1536]{1,0:T(8,128)} %copy-done.1) | copy-start | bytes 2359300
  43.3 4.4 %slice-start = ((f32[128,1536]{1,0:T(8,128)}), f32[64,1536]{1,0:T(8,128)S(1)}, s32[]{:S(2)}) async-start(f32[128,1536]{1,0:T(8,128)} %copy-done.1), calls=%async_computation.2 | async-start | bytes 786432 | tf_op jit(solution)/shard_map/slice | solution.py:89
  43.3 6.3 %copy-start.3 = (f32[64,1536]{1,0:T(8,128)S(1)}, f32[64,1536]{1,0:T(8,128)}, u32[]{:S(2)}) copy-start(f32[64,1536]{1,0:T(8,128)} %param.11) | copy-start | bytes 1179652

commit v9 on v8

--- a/solution.py
+++ b/solution.py
@@ -59,11 +59,17 @@
     moved = jnp.einsum(
         "sdc,kfc->ksdf", weighted, translations, preferred_element_type=jnp.float32
     ).reshape(classes, spheres, columns)
+    high = lax.reduce_precision(moved, exponent_bits=8, mantissa_bits=7)
+    rest = moved - high
+    middle = lax.reduce_precision(rest, exponent_bits=8, mantissa_bits=7)
+    low = rest - middle
+    pieces = jnp.concatenate(
+        [high.astype(jnp.bfloat16), middle.astype(jnp.bfloat16), low.astype(jnp.bfloat16)], axis=0
+    )
     contrib = jnp.einsum(
         "kse,ksx->ex",
-        blocks,
-        moved,
-        precision=lax.Precision.HIGHEST,
+        jnp.concatenate([blocks_half] * 3, axis=0),
+        pieces,
         preferred_element_type=jnp.float32,
     )
     sends = lax.optimization_barrier((source[spheres - band :], source[:band], contrib[:band], contrib[band + spheres :]))

time: 84.1 us -> 90 us (1.070)
  waiting for transfers between devices: 0.01 us -> 4.94 us
  other arithmetic: 6.5 us -> 9.72 us
  matrix products: 11.1 us -> 10.2 us
    ppermute x4, waiting for transfers between devices: 0.01 us -> 4.94 us  [passed_along(): lax.ppermute(x, axes, [(i, (i + by) % devices) for i in range(devices)])]
    convert_element_type x0 -> x1, other arithmetic: none -> 4.69 us  [on_device(): high.astype(jnp.bfloat16)]
  transfers between devices with their start and end apart: 4 -> 4, of which waited for: 0 -> 1; matrix products, arithmetic and copies ran while one was open for 11% -> 10% of each run, Pallas kernels for 0% -> 0%
where the time goes in v9:
time: 90 us; the launch traced here: 89.4 us
  blocking collectives  31.4 us (35%)
  starting transfers between devices  20.5 us (23%)
  local copies, waits for them, and re-layouts  11.8 us (13%)
  matrix products  10.2 us (11%)
  other arithmetic  9.72 us (11%)
  waiting for transfers between devices  4.94 us (5%)
    all_to_all x2, blocking collectives, exchange_sum(): return jnp.sum(lax.all_to_all(spread, axes, 0, 0, tiled=True), axis=0)  31.4 us
    ppermute x4, starting transfers between devices, passed_along(): lax.ppermute(x, axes, [(i, (i + by) % devices) for i in range(devices)])  20.5 us
    reshape x1, local copies, waits for them, and re-layouts, on_device(): moved = jnp.einsum('sdc,kfc->ksdf', weighted, translations, preferred_ele...  5.18 us
    ppermute x4, waiting for transfers between devices, passed_along(): lax.ppermute(x, axes, [(i, (i + by) % devices) for i in range(devices)])  4.94 us
    convert_element_type x1, other arithmetic, on_device(): high.astype(jnp.bfloat16)  4.69 us
    dot_general x1, matrix products, on_device(): jnp.einsum('ksdc,kcf->sdf', gathered.reshape(classes, spheres, groups, or...  3.15 us
    dot_general x1, matrix products, on_device(): jnp.einsum('kse,ksx->ex', jnp.concatenate([blocks_half] * 3, axis=0), pie...  2.87 us
    dot_general x1, matrix products, on_device(): jnp.einsum('sdc,kfc->ksdf', weighted, translations, preferred_element_typ...  2.74 us
  transfers between devices with their start and end apart: 4, of which 1 were waited for; matrix products, arithmetic and copies ran while one was open for 10% of the time, Pallas kernels for 0%

profile of v9, /device:TPU:1, one launch (start us, length us, event | category | flops | bytes accessed | tf_op | source)
XLA Modules:
  0.0 89.4 jit_solution(1150730604337676350)
XLA Ops:
  0.6 0.0 copy-start
  0.6 0.9 %tile.4 = f32[64,8,192]{2,1,0:T(8,128)S(1)} broadcast(f32[64,192]{1,0:T(8,128)} %param.12), dimensions={0,2} | broadcast | bytes 442368 | tf_op jit(solution)/shard_map/tile | solution.py:57
  1.6 0.2 tile.10
  1.8 1.2 %fusion.45 = (bf16[64,1536]{1,0:T(8,128)(2,1)S(1)}, bf16[64,1536]{1,0:T(8,128)(2,1)S(1)}) fusion(f32[64,1536]{1,0:T(8,128)} %param.11, f32[64,1536]{1,0:T(8,128)S(1)} %tile.10), kind=kLoop, calls=%fused_computation.82 | loop fusion | flops 294912 | bytes 1179648 | tf_op jit(solution)/shard_map/convert_element_type | solution.py:38
  3.0 0.2 reshape.94
  3.2 0.0 copy-done
  3.2 2.7 %convolution_bitcast_fusion = f32[8,64,8,192]{3,2,0,1:T(8,128)} fusion(bf16[8,192,192]{2,1,0:T(8,128)(2,1)S(1)} %copy-done, bf16[64,8,192,1]{2,1,0,3:T(8,128)(2,1)S(1)} %reshape.94), kind=kOutput, calls=%fused_computation.14 | convolution fusion | flops 301989888 | bytes 3932160 | tf_op jit(solution)/shard_map/sdc,kfc->ksdf/dot_general | solution.py:59
  5.9 5.2 %reshape.90 = f32[8,64,1536]{2,0,1:T(8,128)} reshape(f32[8,64,8,192]{3,2,0,1:T(8,128)} %convolution_bitcast_fusion) | data formatting | bytes 6291456 | tf_op jit(solution)/shard_map/reshape | solution.py:61
  11.1 4.7 %reduce-precision_convert_fusion.1 = (bf16[8,64,1536]{2,0,1:T(8,128)(2,1)}, bf16[8,64,1536]{2,0,1:T(8,128)(2,1)}, bf16[8,64,1536]{2,0,1:T(8,128)(2,1)}) fusion(f32[8,64,1536]{2,0,1:T(8,128)} %reshape.90), kind=kLoop, calls=%fused_computation.9 | loop fusion | flops 5505024 | bytes 7864320 | tf_op jit(solution)/shard_map/convert_element_type | solution.py:67
  15.8 0.0 copy-done.5
  15.9 0.1 copy.29
  15.9 0.0 copy-done.6
  15.9 0.0 copy-done.7
  16.0 0.1 copy.31
  16.1 0.1 copy.30
  16.2 0.3 fusion.11
  16.5 2.9 %fusion.8 = f32[128,1536]{1,0:T(8,128)S(1)} fusion(bf16[8,64,1536]{2,0,1:T(8,128)(2,1)} %get-tuple-element.41, bf16[8,64,1536]{2,0,1:T(8,128)(2,1)} %get-tuple-element.42, bf16[8,64,1536]{2,0,1:T(8,128)(2,1)} %get-tuple-element.40, bf16[8,64,128]{2,0,1:T(8,128)(2,1)S(1)} %fusion.11), kind=kOutput, calls=%fused_computation.13 | convolution fusion | flops 619315200 | bytes 5636096 | tf_op jit(solution)/shard_map/kse,ksx->ex/dot_general | solution.py:69
  19.4 0.8 fusion.44
  20.2 8.8 %collective-permute-start.2 = (f32[32,1536]{1,0:T(8,128)}, f32[32,1536]{1,0:T(8,128)}, u32[]{:S(2)}, u32[]{:S(2)}) collective-permute-start(f32[32,1536]{1,0:T(8,128)} %get-tuple-element.34), channel_id=1, source_target_pairs={{0,508},{4,0},{8,4},{12,8},{16,12},{20,16},{24,20},{28,24},{32,28}... | collective-permute-start | bytes 589832 | tf_op jit(solution)/shard_map/ppermute | solution.py:11
  29.0 1.9 %collective-permute-start.3 = (f32[32,1536]{1,0:T(8,128)}, f32[32,1536]{1,0:T(8,128)}, u32[]{:S(2)}, u32[]{:S(2)}) collective-permute-start(f32[32,1536]{1,0:T(8,128)} %get-tuple-element.35), channel_id=1, source_target_pairs={{0,4},{4,8},{8,12},{12,16},{16,20},{20,24},{24,28},{28,32},{32,36}... | collective-permute-start | bytes 589832 | tf_op jit(solution)/shard_map/ppermute | solution.py:11
  30.9 7.9 %collective-permute-start.1 = (bf16[32,1536]{1,0:T(8,128)(2,1)S(1)}, bf16[32,1536]{1,0:T(8,128)(2,1)S(1)}, u32[]{:S(2)}, u32[]{:S(2)}) collective-permute-start(bf16[32,1536]{1,0:T(8,128)(2,1)S(1)} %get-tuple-element.33), channel_id=1, source_target_pairs={{0,508},{4,0},{8,4},{12,8},{16,12},{20,16},{24,20},{28,24},{32,28}... | collective-permute-start | bytes 294920 | tf_op jit(solution)/shard_map/ppermute | solution.py:11
  38.9 1.9 %collective-permute-start = (bf16[32,1536]{1,0:T(8,128)(2,1)S(1)}, bf16[32,1536]{1,0:T(8,128)(2,1)S(1)}, u32[]{:S(2)}, u32[]{:S(2)}) collective-permute-start(bf16[32,1536]{1,0:T(8,128)(2,1)S(1)} %get-tuple-element.32), channel_id=1, source_target_pairs={{0,4},{4,8},{8,12},{12,16},{16,20},{20,24},{24,28},{28,32},{32,36}... | collective-permute-start | bytes 294920 | tf_op jit(solution)/shard_map/ppermute | solution.py:11
  40.8 0.1 slice.89
  40.9 0.1 fusion.47
  41.0 0.5 fusion.25
  41.5 0.0 copy-done.1
  41.5 0.1 pad_maximum_fusion
  41.7 0.0 collective-permute-done.1
  41.7 4.9 %collective-permute-done = bf16[32,1536]{1,0:T(8,128)(2,1)S(1)} collective-permute-done((bf16[32,1536]{1,0:T(8,128)(2,1)S(1)}, bf16[32,1536]{1,0:T(8,128)(2,1)S(1)}, u32[]{:S(2)}, u32[]{:S(2)}) %collective-permute-start) | collective-permute-done | bytes 98336 | tf_op jit(solution)/shard_map/ppermute | solution.py:11
  46.6 0.5 fusion.7
  47.2 2.7 %reshape.91 = bf16[8,64,8,192]{3,2,1,0:T(8,128)(2,1)} reshape(bf16[8,64,1536]{2,1,0:T(8,128)(2,1)S(1)} %fusion.7) | data formatting | bytes 3145728 | tf_op jit(solution)/shard_map/reshape | solution.py:90
  49.8 3.1 %convolution_bitcast_fusion.1 = f32[64,8,192]{2,1,0:T(8,128)} fusion(bf16[8,64,8,192]{3,2,1,0:T(8,128)(2,1)} %reshape.91, bf16[8,192,192]{2,1,0:T(8,128)(2,1)S(1)} %copy-done), kind=kOutput, calls=%fused_computation.16 | convolution fusion | flops 301989888 | bytes 2555904 | tf_op jit(solution)/shard_map/ksdc,kcf->sdf/dot_general | solution.py:88
  53.0 1.2 %reshape.92 = f32[64,1536]{1,0:T(8,128)S(1)} reshape(f32[64,8,192]{2,1,0:T(8,128)} %convolution_bitcast_fusion.1) | data formatting | bytes 786432 | tf_op jit(solution)/shard_map/reshape | solution.py:93
  54.2 0.0 collective-permute-done.2
  54.2 0.0 copy-done.2
  54.2 0.0 slice-done
  54.2 1.0 %fusion.22 = f32[64,1536]{1,0:T(8,128)S(1)} fusion(f32[64,1536]{1,0:T(8,128)S(1)} %slice-done, f32[32,1536]{1,0:T(8,128)} %collective-permute-done.2, f32[128,1536]{1,0:T(8,128)S(1)} %copy-done.2), kind=kLoop, calls=%fused_computation.42 | loop fusion | flops 49152 | bytes 589824 | tf_op jit(solution)/shard_map/scatter-add | solution.py:96
  55.2 0.0 collective-permute-done.3
  55.2 1.0 %fusion.21 = f32[64,1536]{1,0:T(8,128)S(1)} fusion(f32[64,1536]{1,0:T(8,128)S(1)} %fusion.22, f32[32,1536]{1,0:T(8,128)} %collective-permute-done.3), kind=kLoop, calls=%fused_computation.40 | loop fusion | flops 49152 | bytes 589824 | tf_op jit(solution)/shard_map/scatter-add | solution.py:97
  56.2 0.2 multiply_bitcast_fusion.2
  56.3 0.1 maximum_reduce_fusion
  56.5 0.1 reduce_sum.37
  56.6 21.1 %all_to_all.12 = f32[32,1,4]{2,1,0:T(1,128)S(1)} all-to-all(f32[32,1,4]{2,1,0:T(1,128)S(1)} %broadcast_in_dim.20), channel_id=1, replica_groups=mesh['y'=4,'z'=16,'core'=2,'x'=4] {'z','core'}, dimensions={0} | all-to-all | bytes 1024 | tf_op jit(solution)/shard_map/all_to_all | solution.py:23
  77.7 0.1 reduce_sum.38
  77.7 10.3 %all_to_all.13 = f32[16,1,4]{2,1,0:T(1,128)S(1)} all-to-all(f32[16,1,4]{2,1,0:T(1,128)S(1)} %broadcast_in_dim.21), channel_id=1, replica_groups=mesh['y'=4,'z'=16,'core'=2,'x'=4] {'y','x'}, dimensions={0} | all-to-all | bytes 512 | tf_op jit(solution)/shard_map/all_to_all | solution.py:23
  88.1 0.1 broadcast_in_dim.22
  88.2 0.1 fusion.39
  88.2 1.2 %multiply_subtract_fusion = (f32[64,1536]{1,0:T(8,128)}, f32[64,1536]{1,0:T(8,128)}, f32[64,1536]{1,0:T(8,128)}, f32[64,1536]{1,0:T(8,128)}) fusion(f32[64,1536]{1,0:T(8,128)S(1)} %copy-done.3, f32[64,1536]{1,0:T(8,128)S(1)} %fusion.21, f32[1536]{0:T(1024)S(1)} %get-tuple-element.37, f32[1536]{0:T(1024)S(1)} %get-tuple-element.36, f32[64,1536]{1,0:T(8,128)S(1)} %tile.10, ...), kind=kLoop, calls=%fused_computation.28 | loop fusion | flops 983040 | bytes 3158016 | tf_op jit(solution)/shard_map/sub | solution.py:121
  (16 shorter events, 0.1 us)
Async XLA Ops:
  0.6 2.6 %copy-start = (bf16[8,192,192]{2,1,0:T(8,128)(2,1)S(1)}, bf16[8,192,192]{2,1,0:T(8,128)(2,1)}, u32[]{:S(2)}) copy-start(bf16[8,192,192]{2,1,0:T(8,128)(2,1)} %param.13) | copy-start | bytes 1769476
  11.1 4.7 %copy-start.5 = (s32[64,16]{0,1:T(8,128)S(1)}, s32[64,16]{0,1:T(8,128)}, u32[]{:S(2)}) copy-start(s32[64,16]{0,1:T(8,128)} %param.14) | copy-start | bytes 12292
  11.1 4.8 %copy-start.6 = (s32[64,16]{0,1:T(8,128)S(1)}, s32[64,16]{0,1:T(8,128)}, u32[]{:S(2)}) copy-start(s32[64,16]{0,1:T(8,128)} %param.17) | copy-start | bytes 12292
  11.1 4.8 %copy-start.7 = (bf16[64,16]{0,1:T(8,128)(2,1)S(1)}, bf16[64,16]{0,1:T(8,128)(2,1)}, u32[]{:S(2)}) copy-start(bf16[64,16]{0,1:T(8,128)(2,1)} %param.16) | copy-start | bytes 6148
  11.1 4.9 %copy-start.4 = (s32[64,16]{0,1:T(8,128)S(1)}, s32[64,16]{0,1:T(8,128)}, u32[]{:S(2)}) copy-start(s32[64,16]{0,1:T(8,128)} %param.15) | copy-start | bytes 12292
  19.4 22.2 %copy-start.1 = (f32[128,1536]{1,0:T(8,128)}, f32[128,1536]{1,0:T(8,128)S(1)}, u32[]{:S(2)}) copy-start(f32[128,1536]{1,0:T(8,128)S(1)} %fusion.8) | copy-start | bytes 2359300
  20.2 34.0 %collective-permute-start.2 = (f32[32,1536]{1,0:T(8,128)}, f32[32,1536]{1,0:T(8,128)}, u32[]{:S(2)}, u32[]{:S(2)}) collective-permute-start(f32[32,1536]{1,0:T(8,128)} %get-tuple-element.34), channel_id=1, source_target_pairs={{0,508},{4,0},{8,4},{12,8},{16,12},{20,16},{24,20},{28,24},{32,28}... | collective-permute-start | bytes 589832 | tf_op jit(solution)/shard_map/ppermute | solution.py:11
  29.0 26.2 %collective-permute-start.3 = (f32[32,1536]{1,0:T(8,128)}, f32[32,1536]{1,0:T(8,128)}, u32[]{:S(2)}, u32[]{:S(2)}) collective-permute-start(f32[32,1536]{1,0:T(8,128)} %get-tuple-element.35), channel_id=1, source_target_pairs={{0,4},{4,8},{8,12},{12,16},{16,20},{20,24},{24,28},{28,32},{32,36}... | collective-permute-start | bytes 589832 | tf_op jit(solution)/shard_map/ppermute | solution.py:11
  30.9 10.7 %collective-permute-start.1 = (bf16[32,1536]{1,0:T(8,128)(2,1)S(1)}, bf16[32,1536]{1,0:T(8,128)(2,1)S(1)}, u32[]{:S(2)}, u32[]{:S(2)}) collective-permute-start(bf16[32,1536]{1,0:T(8,128)(2,1)S(1)} %get-tuple-element.33), channel_id=1, source_target_pairs={{0,508},{4,0},{8,4},{12,8},{16,12},{20,16},{24,20},{28,24},{32,28}... | collective-permute-start | bytes 294920 | tf_op jit(solution)/shard_map/ppermute | solution.py:11
  38.9 7.8 %collective-permute-start = (bf16[32,1536]{1,0:T(8,128)(2,1)S(1)}, bf16[32,1536]{1,0:T(8,128)(2,1)S(1)}, u32[]{:S(2)}, u32[]{:S(2)}) collective-permute-start(bf16[32,1536]{1,0:T(8,128)(2,1)S(1)} %get-tuple-element.32), channel_id=1, source_target_pairs={{0,4},{4,8},{8,12},{12,16},{16,20},{20,24},{24,28},{28,32},{32,36}... | collective-permute-start | bytes 294920 | tf_op jit(solution)/shard_map/ppermute | solution.py:11
  49.8 4.4 %copy-start.2 = (f32[128,1536]{1,0:T(8,128)S(1)}, f32[128,1536]{1,0:T(8,128)}, u32[]{:S(2)}) copy-start(f32[128,1536]{1,0:T(8,128)} %copy-done.1) | copy-start | bytes 2359300
  49.8 4.4 %slice-start = ((f32[128,1536]{1,0:T(8,128)}), f32[64,1536]{1,0:T(8,128)S(1)}, s32[]{:S(2)}) async-start(f32[128,1536]{1,0:T(8,128)} %copy-done.1), calls=%async_computation.2 | async-start | bytes 786432 | tf_op jit(solution)/shard_map/slice | solution.py:95
  49.8 6.3 %copy-start.3 = (f32[64,1536]{1,0:T(8,128)S(1)}, f32[64,1536]{1,0:T(8,128)}, u32[]{:S(2)}) copy-start(f32[64,1536]{1,0:T(8,128)} %param.11) | copy-start | bytes 1179652

commit v10 on v7

--- a/solution.py
+++ b/solution.py
@@ -47,13 +47,11 @@
         band + within,
         jnp.where(offset == 1, band + spheres + within, within - (spheres - band)),
     )
-    placed = (column[:, :, None] == jnp.arange(extent, dtype=jnp.int32)[None, None, :]).astype(
-        jnp.bfloat16
+    strength = pair_weight.astype(jnp.float32) * pair_mask.astype(jnp.float32)
+    hit = (pair_class[:, :, None, None] == jnp.arange(classes, dtype=jnp.int32)[None, None, :, None]) & (
+        column[:, :, None, None] == jnp.arange(extent, dtype=jnp.int32)[None, None, None, :]
     )
-    strength = pair_weight.astype(jnp.float32) * pair_mask.astype(jnp.float32)
-    chosen = pair_class[:, :, None] == jnp.arange(classes, dtype=jnp.int32)[None, None, :]
-    coupling = jnp.where(chosen, strength[:, :, None], jnp.float32(0.0)).astype(jnp.bfloat16)
-    blocks = jnp.einsum("smk,sme->kse", coupling, placed, preferred_element_type=jnp.float32)
+    blocks = jnp.sum(jnp.where(hit, strength[:, :, None, None], jnp.float32(0.0)), axis=1).transpose(1, 0, 2)
     blocks_half = blocks.astype(jnp.bfloat16)
 
     gain = jnp.tile(scattering, (1, groups))

time: 82.6 us -> 89.1 us (1.079)
  waiting for transfers between devices: 0.01 us -> 5.8 us
  other arithmetic: 4.95 us -> 8.1 us
  blocking collectives: 33.5 us -> 31.4 us
    ppermute x4, waiting for transfers between devices: 0.01 us -> 5.8 us  [passed_along(): lax.ppermute(x, axes, [(i, (i + by) % devices) for i in range(devices)])]
    reduce_sum x0 -> x1, other arithmetic: none -> 2.74 us  [on_device(): jnp.sum(jnp.where(hit, strength[:, :, None, None], jnp.float32(0.0)), axi...]
    all_to_all x2, blocking collectives: 33.5 us -> 31.4 us  [exchange_sum(): return jnp.sum(lax.all_to_all(spread, axes, 0, 0, tiled=True), axis=0)]
  transfers between devices with their start and end apart: 4 -> 4, of which waited for: 0 -> 1; matrix products, arithmetic and copies ran while one was open for 27% -> 10% of each run, Pallas kernels for 0% -> 0%
where the time goes in v10:
time: 89.1 us; the launch traced here: 88.6 us
  blocking collectives  31.4 us (35%)
  starting transfers between devices  20.5 us (23%)
  local copies, waits for them, and re-layouts  11.8 us (13%)
  matrix products  10.1 us (11%)
  other arithmetic  8.1 us (9%)
  waiting for transfers between devices  5.8 us (7%)
    all_to_all x2, blocking collectives, exchange_sum(): return jnp.sum(lax.all_to_all(spread, axes, 0, 0, tiled=True), axis=0)  31.4 us
    ppermute x4, starting transfers between devices, passed_along(): lax.ppermute(x, axes, [(i, (i + by) % devices) for i in range(devices)])  20.5 us
    ppermute x4, waiting for transfers between devices, passed_along(): lax.ppermute(x, axes, [(i, (i + by) % devices) for i in range(devices)])  5.8 us
    reshape x1, local copies, waits for them, and re-layouts, on_device(): moved = jnp.einsum('sdc,kfc->ksdf', weighted, translations, preferred_ele...  5.27 us
    dot_general x1, matrix products, on_device(): jnp.einsum('kse,ksx->ex', blocks, moved, precision=lax.Precision.HIGHEST,...  3.74 us
    dot_general x1, matrix products, on_device(): jnp.einsum('ksdc,kcf->sdf', gathered.reshape(classes, spheres, groups, or...  3.14 us
    reduce_sum x1, other arithmetic, on_device(): jnp.sum(jnp.where(hit, strength[:, :, None, None], jnp.float32(0.0)), axi...  2.74 us
    reshape x1, local copies, waits for them, and re-layouts, on_device(): gathered.reshape(classes, spheres, groups, order)  2.71 us
  transfers between devices with their start and end apart: 4, of which 1 were waited for; matrix products, arithmetic and copies ran while one was open for 10% of the time, Pallas kernels for 0%

profile of v10, /device:TPU:1, one launch (start us, length us, event | category | flops | bytes accessed | tf_op | source)
XLA Modules:
  0.0 88.6 jit_solution(16982116762293596949)
XLA Ops:
  0.6 0.0 copy-start
  0.6 0.9 %tile.4 = f32[64,8,192]{2,1,0:T(8,128)S(1)} broadcast(f32[64,192]{1,0:T(8,128)} %param.12), dimensions={0,2} | broadcast | bytes 442368 | tf_op jit(solution)/shard_map/tile | solution.py:57
  1.6 0.2 tile.10
  1.8 1.2 %fusion.18 = (bf16[64,1536]{1,0:T(8,128)(2,1)S(1)}, bf16[64,1536]{1,0:T(8,128)(2,1)S(1)}) fusion(f32[64,1536]{1,0:T(8,128)} %param.11, f32[64,1536]{1,0:T(8,128)S(1)} %tile.10), kind=kLoop, calls=%fused_computation.53 | loop fusion | flops 294912 | bytes 1179648 | tf_op jit(solution)/shard_map/convert_element_type | solution.py:38
  3.0 0.2 reshape.107
  3.2 0.0 copy-done
  3.2 2.7 %convolution_bitcast_fusion.1 = f32[8,64,8,192]{3,2,0,1:T(8,128)} fusion(bf16[8,192,192]{2,1,0:T(8,128)(2,1)S(1)} %copy-done, bf16[64,8,192,1]{2,1,0,3:T(8,128)(2,1)S(1)} %reshape.107), kind=kOutput, calls=%fused_computation.3 | convolution fusion | flops 301989888 | bytes 3932160 | tf_op jit(solution)/shard_map/sdc,kfc->ksdf/dot_general | solution.py:59
  5.9 5.3 %reshape.104 = f32[8,64,1536]{2,0,1:T(8,128)} reshape(f32[8,64,8,192]{3,2,0,1:T(8,128)} %convolution_bitcast_fusion.1) | data formatting | bytes 6291456 | tf_op jit(solution)/shard_map/reshape | solution.py:61
  11.2 0.0 copy-done.5
  11.2 0.0 copy-done.7
  11.2 0.1 copy.25
  11.2 0.0 copy-done.6
  11.3 0.1 copy.24
  11.4 0.2 iota_compare_fusion
  11.6 0.0 copy-done.4
  11.6 0.1 copy.23
  11.7 0.2 iota_compare_fusion.1
  11.9 2.7 %select_reduce_fusion = f32[64,8,128]{2,1,0:T(8,128)S(1)} fusion(f32[64,16]{1,0:T(8,128)S(1)} %copy.25, pred[64,16,128]{2,1,0:T(8,128)(4,1)S(1)} %iota_compare_fusion, pred[64,16,8]{2,1,0:T(8,128)(4,1)S(1)} %iota_compare_fusion.1), kind=kLoop, calls=%fused_computation | loop fusion | flops 3080192 | bytes 405504 | tf_op jit(solution)/shard_map/reduce_sum | solution.py:54
  14.6 3.7 %convolution_bitcast_fusion = f32[128,1536]{1,0:T(8,128)S(1)} fusion(f32[8,64,1536]{2,0,1:T(8,128)} %reshape.104, f32[64,8,128]{2,1,0:T(8,128)S(1)} %select_reduce_fusion), kind=kOutput, calls=%fused_computation.2 | convolution fusion | flops 1207959552 | bytes 4194304 | tf_op jit(solution)/shard_map/kse,ksx->ex/dot_general | solution.py:62
  18.4 0.0 copy-start.1
  18.4 0.8 fusion.17
  19.2 8.8 %collective-permute-start.2 = (f32[32,1536]{1,0:T(8,128)}, f32[32,1536]{1,0:T(8,128)}, u32[]{:S(2)}, u32[]{:S(2)}) collective-permute-start(f32[32,1536]{1,0:T(8,128)} %get-tuple-element.40), channel_id=1, source_target_pairs={{0,508},{4,0},{8,4},{12,8},{16,12},{20,16},{24,20},{28,24},{32,28}... | collective-permute-start | bytes 589832 | tf_op jit(solution)/shard_map/ppermute | solution.py:11
  28.0 1.9 %collective-permute-start.3 = (f32[32,1536]{1,0:T(8,128)}, f32[32,1536]{1,0:T(8,128)}, u32[]{:S(2)}, u32[]{:S(2)}) collective-permute-start(f32[32,1536]{1,0:T(8,128)} %get-tuple-element.39), channel_id=1, source_target_pairs={{0,4},{4,8},{8,12},{12,16},{16,20},{20,24},{24,28},{28,32},{32,36}... | collective-permute-start | bytes 589832 | tf_op jit(solution)/shard_map/ppermute | solution.py:11
  29.9 7.9 %collective-permute-start.1 = (bf16[32,1536]{1,0:T(8,128)(2,1)S(1)}, bf16[32,1536]{1,0:T(8,128)(2,1)S(1)}, u32[]{:S(2)}, u32[]{:S(2)}) collective-permute-start(bf16[32,1536]{1,0:T(8,128)(2,1)S(1)} %get-tuple-element.49), channel_id=1, source_target_pairs={{0,508},{4,0},{8,4},{12,8},{16,12},{20,16},{24,20},{28,24},{32,28}... | collective-permute-start | bytes 294920 | tf_op jit(solution)/shard_map/ppermute | solution.py:11
  37.9 1.9 %collective-permute-start = (bf16[32,1536]{1,0:T(8,128)(2,1)S(1)}, bf16[32,1536]{1,0:T(8,128)(2,1)S(1)}, u32[]{:S(2)}, u32[]{:S(2)}) collective-permute-start(bf16[32,1536]{1,0:T(8,128)(2,1)S(1)} %get-tuple-element.48), channel_id=1, source_target_pairs={{0,4},{4,8},{8,12},{12,16},{16,20},{20,24},{24,28},{28,32},{32,36}... | collective-permute-start | bytes 294920 | tf_op jit(solution)/shard_map/ppermute | solution.py:11
  39.8 0.0 collective-permute-done.1
  39.8 5.8 %collective-permute-done = bf16[32,1536]{1,0:T(8,128)(2,1)S(1)} collective-permute-done((bf16[32,1536]{1,0:T(8,128)(2,1)S(1)}, bf16[32,1536]{1,0:T(8,128)(2,1)S(1)}, u32[]{:S(2)}, u32[]{:S(2)}) %collective-permute-start) | collective-permute-done | bytes 98336 | tf_op jit(solution)/shard_map/ppermute | solution.py:11
  45.6 0.6 convolution_convert_fusion
  46.2 0.0 copy-done.1
  46.2 2.7 %reshape.105 = bf16[8,64,8,192]{3,2,1,0:T(8,128)(2,1)} reshape(bf16[8,64,1536]{2,1,0:T(8,128)(2,1)S(1)} %convolution_convert_fusion) | data formatting | bytes 3145728 | tf_op jit(solution)/shard_map/reshape | solution.py:79
  48.9 3.1 %convolution_bitcast_fusion.2 = f32[64,8,192]{2,1,0:T(8,128)} fusion(bf16[8,64,8,192]{3,2,1,0:T(8,128)(2,1)} %reshape.105, bf16[8,192,192]{2,1,0:T(8,128)(2,1)S(1)} %copy-done), kind=kOutput, calls=%fused_computation.5 | convolution fusion | flops 301989888 | bytes 2555904 | tf_op jit(solution)/shard_map/ksdc,kcf->sdf/dot_general | solution.py:77
  52.1 1.2 %reshape.106 = f32[64,1536]{1,0:T(8,128)S(1)} reshape(f32[64,8,192]{2,1,0:T(8,128)} %convolution_bitcast_fusion.2) | data formatting | bytes 786432 | tf_op jit(solution)/shard_map/reshape | solution.py:82
  53.3 0.0 collective-permute-done.2
  53.3 0.0 copy-done.2
  53.3 0.0 slice-done
  53.3 1.0 %fusion.6 = f32[64,1536]{1,0:T(8,128)S(1)} fusion(f32[64,1536]{1,0:T(8,128)S(1)} %slice-done, f32[32,1536]{1,0:T(8,128)} %collective-permute-done.2, f32[128,1536]{1,0:T(8,128)S(1)} %copy-done.2), kind=kLoop, calls=%fused_computation.26 | loop fusion | flops 49152 | bytes 589824 | tf_op jit(solution)/shard_map/scatter-add | solution.py:85
  54.3 0.0 collective-permute-done.3
  54.3 1.0 %fusion.5 = f32[64,1536]{1,0:T(8,128)S(1)} fusion(f32[64,1536]{1,0:T(8,128)S(1)} %fusion.6, f32[32,1536]{1,0:T(8,128)} %collective-permute-done.3), kind=kLoop, calls=%fused_computation.24 | loop fusion | flops 49152 | bytes 589824 | tf_op jit(solution)/shard_map/scatter-add | solution.py:86
  55.3 0.0 copy-done.3
  55.3 0.2 multiply_bitcast_fusion.2
  55.5 0.1 maximum_reduce_fusion
  55.6 0.1 reduce_sum.47
  55.7 21.1 %all_to_all.12 = f32[32,1,4]{2,1,0:T(1,128)S(1)} all-to-all(f32[32,1,4]{2,1,0:T(1,128)S(1)} %broadcast_in_dim.20), channel_id=1, replica_groups=mesh['y'=4,'z'=16,'core'=2,'x'=4] {'z','core'}, dimensions={0} | all-to-all | bytes 1024 | tf_op jit(solution)/shard_map/all_to_all | solution.py:23
  76.8 0.1 reduce_sum.48
  76.9 10.3 %all_to_all.13 = f32[16,1,4]{2,1,0:T(1,128)S(1)} all-to-all(f32[16,1,4]{2,1,0:T(1,128)S(1)} %broadcast_in_dim.21), channel_id=1, replica_groups=mesh['y'=4,'z'=16,'core'=2,'x'=4] {'y','x'}, dimensions={0} | all-to-all | bytes 512 | tf_op jit(solution)/shard_map/all_to_all | solution.py:23
  87.2 0.1 broadcast_in_dim.22
  87.3 0.1 fusion.15
  87.4 1.2 %multiply_subtract_fusion = (f32[64,1536]{1,0:T(8,128)}, f32[64,1536]{1,0:T(8,128)}, f32[64,1536]{1,0:T(8,128)}, f32[64,1536]{1,0:T(8,128)}) fusion(f32[64,1536]{1,0:T(8,128)S(1)} %copy-done.3, f32[64,1536]{1,0:T(8,128)S(1)} %fusion.5, f32[1536]{0:T(1024)S(1)} %get-tuple-element.33, f32[1536]{0:T(1024)S(1)} %get-tuple-element.32, f32[64,1536]{1,0:T(8,128)S(1)} %tile.10, ...), kind=kLoop, calls=%fused_computation.13 | loop fusion | flops 983040 | bytes 3158016 | tf_op jit(solution)/shard_map/sub | solution.py:110
  (15 shorter events, 0.1 us)
Async XLA Ops:
  0.6 2.6 %copy-start = (bf16[8,192,192]{2,1,0:T(8,128)(2,1)S(1)}, bf16[8,192,192]{2,1,0:T(8,128)(2,1)}, u32[]{:S(2)}) copy-start(bf16[8,192,192]{2,1,0:T(8,128)(2,1)} %param.13) | copy-start | bytes 1769476
  5.9 5.3 %copy-start.5 = (s32[64,16]{0,1:T(8,128)S(1)}, s32[64,16]{0,1:T(8,128)}, u32[]{:S(2)}) copy-start(s32[64,16]{0,1:T(8,128)} %param.17) | copy-start | bytes 12292
  5.9 5.3 %copy-start.7 = (bf16[64,16]{0,1:T(8,128)(2,1)S(1)}, bf16[64,16]{0,1:T(8,128)(2,1)}, u32[]{:S(2)}) copy-start(bf16[64,16]{0,1:T(8,128)(2,1)} %param.16) | copy-start | bytes 6148
  5.9 5.4 %copy-start.6 = (s32[64,16]{0,1:T(8,128)S(1)}, s32[64,16]{0,1:T(8,128)}, u32[]{:S(2)}) copy-start(s32[64,16]{0,1:T(8,128)} %param.14) | copy-start | bytes 12292
  5.9 5.7 %copy-start.4 = (s32[64,16]{0,1:T(8,128)S(1)}, s32[64,16]{0,1:T(8,128)}, u32[]{:S(2)}) copy-start(s32[64,16]{0,1:T(8,128)} %param.15) | copy-start | bytes 12292
  18.4 27.8 %copy-start.1 = (f32[128,1536]{1,0:T(8,128)}, f32[128,1536]{1,0:T(8,128)S(1)}, u32[]{:S(2)}) copy-start(f32[128,1536]{1,0:T(8,128)S(1)} %convolution_bitcast_fusion) | copy-start | bytes 2359300
  19.2 34.1 %collective-permute-start.2 = (f32[32,1536]{1,0:T(8,128)}, f32[32,1536]{1,0:T(8,128)}, u32[]{:S(2)}, u32[]{:S(2)}) collective-permute-start(f32[32,1536]{1,0:T(8,128)} %get-tuple-element.40), channel_id=1, source_target_pairs={{0,508},{4,0},{8,4},{12,8},{16,12},{20,16},{24,20},{28,24},{32,28}... | collective-permute-start | bytes 589832 | tf_op jit(solution)/shard_map/ppermute | solution.py:11
  28.0 26.3 %collective-permute-start.3 = (f32[32,1536]{1,0:T(8,128)}, f32[32,1536]{1,0:T(8,128)}, u32[]{:S(2)}, u32[]{:S(2)}) collective-permute-start(f32[32,1536]{1,0:T(8,128)} %get-tuple-element.39), channel_id=1, source_target_pairs={{0,4},{4,8},{8,12},{12,16},{16,20},{20,24},{24,28},{28,32},{32,36}... | collective-permute-start | bytes 589832 | tf_op jit(solution)/shard_map/ppermute | solution.py:11
  29.9 9.9 %collective-permute-start.1 = (bf16[32,1536]{1,0:T(8,128)(2,1)S(1)}, bf16[32,1536]{1,0:T(8,128)(2,1)S(1)}, u32[]{:S(2)}, u32[]{:S(2)}) collective-permute-start(bf16[32,1536]{1,0:T(8,128)(2,1)S(1)} %get-tuple-element.49), channel_id=1, source_target_pairs={{0,508},{4,0},{8,4},{12,8},{16,12},{20,16},{24,20},{28,24},{32,28}... | collective-permute-start | bytes 294920 | tf_op jit(solution)/shard_map/ppermute | solution.py:11
  37.9 7.8 %collective-permute-start = (bf16[32,1536]{1,0:T(8,128)(2,1)S(1)}, bf16[32,1536]{1,0:T(8,128)(2,1)S(1)}, u32[]{:S(2)}, u32[]{:S(2)}) collective-permute-start(bf16[32,1536]{1,0:T(8,128)(2,1)S(1)} %get-tuple-element.48), channel_id=1, source_target_pairs={{0,4},{4,8},{8,12},{12,16},{16,20},{20,24},{24,28},{28,32},{32,36}... | collective-permute-start | bytes 294920 | tf_op jit(solution)/shard_map/ppermute | solution.py:11
  48.9 4.4 %copy-start.2 = (f32[128,1536]{1,0:T(8,128)S(1)}, f32[128,1536]{1,0:T(8,128)}, u32[]{:S(2)}) copy-start(f32[128,1536]{1,0:T(8,128)} %copy-done.1) | copy-start | bytes 2359300
  48.9 4.4 %slice-start = ((f32[128,1536]{1,0:T(8,128)}), f32[64,1536]{1,0:T(8,128)S(1)}, s32[]{:S(2)}) async-start(f32[128,1536]{1,0:T(8,128)} %copy-done.1), calls=%async_computation.2 | async-start | bytes 786432 | tf_op jit(solution)/shard_map/slice | solution.py:84
  48.9 6.3 %copy-start.3 = (f32[64,1536]{1,0:T(8,128)S(1)}, f32[64,1536]{1,0:T(8,128)}, u32[]{:S(2)}) copy-start(f32[64,1536]{1,0:T(8,128)} %param.11) | copy-start | bytes 1179652

commit v11 on v6

--- a/solution.py
+++ b/solution.py
@@ -68,10 +68,12 @@
         precision=lax.Precision.HIGHEST,
         preferred_element_type=jnp.float32,
     )
-    from_next = passed_along(contrib[:band], CELLS, -1)
-    from_prev = passed_along(contrib[band + spheres :], CELLS, 1)
+    sends = lax.optimization_barrier((contrib[:band], contrib[band + spheres :]))
+    from_next = passed_along(sends[0], CELLS, -1)
+    from_prev = passed_along(sends[1], CELLS, 1)
 
     padded = jnp.concatenate([from_prev_rows, source, from_next_rows], axis=0)
+    padded, blocks_half, unused = lax.optimization_barrier((padded, blocks_half, contrib))
     gathered = jnp.einsum(
         "kse,ex->ksx", blocks_half, padded, preferred_element_type=jnp.float32
     ).astype(jnp.bfloat16)

time: 93.8 us -> 81.8 us (0.87)
  waiting for transfers between devices: 6.93 us -> 0.01 us
  other arithmetic: 6.71 us -> 4.07 us
  local copies, waits for them, and re-layouts: 15.8 us -> 13.6 us
  blocking collectives: 30 us -> 31.9 us
  starting transfers between devices: 22 us -> 20.5 us
    ppermute x4, waiting for transfers between devices: 6.93 us -> 0.01 us  [passed_along(): lax.ppermute(x, axes, [(i, (i + by) % devices) for i in range(devices)])]
    all_to_all x2, blocking collectives: 30 us -> 31.9 us  [exchange_sum(): return jnp.sum(lax.all_to_all(spread, axes, 0, 0, tiled=True), axis=0)]
    unnamed x13 -> x19, local copies, waits for them, and re-layouts: 1.69 us -> 0.12 us
    ppermute x4, starting transfers between devices: 22 us -> 20.5 us  [passed_along(): lax.ppermute(x, axes, [(i, (i + by) % devices) for i in range(devices)])]
    add x1, other arithmetic: 0.04 us -> 1.07 us  [on_device(): contrib[band:band + band] + from_prev]
    another operation x2 -> x1, other arithmetic: 1.13 us -> 0.11 us  [on_device(): jnp.stack([incident * incident, incident * scattered, incident * back, sc...]
  transfers between devices with their start and end apart: 4 -> 4, of which waited for: 1 -> 0; matrix products, arithmetic and copies ran while one was open for 8% -> 28% of each run, Pallas kernels for 0% -> 0%
where the time goes in v11:
time: 81.8 us; the launch traced here: 81.3 us
  blocking collectives  31.9 us (39%)
  starting transfers between devices  20.5 us (25%)
  local copies, waits for them, and re-layouts  13.6 us (17%)
  matrix products  10.3 us (13%)
  other arithmetic  4.07 us (5%)
  between operations  0.92 us (1%)
    all_to_all x2, blocking collectives, exchange_sum(): return jnp.sum(lax.all_to_all(spread, axes, 0, 0, tiled=True), axis=0)  31.9 us
    ppermute x4, starting transfers between devices, passed_along(): lax.ppermute(x, axes, [(i, (i + by) % devices) for i in range(devices)])  20.5 us
    reshape x1, local copies, waits for them, and re-layouts, on_device(): moved = jnp.einsum('sdc,kfc->ksdf', weighted, translations, preferred_ele...  5.21 us
    dot_general x1, matrix products, on_device(): jnp.einsum('kse,ksx->ex', blocks, moved, precision=lax.Precision.HIGHEST,...  3.74 us
    reshape x1, local copies, waits for them, and re-layouts, on_device(): gathered.reshape(classes, spheres, groups, order)  3.34 us
    dot_general x1, matrix products, on_device(): jnp.einsum('sdc,kfc->ksdf', weighted, translations, preferred_element_typ...  2.68 us
    dot_general x1, matrix products, on_device(): jnp.einsum('kse,ex->ksx', blocks_half, padded, preferred_element_type=jnp...  1.72 us
  transfers between devices with their start and end apart: 4, of which 0 were waited for; matrix products, arithmetic and copies ran while one was open for 28% of the time, Pallas kernels for 0%

profile of v11, /device:TPU:1, one launch (start us, length us, event | category | flops | bytes accessed | tf_op | source)
XLA Modules:
  0.0 81.3 jit_solution(15524629004760161902)
XLA Ops:
  0.6 0.0 copy-start
  0.6 0.0 copy-start.6
  0.7 0.0 copy-start.8
  0.7 0.0 copy-start.5
  0.7 0.0 copy-start.7
  0.7 0.9 %tile.4 = f32[64,8,192]{2,1,0:T(8,128)S(1)} broadcast(f32[64,192]{1,0:T(8,128)} %param.8), dimensions={0,2} | broadcast | bytes 442368 | tf_op jit(solution)/shard_map/tile | solution.py:59
  1.6 0.2 tile.10
  1.8 1.2 %multiply_convert_fusion = (bf16[64,1536]{1,0:T(8,128)(2,1)S(1)}, bf16[64,1536]{1,0:T(8,128)(2,1)S(1)}) fusion(f32[64,1536]{1,0:T(8,128)S(1)} %tile.10, f32[64,1536]{1,0:T(8,128)} %param.7), kind=kLoop, calls=%fused_computation.18 | loop fusion | flops 294912 | bytes 1179648 | tf_op jit(solution)/shard_map/convert_element_type | solution.py:60
  3.0 8.8 %collective-permute-start.1 = (bf16[32,1536]{1,0:T(8,128)(2,1)S(1)}, bf16[32,1536]{1,0:T(8,128)(2,1)S(1)}, u32[]{:S(2)}, u32[]{:S(2)}) collective-permute-start(bf16[32,1536]{1,0:T(8,128)(2,1)S(1)} %get-tuple-element.30), channel_id=1, source_target_pairs={{0,508},{4,0},{8,4},{12,8},{16,12},{20,16},{24,20},{28,24},{32,28}... | collective-permute-start | bytes 294920 | tf_op jit(solution)/shard_map/ppermute | solution.py:11
  11.8 1.9 %collective-permute-start = (bf16[32,1536]{1,0:T(8,128)(2,1)S(1)}, bf16[32,1536]{1,0:T(8,128)(2,1)S(1)}, u32[]{:S(2)}, u32[]{:S(2)}) collective-permute-start(bf16[32,1536]{1,0:T(8,128)(2,1)S(1)} %get-tuple-element.29), channel_id=1, source_target_pairs={{0,4},{4,8},{8,12},{12,16},{16,20},{20,24},{24,28},{28,32},{32,36}... | collective-permute-start | bytes 294920 | tf_op jit(solution)/shard_map/ppermute | solution.py:11
  13.7 0.0 copy-done.6
  13.8 0.0 copy-done.8
  13.8 0.1 copy.27
  13.9 0.0 copy-done.5
  13.9 0.1 copy.26
  14.0 0.0 copy-done.7
  14.0 0.1 copy.25
  14.1 0.2 reshape.94
  14.3 0.0 copy-done
  14.3 2.7 %convolution_bitcast_fusion.1 = f32[8,64,8,192]{3,2,0,1:T(8,128)} fusion(bf16[8,192,192]{2,1,0:T(8,128)(2,1)S(1)} %copy-done, bf16[64,8,192,1]{2,1,0,3:T(8,128)(2,1)S(1)} %reshape.94), kind=kOutput, calls=%fused_computation.2 | convolution fusion | flops 301989888 | bytes 3932160 | tf_op jit(solution)/shard_map/sdc,kfc->ksdf/dot_general | solution.py:61
  17.0 5.2 %reshape.91 = f32[8,64,1536]{2,0,1:T(8,128)} reshape(f32[8,64,8,192]{3,2,0,1:T(8,128)} %convolution_bitcast_fusion.1) | data formatting | bytes 6291456 | tf_op jit(solution)/shard_map/reshape | solution.py:63
  22.2 0.5 fusion.21
  22.7 3.7 %convolution_bitcast_fusion = f32[128,1536]{1,0:T(8,128)S(1)} fusion(f32[8,64,128]{2,0,1:T(8,128)S(1)} %get-tuple-element.32, f32[8,64,1536]{2,0,1:T(8,128)} %reshape.91), kind=kOutput, calls=%fused_computation.1 | convolution fusion | flops 1207959552 | bytes 4194304 | tf_op jit(solution)/shard_map/kse,ksx->ex/dot_general | solution.py:64
  26.5 0.0 copy-start.2
  26.5 0.8 %fusion.19 = (f32[32,1536]{1,0:T(8,128)}, f32[32,1536]{1,0:T(8,128)}) fusion(f32[128,1536]{1,0:T(8,128)S(1)} %convolution_bitcast_fusion), kind=kLoop, calls=%fused_computation.56 | loop fusion | bytes 786432 | tf_op jit(solution)/shard_map/slice | solution.py:71
  27.3 1.9 %collective-permute-start.2 = (f32[32,1536]{1,0:T(8,128)}, f32[32,1536]{1,0:T(8,128)}, u32[]{:S(2)}, u32[]{:S(2)}) collective-permute-start(f32[32,1536]{1,0:T(8,128)} %get-tuple-element.10), channel_id=1, source_target_pairs={{0,4},{4,8},{8,12},{12,16},{16,20},{20,24},{24,28},{28,32},{32,36}... | collective-permute-start | bytes 589832 | tf_op jit(solution)/shard_map/ppermute | solution.py:11
  29.2 7.9 %collective-permute-start.3 = (f32[32,1536]{1,0:T(8,128)}, f32[32,1536]{1,0:T(8,128)}, u32[]{:S(2)}, u32[]{:S(2)}) collective-permute-start(f32[32,1536]{1,0:T(8,128)} %get-tuple-element.11), channel_id=1, source_target_pairs={{0,508},{4,0},{8,4},{12,8},{16,12},{20,16},{24,20},{28,24},{32,28}... | collective-permute-start | bytes 589832 | tf_op jit(solution)/shard_map/ppermute | solution.py:11
  37.2 0.0 collective-permute-done.1
  37.2 0.0 collective-permute-done
  37.2 0.0 copy-done.2
  37.2 1.7 %convolution_convert_fusion = bf16[8,64,1536]{2,1,0:T(8,128)(2,1)} fusion(bf16[128,1536]{1,0:T(8,128)(2,1)S(1)} %pad_maximum_fusion, bf16[8,64,128]{2,0,1:T(8,128)(2,1)S(1)} %get-tuple-element.8), kind=kOutput, calls=%fused_computation | convolution fusion | flops 202113024 | bytes 2097152 | tf_op jit(solution)/shard_map/kse,ex->ksx/dot_general | solution.py:77
  39.0 3.3 %reshape.92 = bf16[8,64,8,192]{3,2,1,0:T(8,128)(2,1)S(1)} reshape(bf16[8,64,1536]{2,1,0:T(8,128)(2,1)} %convolution_convert_fusion) | data formatting | bytes 3145728 | tf_op jit(solution)/shard_map/reshape | solution.py:82
  42.3 1.6 %broadcast_multiply_fusion = (f32[64,8,192]{2,1,0:T(8,128)}, f32[64,8,192]{2,1,0:T(8,128)}) fusion(f32[64,192]{1,0:T(8,128)S(1)} %copy-done.4, bf16[8,64,8,192]{3,2,1,0:T(8,128)(2,1)S(1)} %reshape.92, bf16[8,192,192]{2,1,0:T(8,128)(2,1)S(1)} %copy-done), kind=kOutput, calls=%fused_computation.24 | convolution fusion | flops 302088192 | bytes 2998272 | tf_op jit(solution)/shard_map/ksdc,kcf->sdf/dot_general | solution.py:80
  43.9 1.3 %mul.105 = f32[1,64,1536]{2,1,0:T(8,128)S(1)} reshape(f32[64,8,192]{2,1,0:T(8,128)} %get-tuple-element.33) | data formatting | bytes 786432 | tf_op jit(solution)/shard_map/mul | solution.py:91
  45.2 1.2 %reshape.93 = f32[64,1536]{1,0:T(8,128)S(1)} reshape(f32[64,8,192]{2,1,0:T(8,128)} %get-tuple-element.34) | data formatting | bytes 786432 | tf_op jit(solution)/shard_map/reshape | solution.py:85
  46.4 0.0 collective-permute-done.2
  46.5 0.0 collective-permute-done.3
  46.5 1.1 %slice_add_fusion.1 = (f32[32,1536]{1,0:T(8,128)S(1)}, f32[32,1536]{1,0:T(8,128)S(1)}) fusion(f32[32,1536]{1,0:T(8,128)} %collective-permute-done.2, f32[128,1536]{1,0:T(8,128)S(1)} %copy-done.3, f32[32,1536]{1,0:T(8,128)} %collective-permute-done.3), kind=kLoop, calls=%fused_computation.26 | loop fusion | flops 98304 | bytes 1179648 | tf_op jit(solution)/shard_map/add | solution.py:88
  47.5 0.0 copy-done.1
  47.6 0.1 multiply_bitcast_fusion.2
  47.7 0.1 maximum_reduce_fusion
  47.9 0.1 reduce_sum.37
  48.0 19.6 %all_to_all.12 = f32[32,1,4]{2,1,0:T(1,128)S(1)} all-to-all(f32[32,1,4]{2,1,0:T(1,128)S(1)} %broadcast_in_dim.20), channel_id=1, replica_groups=mesh['y'=4,'z'=16,'core'=2,'x'=4] {'z','core'}, dimensions={0} | all-to-all | bytes 1024 | tf_op jit(solution)/shard_map/all_to_all | solution.py:23
  67.6 0.1 reduce_sum.38
  67.6 12.3 %all_to_all.13 = f32[16,1,4]{2,1,0:T(1,128)S(1)} all-to-all(f32[16,1,4]{2,1,0:T(1,128)S(1)} %broadcast_in_dim.21), channel_id=1, replica_groups=mesh['y'=4,'z'=16,'core'=2,'x'=4] {'y','x'}, dimensions={0} | all-to-all | bytes 512 | tf_op jit(solution)/shard_map/all_to_all | solution.py:23
  80.0 0.1 broadcast_in_dim.22
  80.0 0.1 fusion.16
  80.1 1.2 %multiply_subtract_fusion = (f32[64,1536]{1,0:T(8,128)}, f32[64,1536]{1,0:T(8,128)}, f32[64,1536]{1,0:T(8,128)}, f32[64,1536]{1,0:T(8,128)}) fusion(f32[64,1536]{1,0:T(8,128)S(1)} %copy-done.1, f32[32,1536]{1,0:T(8,128)S(1)} %get-tuple-element.17, f32[32,1536]{1,0:T(8,128)S(1)} %get-tuple-element.16, f32[1536]{0:T(1024)S(1)} %get-tuple-element.13, ...), kind=kLoop, calls=%fused_computation.14 | loop fusion | flops 1081344 | bytes 3158016 | tf_op jit(solution)/shard_map/sub | solution.py:113
  (13 shorter events, 0.2 us)
Async XLA Ops:
  0.6 13.7 %copy-start = (bf16[8,192,192]{2,1,0:T(8,128)(2,1)S(1)}, bf16[8,192,192]{2,1,0:T(8,128)(2,1)}, u32[]{:S(2)}) copy-start(bf16[8,192,192]{2,1,0:T(8,128)(2,1)} %param.9) | copy-start | bytes 1769476
  0.6 13.1 %copy-start.6 = (s32[64,16]{0,1:T(8,128)S(1)}, s32[64,16]{0,1:T(8,128)}, u32[]{:S(2)}) copy-start(s32[64,16]{0,1:T(8,128)} %param.13) | copy-start | bytes 12292
  0.7 13.1 %copy-start.8 = (bf16[64,16]{0,1:T(8,128)(2,1)S(1)}, bf16[64,16]{0,1:T(8,128)(2,1)}, u32[]{:S(2)}) copy-start(bf16[64,16]{0,1:T(8,128)(2,1)} %param.12) | copy-start | bytes 6148
  0.7 13.2 %copy-start.5 = (s32[64,16]{0,1:T(8,128)S(1)}, s32[64,16]{0,1:T(8,128)}, u32[]{:S(2)}) copy-start(s32[64,16]{0,1:T(8,128)} %param.11) | copy-start | bytes 12292
  0.7 13.3 %copy-start.7 = (s32[64,16]{0,1:T(8,128)S(1)}, s32[64,16]{0,1:T(8,128)}, u32[]{:S(2)}) copy-start(s32[64,16]{0,1:T(8,128)} %param.10) | copy-start | bytes 12292
  3.0 34.2 %collective-permute-start.1 = (bf16[32,1536]{1,0:T(8,128)(2,1)S(1)}, bf16[32,1536]{1,0:T(8,128)(2,1)S(1)}, u32[]{:S(2)}, u32[]{:S(2)}) collective-permute-start(bf16[32,1536]{1,0:T(8,128)(2,1)S(1)} %get-tuple-element.30), channel_id=1, source_target_pairs={{0,508},{4,0},{8,4},{12,8},{16,12},{20,16},{24,20},{28,24},{32,28}... | collective-permute-start | bytes 294920 | tf_op jit(solution)/shard_map/ppermute | solution.py:11
  11.8 25.4 %collective-permute-start = (bf16[32,1536]{1,0:T(8,128)(2,1)S(1)}, bf16[32,1536]{1,0:T(8,128)(2,1)S(1)}, u32[]{:S(2)}, u32[]{:S(2)}) collective-permute-start(bf16[32,1536]{1,0:T(8,128)(2,1)S(1)} %get-tuple-element.29), channel_id=1, source_target_pairs={{0,4},{4,8},{8,12},{12,16},{16,20},{20,24},{24,28},{28,32},{32,36}... | collective-permute-start | bytes 294920 | tf_op jit(solution)/shard_map/ppermute | solution.py:11
  26.5 10.7 %copy-start.2 = (f32[128,1536]{1,0:T(8,128)}, f32[128,1536]{1,0:T(8,128)S(1)}, u32[]{:S(2)}) copy-start(f32[128,1536]{1,0:T(8,128)S(1)} %convolution_bitcast_fusion) | copy-start | bytes 2359300
  27.3 19.1 %collective-permute-start.2 = (f32[32,1536]{1,0:T(8,128)}, f32[32,1536]{1,0:T(8,128)}, u32[]{:S(2)}, u32[]{:S(2)}) collective-permute-start(f32[32,1536]{1,0:T(8,128)} %get-tuple-element.10), channel_id=1, source_target_pairs={{0,4},{4,8},{8,12},{12,16},{16,20},{20,24},{24,28},{28,32},{32,36}... | collective-permute-start | bytes 589832 | tf_op jit(solution)/shard_map/ppermute | solution.py:11
  29.2 17.2 %collective-permute-start.3 = (f32[32,1536]{1,0:T(8,128)}, f32[32,1536]{1,0:T(8,128)}, u32[]{:S(2)}, u32[]{:S(2)}) collective-permute-start(f32[32,1536]{1,0:T(8,128)} %get-tuple-element.11), channel_id=1, source_target_pairs={{0,508},{4,0},{8,4},{12,8},{16,12},{20,16},{24,20},{28,24},{32,28}... | collective-permute-start | bytes 589832 | tf_op jit(solution)/shard_map/ppermute | solution.py:11
  38.9 3.3 %copy-start.4 = (f32[64,192]{1,0:T(8,128)S(1)}, f32[64,192]{1,0:T(8,128)}, u32[]{:S(2)}) copy-start(f32[64,192]{1,0:T(8,128)} %param.8) | copy-start | bytes 147460
  43.9 2.5 %copy-start.3 = (f32[128,1536]{1,0:T(8,128)S(1)}, f32[128,1536]{1,0:T(8,128)}, u32[]{:S(2)}) copy-start(f32[128,1536]{1,0:T(8,128)} %copy-done.2) | copy-start | bytes 2359300
  43.9 3.6 %copy-start.1 = (f32[64,1536]{1,0:T(8,128)S(1)}, f32[64,1536]{1,0:T(8,128)}, u32[]{:S(2)}) copy-start(f32[64,1536]{1,0:T(8,128)} %param.7) | copy-start | bytes 1179652

commit v12 on v11

--- a/solution.py
+++ b/solution.py
@@ -65,7 +65,7 @@
         "kse,ksx->ex",
         blocks,
         moved,
-        precision=lax.Precision.HIGHEST,
+        precision=lax.Precision.HIGH,
         preferred_element_type=jnp.float32,
     )
     sends = lax.optimization_barrier((contrib[:band], contrib[band + spheres :]))

time: 81.8 us -> 81 us (level)
  matrix products: 10.3 us -> 9.47 us
  transfers between devices with their start and end apart: 4 -> 4, of which waited for: 0 -> 0; matrix products, arithmetic and copies ran while one was open for 28% -> 27% of each run, Pallas kernels for 0% -> 0%
where the time goes in v12:
time: 81 us; the launch traced here: 80.5 us
  blocking collectives  31.9 us (39%)
  starting transfers between devices  20.5 us (25%)
  local copies, waits for them, and re-layouts  13.6 us (17%)
  matrix products  9.47 us (12%)
  other arithmetic  4.07 us (5%)
  between operations  0.92 us (1%)
    all_to_all x2, blocking collectives, exchange_sum(): return jnp.sum(lax.all_to_all(spread, axes, 0, 0, tiled=True), axis=0)  31.9 us
    ppermute x4, starting transfers between devices, passed_along(): lax.ppermute(x, axes, [(i, (i + by) % devices) for i in range(devices)])  20.5 us
    reshape x1, local copies, waits for them, and re-layouts, on_device(): moved = jnp.einsum('sdc,kfc->ksdf', weighted, translations, preferred_ele...  5.21 us
    reshape x1, local copies, waits for them, and re-layouts, on_device(): gathered.reshape(classes, spheres, groups, order)  3.34 us
    dot_general x1, matrix products, on_device(): jnp.einsum('kse,ksx->ex', blocks, moved, precision=lax.Precision.HIGH, pr...  2.94 us
    dot_general x1, matrix products, on_device(): jnp.einsum('sdc,kfc->ksdf', weighted, translations, preferred_element_typ...  2.68 us
    dot_general x1, matrix products, on_device(): jnp.einsum('kse,ex->ksx', blocks_half, padded, preferred_element_type=jnp...  1.72 us
  transfers between devices with their start and end apart: 4, of which 0 were waited for; matrix products, arithmetic and copies ran while one was open for 27% of the time, Pallas kernels for 0%

profile of v12, /device:TPU:1, one launch (start us, length us, event | category | flops | bytes accessed | tf_op | source)
XLA Modules:
  0.0 80.5 jit_solution(8687023274835708475)
XLA Ops:
  0.6 0.0 copy-start
  0.6 0.0 copy-start.6
  0.7 0.0 copy-start.8
  0.7 0.0 copy-start.5
  0.7 0.0 copy-start.7
  0.7 0.9 %tile.4 = f32[64,8,192]{2,1,0:T(8,128)S(1)} broadcast(f32[64,192]{1,0:T(8,128)} %param.8), dimensions={0,2} | broadcast | bytes 442368 | tf_op jit(solution)/shard_map/tile | solution.py:59
  1.6 0.2 tile.10
  1.8 1.2 %multiply_convert_fusion = (bf16[64,1536]{1,0:T(8,128)(2,1)S(1)}, bf16[64,1536]{1,0:T(8,128)(2,1)S(1)}) fusion(f32[64,1536]{1,0:T(8,128)S(1)} %tile.10, f32[64,1536]{1,0:T(8,128)} %param.7), kind=kLoop, calls=%fused_computation.18 | loop fusion | flops 294912 | bytes 1179648 | tf_op jit(solution)/shard_map/convert_element_type | solution.py:60
  3.0 8.8 %collective-permute-start.1 = (bf16[32,1536]{1,0:T(8,128)(2,1)S(1)}, bf16[32,1536]{1,0:T(8,128)(2,1)S(1)}, u32[]{:S(2)}, u32[]{:S(2)}) collective-permute-start(bf16[32,1536]{1,0:T(8,128)(2,1)S(1)} %get-tuple-element.30), channel_id=1, source_target_pairs={{0,508},{4,0},{8,4},{12,8},{16,12},{20,16},{24,20},{28,24},{32,28}... | collective-permute-start | bytes 294920 | tf_op jit(solution)/shard_map/ppermute | solution.py:11
  11.8 1.9 %collective-permute-start = (bf16[32,1536]{1,0:T(8,128)(2,1)S(1)}, bf16[32,1536]{1,0:T(8,128)(2,1)S(1)}, u32[]{:S(2)}, u32[]{:S(2)}) collective-permute-start(bf16[32,1536]{1,0:T(8,128)(2,1)S(1)} %get-tuple-element.29), channel_id=1, source_target_pairs={{0,4},{4,8},{8,12},{12,16},{16,20},{20,24},{24,28},{28,32},{32,36}... | collective-permute-start | bytes 294920 | tf_op jit(solution)/shard_map/ppermute | solution.py:11
  13.7 0.0 copy-done.6
  13.8 0.0 copy-done.8
  13.8 0.1 copy.27
  13.9 0.0 copy-done.5
  13.9 0.1 copy.26
  14.0 0.0 copy-done.7
  14.0 0.1 copy.25
  14.1 0.2 reshape.94
  14.3 0.0 copy-done
  14.3 2.7 %convolution_bitcast_fusion.1 = f32[8,64,8,192]{3,2,0,1:T(8,128)} fusion(bf16[8,192,192]{2,1,0:T(8,128)(2,1)S(1)} %copy-done, bf16[64,8,192,1]{2,1,0,3:T(8,128)(2,1)S(1)} %reshape.94), kind=kOutput, calls=%fused_computation.2 | convolution fusion | flops 301989888 | bytes 3932160 | tf_op jit(solution)/shard_map/sdc,kfc->ksdf/dot_general | solution.py:61
  17.0 5.2 %reshape.91 = f32[8,64,1536]{2,0,1:T(8,128)} reshape(f32[8,64,8,192]{3,2,0,1:T(8,128)} %convolution_bitcast_fusion.1) | data formatting | bytes 6291456 | tf_op jit(solution)/shard_map/reshape | solution.py:63
  22.2 0.5 fusion.21
  22.7 2.9 %convolution_bitcast_fusion = f32[128,1536]{1,0:T(8,128)S(1)} fusion(f32[8,64,128]{2,0,1:T(8,128)S(1)} %get-tuple-element.32, f32[8,64,1536]{2,0,1:T(8,128)} %reshape.91), kind=kOutput, calls=%fused_computation.1 | convolution fusion | flops 603979776 | bytes 4194304 | tf_op jit(solution)/shard_map/kse,ksx->ex/dot_general | solution.py:64
  25.7 0.0 copy-start.2
  25.7 0.8 %fusion.19 = (f32[32,1536]{1,0:T(8,128)}, f32[32,1536]{1,0:T(8,128)}) fusion(f32[128,1536]{1,0:T(8,128)S(1)} %convolution_bitcast_fusion), kind=kLoop, calls=%fused_computation.56 | loop fusion | bytes 786432 | tf_op jit(solution)/shard_map/slice | solution.py:71
  26.5 1.9 %collective-permute-start.2 = (f32[32,1536]{1,0:T(8,128)}, f32[32,1536]{1,0:T(8,128)}, u32[]{:S(2)}, u32[]{:S(2)}) collective-permute-start(f32[32,1536]{1,0:T(8,128)} %get-tuple-element.10), channel_id=1, source_target_pairs={{0,4},{4,8},{8,12},{12,16},{16,20},{20,24},{24,28},{28,32},{32,36}... | collective-permute-start | bytes 589832 | tf_op jit(solution)/shard_map/ppermute | solution.py:11
  28.4 7.9 %collective-permute-start.3 = (f32[32,1536]{1,0:T(8,128)}, f32[32,1536]{1,0:T(8,128)}, u32[]{:S(2)}, u32[]{:S(2)}) collective-permute-start(f32[32,1536]{1,0:T(8,128)} %get-tuple-element.11), channel_id=1, source_target_pairs={{0,508},{4,0},{8,4},{12,8},{16,12},{20,16},{24,20},{28,24},{32,28}... | collective-permute-start | bytes 589832 | tf_op jit(solution)/shard_map/ppermute | solution.py:11
  36.4 0.0 collective-permute-done.1
  36.4 0.0 collective-permute-done
  36.4 0.0 copy-done.2
  36.4 1.7 %convolution_convert_fusion = bf16[8,64,1536]{2,1,0:T(8,128)(2,1)} fusion(bf16[128,1536]{1,0:T(8,128)(2,1)S(1)} %pad_maximum_fusion, bf16[8,64,128]{2,0,1:T(8,128)(2,1)S(1)} %get-tuple-element.8), kind=kOutput, calls=%fused_computation | convolution fusion | flops 202113024 | bytes 2097152 | tf_op jit(solution)/shard_map/kse,ex->ksx/dot_general | solution.py:77
  38.2 3.3 %reshape.92 = bf16[8,64,8,192]{3,2,1,0:T(8,128)(2,1)S(1)} reshape(bf16[8,64,1536]{2,1,0:T(8,128)(2,1)} %convolution_convert_fusion) | data formatting | bytes 3145728 | tf_op jit(solution)/shard_map/reshape | solution.py:82
  41.5 1.6 %broadcast_multiply_fusion = (f32[64,8,192]{2,1,0:T(8,128)}, f32[64,8,192]{2,1,0:T(8,128)}) fusion(f32[64,192]{1,0:T(8,128)S(1)} %copy-done.4, bf16[8,64,8,192]{3,2,1,0:T(8,128)(2,1)S(1)} %reshape.92, bf16[8,192,192]{2,1,0:T(8,128)(2,1)S(1)} %copy-done), kind=kOutput, calls=%fused_computation.24 | convolution fusion | flops 302088192 | bytes 2998272 | tf_op jit(solution)/shard_map/ksdc,kcf->sdf/dot_general | solution.py:80
  43.1 1.3 %mul.105 = f32[1,64,1536]{2,1,0:T(8,128)S(1)} reshape(f32[64,8,192]{2,1,0:T(8,128)} %get-tuple-element.33) | data formatting | bytes 786432 | tf_op jit(solution)/shard_map/mul | solution.py:91
  44.4 1.2 %reshape.93 = f32[64,1536]{1,0:T(8,128)S(1)} reshape(f32[64,8,192]{2,1,0:T(8,128)} %get-tuple-element.34) | data formatting | bytes 786432 | tf_op jit(solution)/shard_map/reshape | solution.py:85
  45.6 0.0 collective-permute-done.2
  45.7 0.0 collective-permute-done.3
  45.7 1.1 %slice_add_fusion.1 = (f32[32,1536]{1,0:T(8,128)S(1)}, f32[32,1536]{1,0:T(8,128)S(1)}) fusion(f32[32,1536]{1,0:T(8,128)} %collective-permute-done.2, f32[128,1536]{1,0:T(8,128)S(1)} %copy-done.3, f32[32,1536]{1,0:T(8,128)} %collective-permute-done.3), kind=kLoop, calls=%fused_computation.26 | loop fusion | flops 98304 | bytes 1179648 | tf_op jit(solution)/shard_map/add | solution.py:88
  46.7 0.0 copy-done.1
  46.8 0.1 multiply_bitcast_fusion.2
  46.9 0.1 maximum_reduce_fusion
  47.1 0.1 reduce_sum.37
  47.2 19.6 %all_to_all.12 = f32[32,1,4]{2,1,0:T(1,128)S(1)} all-to-all(f32[32,1,4]{2,1,0:T(1,128)S(1)} %broadcast_in_dim.20), channel_id=1, replica_groups=mesh['y'=4,'z'=16,'core'=2,'x'=4] {'z','core'}, dimensions={0} | all-to-all | bytes 1024 | tf_op jit(solution)/shard_map/all_to_all | solution.py:23
  66.8 0.1 reduce_sum.38
  66.8 12.3 %all_to_all.13 = f32[16,1,4]{2,1,0:T(1,128)S(1)} all-to-all(f32[16,1,4]{2,1,0:T(1,128)S(1)} %broadcast_in_dim.21), channel_id=1, replica_groups=mesh['y'=4,'z'=16,'core'=2,'x'=4] {'y','x'}, dimensions={0} | all-to-all | bytes 512 | tf_op jit(solution)/shard_map/all_to_all | solution.py:23
  79.2 0.1 broadcast_in_dim.22
  79.2 0.1 fusion.16
  79.3 1.2 %multiply_subtract_fusion = (f32[64,1536]{1,0:T(8,128)}, f32[64,1536]{1,0:T(8,128)}, f32[64,1536]{1,0:T(8,128)}, f32[64,1536]{1,0:T(8,128)}) fusion(f32[64,1536]{1,0:T(8,128)S(1)} %copy-done.1, f32[32,1536]{1,0:T(8,128)S(1)} %get-tuple-element.17, f32[32,1536]{1,0:T(8,128)S(1)} %get-tuple-element.16, f32[1536]{0:T(1024)S(1)} %get-tuple-element.13, ...), kind=kLoop, calls=%fused_computation.14 | loop fusion | flops 1081344 | bytes 3158016 | tf_op jit(solution)/shard_map/sub | solution.py:113
  (13 shorter events, 0.2 us)
Async XLA Ops:
  0.6 13.7 %copy-start = (bf16[8,192,192]{2,1,0:T(8,128)(2,1)S(1)}, bf16[8,192,192]{2,1,0:T(8,128)(2,1)}, u32[]{:S(2)}) copy-start(bf16[8,192,192]{2,1,0:T(8,128)(2,1)} %param.9) | copy-start | bytes 1769476
  0.6 13.1 %copy-start.6 = (s32[64,16]{0,1:T(8,128)S(1)}, s32[64,16]{0,1:T(8,128)}, u32[]{:S(2)}) copy-start(s32[64,16]{0,1:T(8,128)} %param.13) | copy-start | bytes 12292
  0.7 13.1 %copy-start.8 = (bf16[64,16]{0,1:T(8,128)(2,1)S(1)}, bf16[64,16]{0,1:T(8,128)(2,1)}, u32[]{:S(2)}) copy-start(bf16[64,16]{0,1:T(8,128)(2,1)} %param.12) | copy-start | bytes 6148
  0.7 13.2 %copy-start.5 = (s32[64,16]{0,1:T(8,128)S(1)}, s32[64,16]{0,1:T(8,128)}, u32[]{:S(2)}) copy-start(s32[64,16]{0,1:T(8,128)} %param.11) | copy-start | bytes 12292
  0.7 13.3 %copy-start.7 = (s32[64,16]{0,1:T(8,128)S(1)}, s32[64,16]{0,1:T(8,128)}, u32[]{:S(2)}) copy-start(s32[64,16]{0,1:T(8,128)} %param.10) | copy-start | bytes 12292
  3.0 33.4 %collective-permute-start.1 = (bf16[32,1536]{1,0:T(8,128)(2,1)S(1)}, bf16[32,1536]{1,0:T(8,128)(2,1)S(1)}, u32[]{:S(2)}, u32[]{:S(2)}) collective-permute-start(bf16[32,1536]{1,0:T(8,128)(2,1)S(1)} %get-tuple-element.30), channel_id=1, source_target_pairs={{0,508},{4,0},{8,4},{12,8},{16,12},{20,16},{24,20},{28,24},{32,28}... | collective-permute-start | bytes 294920 | tf_op jit(solution)/shard_map/ppermute | solution.py:11
  11.8 24.6 %collective-permute-start = (bf16[32,1536]{1,0:T(8,128)(2,1)S(1)}, bf16[32,1536]{1,0:T(8,128)(2,1)S(1)}, u32[]{:S(2)}, u32[]{:S(2)}) collective-permute-start(bf16[32,1536]{1,0:T(8,128)(2,1)S(1)} %get-tuple-element.29), channel_id=1, source_target_pairs={{0,4},{4,8},{8,12},{12,16},{16,20},{20,24},{24,28},{28,32},{32,36}... | collective-permute-start | bytes 294920 | tf_op jit(solution)/shard_map/ppermute | solution.py:11
  25.7 10.7 %copy-start.2 = (f32[128,1536]{1,0:T(8,128)}, f32[128,1536]{1,0:T(8,128)S(1)}, u32[]{:S(2)}) copy-start(f32[128,1536]{1,0:T(8,128)S(1)} %convolution_bitcast_fusion) | copy-start | bytes 2359300
  26.5 19.1 %collective-permute-start.2 = (f32[32,1536]{1,0:T(8,128)}, f32[32,1536]{1,0:T(8,128)}, u32[]{:S(2)}, u32[]{:S(2)}) collective-permute-start(f32[32,1536]{1,0:T(8,128)} %get-tuple-element.10), channel_id=1, source_target_pairs={{0,4},{4,8},{8,12},{12,16},{16,20},{20,24},{24,28},{28,32},{32,36}... | collective-permute-start | bytes 589832 | tf_op jit(solution)/shard_map/ppermute | solution.py:11
  28.4 17.2 %collective-permute-start.3 = (f32[32,1536]{1,0:T(8,128)}, f32[32,1536]{1,0:T(8,128)}, u32[]{:S(2)}, u32[]{:S(2)}) collective-permute-start(f32[32,1536]{1,0:T(8,128)} %get-tuple-element.11), channel_id=1, source_target_pairs={{0,508},{4,0},{8,4},{12,8},{16,12},{20,16},{24,20},{28,24},{32,28}... | collective-permute-start | bytes 589832 | tf_op jit(solution)/shard_map/ppermute | solution.py:11
  38.2 3.3 %copy-start.4 = (f32[64,192]{1,0:T(8,128)S(1)}, f32[64,192]{1,0:T(8,128)}, u32[]{:S(2)}) copy-start(f32[64,192]{1,0:T(8,128)} %param.8) | copy-start | bytes 147460
  43.1 2.5 %copy-start.3 = (f32[128,1536]{1,0:T(8,128)S(1)}, f32[128,1536]{1,0:T(8,128)}, u32[]{:S(2)}) copy-start(f32[128,1536]{1,0:T(8,128)} %copy-done.2) | copy-start | bytes 2359300
  43.1 3.6 %copy-start.1 = (f32[64,1536]{1,0:T(8,128)S(1)}, f32[64,1536]{1,0:T(8,128)}, u32[]{:S(2)}) copy-start(f32[64,1536]{1,0:T(8,128)} %param.7) | copy-start | bytes 1179652

commit v13 on v12

--- a/solution.py
+++ b/solution.py
@@ -84,9 +84,9 @@
         preferred_element_type=jnp.float32,
     ).reshape(spheres, columns)
 
-    back = jnp.concatenate(
-        [contrib[band : band + band] + from_prev, contrib[band + band : band + spheres] + from_next], axis=0
-    )
+    back = contrib[band : band + spheres]
+    back = back.at[spheres - band :].add(from_next)
+    back = back.at[:band].add(from_prev)
 
     scattered = gain * coupled
     image = incident - scattered

time: 81 us -> 80.2 us (level)
  local copies, waits for them, and re-layouts: 13.6 us -> 11.7 us
  other arithmetic: 4.07 us -> 4.95 us
    scatter-add x0 -> x2, other arithmetic: none -> 1.92 us  [the longest x1 0.97 us: on_device(): back = back.at[:band].add(from_prev)]
    dot_general x1, matrix products: 1.61 us -> 3.12 us  [on_device(): jnp.einsum('ksdc,kcf->sdf', gathered.reshape(classes, spheres, groups, or...]
    mul x1 -> x0, local copies, waits for them, and re-layouts: 1.3 us -> none  [on_device(): scattered = gain * coupled]
    dot_general x1, matrix products: 1.72 us -> 0.55 us  [on_device(): jnp.einsum('kse,ex->ksx', blocks_half, padded, preferred_element_type=jnp...]
    add x1 -> x0, other arithmetic: 1.07 us -> none  [on_device(): contrib[band:band + band] + from_prev]
where the time goes in v13:
time: 80.2 us; the launch traced here: 79.7 us
  blocking collectives  31.9 us (40%)
  starting transfers between devices  20.5 us (26%)
  local copies, waits for them, and re-layouts  11.7 us (15%)
  matrix products  9.78 us (12%)
  other arithmetic  4.95 us (6%)
  between operations  0.92 us (1%)
    all_to_all x2, blocking collectives, exchange_sum(): return jnp.sum(lax.all_to_all(spread, axes, 0, 0, tiled=True), axis=0)  31.9 us
    ppermute x4, starting transfers between devices, passed_along(): lax.ppermute(x, axes, [(i, (i + by) % devices) for i in range(devices)])  20.5 us
    reshape x1, local copies, waits for them, and re-layouts, on_device(): moved = jnp.einsum('sdc,kfc->ksdf', weighted, translations, preferred_ele...  5.19 us
    dot_general x1, matrix products, on_device(): jnp.einsum('ksdc,kcf->sdf', gathered.reshape(classes, spheres, groups, or...  3.12 us
    dot_general x1, matrix products, on_device(): jnp.einsum('kse,ksx->ex', blocks, moved, precision=lax.Precision.HIGH, pr...  2.9 us
    reshape x1, local copies, waits for them, and re-layouts, on_device(): gathered.reshape(classes, spheres, groups, order)  2.69 us
    dot_general x1, matrix products, on_device(): jnp.einsum('sdc,kfc->ksdf', weighted, translations, preferred_element_typ...  2.68 us
  transfers between devices with their start and end apart: 4, of which 0 were waited for; matrix products, arithmetic and copies ran while one was open for 27% of the time, Pallas kernels for 0%

profile of v13, /device:TPU:1, one launch (start us, length us, event | category | flops | bytes accessed | tf_op | source)
XLA Modules:
  0.0 79.7 jit_solution(2489483334518014233)
XLA Ops:
  0.6 0.0 copy-start
  0.6 0.0 copy-start.5
  0.7 0.0 copy-start.4
  0.7 0.0 copy-start.7
  0.7 0.0 copy-start.6
  0.7 0.9 %tile.4 = f32[64,8,192]{2,1,0:T(8,128)S(1)} broadcast(f32[64,192]{1,0:T(8,128)} %param.12), dimensions={0,2} | broadcast | bytes 442368 | tf_op jit(solution)/shard_map/tile | solution.py:59
  1.6 0.2 tile.10
  1.8 1.2 %fusion.22 = (bf16[64,1536]{1,0:T(8,128)(2,1)S(1)}, bf16[64,1536]{1,0:T(8,128)(2,1)S(1)}) fusion(f32[64,1536]{1,0:T(8,128)} %param.11, f32[64,1536]{1,0:T(8,128)S(1)} %tile.10), kind=kLoop, calls=%fused_computation.57 | loop fusion | flops 294912 | bytes 1179648 | tf_op jit(solution)/shard_map/convert_element_type | solution.py:38
  3.0 4.9 %collective-permute-start = (bf16[32,1536]{1,0:T(8,128)(2,1)S(1)}, bf16[32,1536]{1,0:T(8,128)(2,1)S(1)}, u32[]{:S(2)}, u32[]{:S(2)}) collective-permute-start(bf16[32,1536]{1,0:T(8,128)(2,1)S(1)} %get-tuple-element.52), channel_id=1, source_target_pairs={{0,4},{4,8},{8,12},{12,16},{16,20},{20,24},{24,28},{28,32},{32,36}... | collective-permute-start | bytes 294920 | tf_op jit(solution)/shard_map/ppermute | solution.py:11
  8.0 5.8 %collective-permute-start.1 = (bf16[32,1536]{1,0:T(8,128)(2,1)S(1)}, bf16[32,1536]{1,0:T(8,128)(2,1)S(1)}, u32[]{:S(2)}, u32[]{:S(2)}) collective-permute-start(bf16[32,1536]{1,0:T(8,128)(2,1)S(1)} %get-tuple-element.53), channel_id=1, source_target_pairs={{0,508},{4,0},{8,4},{12,8},{16,12},{20,16},{24,20},{28,24},{32,28}... | collective-permute-start | bytes 294920 | tf_op jit(solution)/shard_map/ppermute | solution.py:11
  13.7 0.0 copy-done.5
  13.8 0.1 copy.25
  13.9 0.0 copy-done.4
  13.9 0.1 copy.26
  14.0 0.0 copy-done.7
  14.0 0.0 copy-done.6
  14.0 0.1 copy.27
  14.1 0.2 reshape.93
  14.3 0.0 copy-done
  14.3 2.7 %convolution_bitcast_fusion.1 = f32[8,64,8,192]{3,2,0,1:T(8,128)} fusion(bf16[8,192,192]{2,1,0:T(8,128)(2,1)S(1)} %copy-done, bf16[64,8,192,1]{2,1,0,3:T(8,128)(2,1)S(1)} %reshape.93), kind=kOutput, calls=%fused_computation.2 | convolution fusion | flops 301989888 | bytes 3932160 | tf_op jit(solution)/shard_map/sdc,kfc->ksdf/dot_general | solution.py:61
  17.0 5.2 %reshape.90 = f32[8,64,1536]{2,0,1:T(8,128)} reshape(f32[8,64,8,192]{3,2,0,1:T(8,128)} %convolution_bitcast_fusion.1) | data formatting | bytes 6291456 | tf_op jit(solution)/shard_map/reshape | solution.py:63
  22.2 0.5 fusion.24
  22.7 2.9 %convolution_bitcast_fusion = f32[128,1536]{1,0:T(8,128)S(1)} fusion(f32[8,64,128]{2,0,1:T(8,128)S(1)} %get-tuple-element.55, f32[8,64,1536]{2,0,1:T(8,128)} %reshape.90), kind=kOutput, calls=%fused_computation.1 | convolution fusion | flops 603979776 | bytes 4194304 | tf_op jit(solution)/shard_map/kse,ksx->ex/dot_general | solution.py:64
  25.6 0.0 copy-start.1
  25.7 0.8 %fusion.21 = (f32[32,1536]{1,0:T(8,128)}, f32[32,1536]{1,0:T(8,128)}) fusion(f32[128,1536]{1,0:T(8,128)S(1)} %convolution_bitcast_fusion), kind=kLoop, calls=%fused_computation.56 | loop fusion | bytes 786432 | tf_op jit(solution)/shard_map/slice | solution.py:71
  26.5 7.9 %collective-permute-start.2 = (f32[32,1536]{1,0:T(8,128)}, f32[32,1536]{1,0:T(8,128)}, u32[]{:S(2)}, u32[]{:S(2)}) collective-permute-start(f32[32,1536]{1,0:T(8,128)} %get-tuple-element.34), channel_id=1, source_target_pairs={{0,508},{4,0},{8,4},{12,8},{16,12},{20,16},{24,20},{28,24},{32,28}... | collective-permute-start | bytes 589832 | tf_op jit(solution)/shard_map/ppermute | solution.py:11
  34.4 1.9 %collective-permute-start.3 = (f32[32,1536]{1,0:T(8,128)}, f32[32,1536]{1,0:T(8,128)}, u32[]{:S(2)}, u32[]{:S(2)}) collective-permute-start(f32[32,1536]{1,0:T(8,128)} %get-tuple-element.35), channel_id=1, source_target_pairs={{0,4},{4,8},{8,12},{12,16},{16,20},{20,24},{24,28},{28,32},{32,36}... | collective-permute-start | bytes 589832 | tf_op jit(solution)/shard_map/ppermute | solution.py:11
  36.3 0.0 collective-permute-done
  36.3 0.0 collective-permute-done.1
  36.4 0.6 convolution_convert_fusion
  36.9 0.0 copy-done.1
  36.9 2.7 %reshape.91 = bf16[8,64,8,192]{3,2,1,0:T(8,128)(2,1)} reshape(bf16[8,64,1536]{2,1,0:T(8,128)(2,1)S(1)} %convolution_convert_fusion) | data formatting | bytes 3145728 | tf_op jit(solution)/shard_map/reshape | solution.py:82
  39.6 3.1 %convolution_bitcast_fusion.2 = f32[64,8,192]{2,1,0:T(8,128)} fusion(bf16[8,64,8,192]{3,2,1,0:T(8,128)(2,1)} %reshape.91, bf16[8,192,192]{2,1,0:T(8,128)(2,1)S(1)} %copy-done), kind=kOutput, calls=%fused_computation.4 | convolution fusion | flops 301989888 | bytes 2555904 | tf_op jit(solution)/shard_map/ksdc,kcf->sdf/dot_general | solution.py:80
  42.8 1.2 %reshape.92 = f32[64,1536]{1,0:T(8,128)S(1)} reshape(f32[64,8,192]{2,1,0:T(8,128)} %convolution_bitcast_fusion.2) | data formatting | bytes 786432 | tf_op jit(solution)/shard_map/reshape | solution.py:85
  44.0 0.0 collective-permute-done.2
  44.0 1.0 %fusion.6 = f32[64,1536]{1,0:T(8,128)S(1)} fusion(f32[64,1536]{1,0:T(8,128)S(1)} %slice-done, f32[32,1536]{1,0:T(8,128)} %collective-permute-done.2, f32[128,1536]{1,0:T(8,128)S(1)} %copy-done.2), kind=kLoop, calls=%fused_computation.26 | loop fusion | flops 49152 | bytes 589824 | tf_op jit(solution)/shard_map/scatter-add | solution.py:88
  45.0 0.0 collective-permute-done.3
  45.0 1.0 %fusion.5 = f32[64,1536]{1,0:T(8,128)S(1)} fusion(f32[64,1536]{1,0:T(8,128)S(1)} %fusion.6, f32[32,1536]{1,0:T(8,128)} %collective-permute-done.3), kind=kLoop, calls=%fused_computation.24 | loop fusion | flops 49152 | bytes 589824 | tf_op jit(solution)/shard_map/scatter-add | solution.py:89
  45.9 0.0 copy-done.3
  46.0 0.2 multiply_bitcast_fusion.2
  46.1 0.1 maximum_reduce_fusion
  46.3 0.1 reduce_sum.37
  46.4 18.9 %all_to_all.12 = f32[32,1,4]{2,1,0:T(1,128)S(1)} all-to-all(f32[32,1,4]{2,1,0:T(1,128)S(1)} %broadcast_in_dim.20), channel_id=1, replica_groups=mesh['y'=4,'z'=16,'core'=2,'x'=4] {'z','core'}, dimensions={0} | all-to-all | bytes 1024 | tf_op jit(solution)/shard_map/all_to_all | solution.py:23
  65.3 0.1 reduce_sum.38
  65.4 13.0 %all_to_all.13 = f32[16,1,4]{2,1,0:T(1,128)S(1)} all-to-all(f32[16,1,4]{2,1,0:T(1,128)S(1)} %broadcast_in_dim.21), channel_id=1, replica_groups=mesh['y'=4,'z'=16,'core'=2,'x'=4] {'y','x'}, dimensions={0} | all-to-all | bytes 512 | tf_op jit(solution)/shard_map/all_to_all | solution.py:23
  78.4 0.1 broadcast_in_dim.22
  78.5 0.1 fusion.18
  78.5 1.2 %multiply_subtract_fusion = (f32[64,1536]{1,0:T(8,128)}, f32[64,1536]{1,0:T(8,128)}, f32[64,1536]{1,0:T(8,128)}, f32[64,1536]{1,0:T(8,128)}) fusion(f32[64,1536]{1,0:T(8,128)S(1)} %copy-done.3, f32[64,1536]{1,0:T(8,128)S(1)} %fusion.5, f32[1536]{0:T(1024)S(1)} %get-tuple-element.37, f32[1536]{0:T(1024)S(1)} %get-tuple-element.36, f32[64,1536]{1,0:T(8,128)S(1)} %tile.10, ...), kind=kLoop, calls=%fused_computation.12 | loop fusion | flops 983040 | bytes 3158016 | tf_op jit(solution)/shard_map/sub | solution.py:113
  (12 shorter events, 0.1 us)
Async XLA Ops:
  0.6 13.7 %copy-start = (bf16[8,192,192]{2,1,0:T(8,128)(2,1)S(1)}, bf16[8,192,192]{2,1,0:T(8,128)(2,1)}, u32[]{:S(2)}) copy-start(bf16[8,192,192]{2,1,0:T(8,128)(2,1)} %param.13) | copy-start | bytes 1769476
  0.6 13.1 %copy-start.5 = (s32[64,16]{0,1:T(8,128)S(1)}, s32[64,16]{0,1:T(8,128)}, u32[]{:S(2)}) copy-start(s32[64,16]{0,1:T(8,128)} %param.14) | copy-start | bytes 12292
  0.7 13.2 %copy-start.4 = (s32[64,16]{0,1:T(8,128)S(1)}, s32[64,16]{0,1:T(8,128)}, u32[]{:S(2)}) copy-start(s32[64,16]{0,1:T(8,128)} %param.15) | copy-start | bytes 12292
  0.7 13.3 %copy-start.7 = (bf16[64,16]{0,1:T(8,128)(2,1)S(1)}, bf16[64,16]{0,1:T(8,128)(2,1)}, u32[]{:S(2)}) copy-start(bf16[64,16]{0,1:T(8,128)(2,1)} %param.16) | copy-start | bytes 6148
  0.7 13.3 %copy-start.6 = (s32[64,16]{0,1:T(8,128)S(1)}, s32[64,16]{0,1:T(8,128)}, u32[]{:S(2)}) copy-start(s32[64,16]{0,1:T(8,128)} %param.17) | copy-start | bytes 12292
  3.0 33.3 %collective-permute-start = (bf16[32,1536]{1,0:T(8,128)(2,1)S(1)}, bf16[32,1536]{1,0:T(8,128)(2,1)S(1)}, u32[]{:S(2)}, u32[]{:S(2)}) collective-permute-start(bf16[32,1536]{1,0:T(8,128)(2,1)S(1)} %get-tuple-element.52), channel_id=1, source_target_pairs={{0,4},{4,8},{8,12},{12,16},{16,20},{20,24},{24,28},{28,32},{32,36}... | collective-permute-start | bytes 294920 | tf_op jit(solution)/shard_map/ppermute | solution.py:11
  8.0 28.4 %collective-permute-start.1 = (bf16[32,1536]{1,0:T(8,128)(2,1)S(1)}, bf16[32,1536]{1,0:T(8,128)(2,1)S(1)}, u32[]{:S(2)}, u32[]{:S(2)}) collective-permute-start(bf16[32,1536]{1,0:T(8,128)(2,1)S(1)} %get-tuple-element.53), channel_id=1, source_target_pairs={{0,508},{4,0},{8,4},{12,8},{16,12},{20,16},{24,20},{28,24},{32,28}... | collective-permute-start | bytes 294920 | tf_op jit(solution)/shard_map/ppermute | solution.py:11
  25.6 11.3 %copy-start.1 = (f32[128,1536]{1,0:T(8,128)}, f32[128,1536]{1,0:T(8,128)S(1)}, u32[]{:S(2)}) copy-start(f32[128,1536]{1,0:T(8,128)S(1)} %convolution_bitcast_fusion) | copy-start | bytes 2359300
  26.5 17.5 %collective-permute-start.2 = (f32[32,1536]{1,0:T(8,128)}, f32[32,1536]{1,0:T(8,128)}, u32[]{:S(2)}, u32[]{:S(2)}) collective-permute-start(f32[32,1536]{1,0:T(8,128)} %get-tuple-element.34), channel_id=1, source_target_pairs={{0,508},{4,0},{8,4},{12,8},{16,12},{20,16},{24,20},{28,24},{32,28}... | collective-permute-start | bytes 589832 | tf_op jit(solution)/shard_map/ppermute | solution.py:11
  34.4 10.6 %collective-permute-start.3 = (f32[32,1536]{1,0:T(8,128)}, f32[32,1536]{1,0:T(8,128)}, u32[]{:S(2)}, u32[]{:S(2)}) collective-permute-start(f32[32,1536]{1,0:T(8,128)} %get-tuple-element.35), channel_id=1, source_target_pairs={{0,4},{4,8},{8,12},{12,16},{16,20},{20,24},{24,28},{28,32},{32,36}... | collective-permute-start | bytes 589832 | tf_op jit(solution)/shard_map/ppermute | solution.py:11
  39.6 4.4 %copy-start.2 = (f32[128,1536]{1,0:T(8,128)S(1)}, f32[128,1536]{1,0:T(8,128)}, u32[]{:S(2)}) copy-start(f32[128,1536]{1,0:T(8,128)} %copy-done.1) | copy-start | bytes 2359300
  39.6 4.4 %slice-start = ((f32[128,1536]{1,0:T(8,128)}), f32[64,1536]{1,0:T(8,128)S(1)}, s32[]{:S(2)}) async-start(f32[128,1536]{1,0:T(8,128)} %copy-done.1), calls=%async_computation.2 | async-start | bytes 786432 | tf_op jit(solution)/shard_map/slice | solution.py:87
  39.6 6.3 %copy-start.3 = (f32[64,1536]{1,0:T(8,128)S(1)}, f32[64,1536]{1,0:T(8,128)}, u32[]{:S(2)}) copy-start(f32[64,1536]{1,0:T(8,128)} %param.11) | copy-start | bytes 1179652

commit v14 on v13

--- a/solution.py
+++ b/solution.py
@@ -36,8 +36,11 @@
     cell_count = lax.axis_size("y") * lax.axis_size("z") * lax.axis_size("core")
 
     source = incident.astype(jnp.bfloat16)
-    from_prev_rows = passed_along(source[spheres - band :], CELLS, 1)
-    from_next_rows = passed_along(source[:band], CELLS, -1)
+    last_rows, first_rows, scattering = lax.optimization_barrier(
+        (incident[spheres - band :].astype(jnp.bfloat16), incident[:band].astype(jnp.bfloat16), scattering)
+    )
+    from_prev_rows = passed_along(last_rows, CELLS, 1)
+    from_next_rows = passed_along(first_rows, CELLS, -1)
 
     owner = pair_sphere // spheres
     within = pair_sphere % spheres

time: 80.2 us -> 79.2 us (0.988)
  other arithmetic: 4.95 us -> 4 us
    convert_element_type x1, other arithmetic: 1.18 us -> 0.04 us  [on_device(): (gain * incident).astype(jnp.bfloat16).reshape(spheres, groups, order)]
    another operation x0 -> x1, other arithmetic: none -> 1.11 us
    scatter-add x1, other arithmetic: 0.97 us -> 0.04 us  [on_device(): back = back.at[:band].add(from_prev)]
  transfers between devices with their start and end apart: 4 -> 4, of which waited for: 0 -> 0; matrix products, arithmetic and copies ran while one was open for 27% -> 28% of each run, Pallas kernels for 0% -> 0%
where the time goes in v14:
time: 79.2 us; the launch traced here: 78.7 us
  blocking collectives  31.9 us (40%)
  starting transfers between devices  20.5 us (26%)
  local copies, waits for them, and re-layouts  11.6 us (15%)
  matrix products  9.77 us (12%)
  other arithmetic  4 us (5%)
  between operations  0.89 us (1%)
    all_to_all x2, blocking collectives, exchange_sum(): return jnp.sum(lax.all_to_all(spread, axes, 0, 0, tiled=True), axis=0)  31.9 us
    ppermute x4, starting transfers between devices, passed_along(): lax.ppermute(x, axes, [(i, (i + by) % devices) for i in range(devices)])  20.5 us
    reshape x1, local copies, waits for them, and re-layouts, on_device(): moved = jnp.einsum('sdc,kfc->ksdf', weighted, translations, preferred_ele...  5.26 us
    dot_general x1, matrix products, on_device(): jnp.einsum('ksdc,kcf->sdf', gathered.reshape(classes, spheres, groups, or...  3.11 us
    dot_general x1, matrix products, on_device(): jnp.einsum('kse,ksx->ex', blocks, moved, precision=lax.Precision.HIGH, pr...  2.9 us
    reshape x1, local copies, waits for them, and re-layouts, on_device(): gathered.reshape(classes, spheres, groups, order)  2.7 us
    dot_general x1, matrix products, on_device(): jnp.einsum('sdc,kfc->ksdf', weighted, translations, preferred_element_typ...  2.67 us
  transfers between devices with their start and end apart: 4, of which 0 were waited for; matrix products, arithmetic and copies ran while one was open for 28% of the time, Pallas kernels for 0%

profile of v14, /device:TPU:1, one launch (start us, length us, event | category | flops | bytes accessed | tf_op | source)
XLA Modules:
  0.0 78.7 jit_solution(2318733727337746693)
XLA Ops:
  0.6 0.0 copy-start
  0.6 0.0 copy-start.1
  0.7 1.1 %convert.4 = bf16[64,1536]{1,0:T(8,128)(2,1)S(1)} convert(f32[64,1536]{1,0:T(8,128)} %param.11) | non-fusion elementwise | flops 98304 | bytes 589824 | tf_op jit(solution)/shard_map/convert.1
  1.8 4.9 %collective-permute-start = (bf16[32,1536]{1,0:T(8,128)(2,1)S(1)}, bf16[32,1536]{1,0:T(8,128)(2,1)S(1)}, u32[]{:S(2)}, u32[]{:S(2)}) collective-permute-start(bf16[32,1536]{1,0:T(8,128)(2,1)S(1)} %get-tuple-element.36), channel_id=1, source_target_pairs={{0,4},{4,8},{8,12},{12,16},{16,20},{20,24},{24,28},{28,32},{32,36}... | collective-permute-start | bytes 294920 | tf_op jit(solution)/shard_map/ppermute | solution.py:11
  6.7 5.8 %collective-permute-start.1 = (bf16[32,1536]{1,0:T(8,128)(2,1)S(1)}, bf16[32,1536]{1,0:T(8,128)(2,1)S(1)}, u32[]{:S(2)}, u32[]{:S(2)}) collective-permute-start(bf16[32,1536]{1,0:T(8,128)(2,1)S(1)} %get-tuple-element.37), channel_id=1, source_target_pairs={{0,508},{4,0},{8,4},{12,8},{16,12},{20,16},{24,20},{28,24},{32,28}... | collective-permute-start | bytes 294920 | tf_op jit(solution)/shard_map/ppermute | solution.py:11
  12.5 0.9 %tile.4 = f32[64,8,192]{2,1,0:T(8,128)S(1)} broadcast(f32[64,192]{1,0:T(8,128)} %param.12), dimensions={0,2} | broadcast | bytes 442368 | tf_op jit(solution)/shard_map/tile | solution.py:62
  13.4 0.2 tile.10
  13.6 0.0 copy-done.1
  13.6 0.2 reshape.93
  13.9 0.0 copy-done
  13.9 2.7 %convolution_bitcast_fusion.1 = f32[8,64,8,192]{3,2,0,1:T(8,128)} fusion(bf16[8,192,192]{2,1,0:T(8,128)(2,1)S(1)} %copy-done, bf16[64,8,192,1]{2,1,0,3:T(8,128)(2,1)S(1)} %reshape.93), kind=kOutput, calls=%fused_computation.2 | convolution fusion | flops 301989888 | bytes 3932160 | tf_op jit(solution)/shard_map/sdc,kfc->ksdf/dot_general | solution.py:64
  16.6 0.0 copy-start.5
  16.6 0.0 copy-start.4
  16.6 5.3 %reshape.90 = f32[8,64,1536]{2,0,1:T(8,128)} reshape(f32[8,64,8,192]{3,2,0,1:T(8,128)} %convolution_bitcast_fusion.1) | data formatting | bytes 6291456 | tf_op jit(solution)/shard_map/reshape | solution.py:66
  21.8 0.0 copy-done.5
  21.9 0.1 copy.25
  21.9 0.0 copy-done.4
  21.9 0.1 copy.26
  22.0 0.0 copy-done.6
  22.0 0.0 copy-done.7
  22.1 0.1 copy.27
  22.1 0.5 fusion.23
  22.7 2.9 %convolution_bitcast_fusion = f32[128,1536]{1,0:T(8,128)S(1)} fusion(f32[8,64,128]{2,0,1:T(8,128)S(1)} %get-tuple-element.59, f32[8,64,1536]{2,0,1:T(8,128)} %reshape.90), kind=kOutput, calls=%fused_computation.1 | convolution fusion | flops 603979776 | bytes 4194304 | tf_op jit(solution)/shard_map/kse,ksx->ex/dot_general | solution.py:67
  25.6 0.0 copy-start.2
  25.6 0.8 fusion.21
  26.4 7.9 %collective-permute-start.2 = (f32[32,1536]{1,0:T(8,128)}, f32[32,1536]{1,0:T(8,128)}, u32[]{:S(2)}, u32[]{:S(2)}) collective-permute-start(f32[32,1536]{1,0:T(8,128)} %get-tuple-element.40), channel_id=1, source_target_pairs={{0,508},{4,0},{8,4},{12,8},{16,12},{20,16},{24,20},{28,24},{32,28}... | collective-permute-start | bytes 589832 | tf_op jit(solution)/shard_map/ppermute | solution.py:11
  34.3 1.9 %collective-permute-start.3 = (f32[32,1536]{1,0:T(8,128)S(1)}, f32[32,1536]{1,0:T(8,128)S(1)}, u32[]{:S(2)}, u32[]{:S(2)}) collective-permute-start(f32[32,1536]{1,0:T(8,128)S(1)} %get-tuple-element.41), channel_id=1, source_target_pairs={{0,4},{4,8},{8,12},{12,16},{16,20},{20,24},{24,28},{28,32},{32,36}... | collective-permute-start | bytes 589832 | tf_op jit(solution)/shard_map/ppermute | solution.py:11
  36.2 0.0 collective-permute-done
  36.2 0.0 collective-permute-done.1
  36.3 0.0 copy-done.2
  36.3 0.5 convolution_convert_fusion
  36.9 2.7 %reshape.91 = bf16[8,64,8,192]{3,2,1,0:T(8,128)(2,1)} reshape(bf16[8,64,1536]{2,1,0:T(8,128)(2,1)S(1)} %convolution_convert_fusion) | data formatting | bytes 3145728 | tf_op jit(solution)/shard_map/reshape | solution.py:85
  39.6 3.1 %convolution_bitcast_fusion.2 = f32[64,8,192]{2,1,0:T(8,128)} fusion(bf16[8,64,8,192]{3,2,1,0:T(8,128)(2,1)} %reshape.91, bf16[8,192,192]{2,1,0:T(8,128)(2,1)S(1)} %copy-done), kind=kOutput, calls=%fused_computation.4 | convolution fusion | flops 301989888 | bytes 2555904 | tf_op jit(solution)/shard_map/ksdc,kcf->sdf/dot_general | solution.py:83
  42.7 1.2 %reshape.92 = f32[64,1536]{1,0:T(8,128)S(1)} reshape(f32[64,8,192]{2,1,0:T(8,128)} %convolution_bitcast_fusion.2) | data formatting | bytes 786432 | tf_op jit(solution)/shard_map/reshape | solution.py:88
  43.9 0.0 collective-permute-done.2
  43.9 0.0 copy-done.3
  43.9 0.0 slice-done
  43.9 1.0 %fusion.6 = f32[64,1536]{1,0:T(8,128)S(1)} fusion(f32[64,1536]{1,0:T(8,128)S(1)} %slice-done, f32[32,1536]{1,0:T(8,128)} %collective-permute-done.2, f32[128,1536]{1,0:T(8,128)S(1)} %copy-done.3), kind=kLoop, calls=%fused_computation.26 | loop fusion | flops 49152 | bytes 589824 | tf_op jit(solution)/shard_map/scatter-add | solution.py:91
  44.9 0.0 collective-permute-done.3
  44.9 0.2 multiply_bitcast_fusion.2
  45.1 0.1 maximum_reduce_fusion
  45.2 0.1 reduce_sum.37
  45.4 18.9 %all_to_all.12 = f32[32,1,4]{2,1,0:T(1,128)S(1)} all-to-all(f32[32,1,4]{2,1,0:T(1,128)S(1)} %broadcast_in_dim.20), channel_id=1, replica_groups=mesh['y'=4,'z'=16,'core'=2,'x'=4] {'z','core'}, dimensions={0} | all-to-all | bytes 1024 | tf_op jit(solution)/shard_map/all_to_all | solution.py:23
  64.3 0.1 reduce_sum.38
  64.4 13.0 %all_to_all.13 = f32[16,1,4]{2,1,0:T(1,128)S(1)} all-to-all(f32[16,1,4]{2,1,0:T(1,128)S(1)} %broadcast_in_dim.21), channel_id=1, replica_groups=mesh['y'=4,'z'=16,'core'=2,'x'=4] {'y','x'}, dimensions={0} | all-to-all | bytes 512 | tf_op jit(solution)/shard_map/all_to_all | solution.py:23
  77.3 0.1 broadcast_in_dim.22
  77.4 0.1 fusion.18
  77.5 1.2 %multiply_subtract_fusion = (f32[64,1536]{1,0:T(8,128)}, f32[64,1536]{1,0:T(8,128)}, f32[64,1536]{1,0:T(8,128)}, f32[64,1536]{1,0:T(8,128)}) fusion(f32[64,1536]{1,0:T(8,128)S(1)} %copy-done.1, f32[64,1536]{1,0:T(8,128)S(1)} %fusion.5, f32[1536]{0:T(1024)S(1)} %get-tuple-element.43, f32[1536]{0:T(1024)S(1)} %get-tuple-element.42, f32[64,1536]{1,0:T(8,128)S(1)} %tile.10, ...), kind=kLoop, calls=%fused_computation.12 | loop fusion | flops 983040 | bytes 3158016 | tf_op jit(solution)/shard_map/sub | solution.py:116
  (13 shorter events, 0.2 us)
Async XLA Ops:
  0.6 13.2 %copy-start = (bf16[8,192,192]{2,1,0:T(8,128)(2,1)S(1)}, bf16[8,192,192]{2,1,0:T(8,128)(2,1)}, u32[]{:S(2)}) copy-start(bf16[8,192,192]{2,1,0:T(8,128)(2,1)} %param.13) | copy-start | bytes 1769476
  0.6 12.9 %copy-start.1 = (f32[64,1536]{1,0:T(8,128)S(1)}, f32[64,1536]{1,0:T(8,128)}, u32[]{:S(2)}) copy-start(f32[64,1536]{1,0:T(8,128)} %param.11) | copy-start | bytes 1179652
  1.8 34.4 %collective-permute-start = (bf16[32,1536]{1,0:T(8,128)(2,1)S(1)}, bf16[32,1536]{1,0:T(8,128)(2,1)S(1)}, u32[]{:S(2)}, u32[]{:S(2)}) collective-permute-start(bf16[32,1536]{1,0:T(8,128)(2,1)S(1)} %get-tuple-element.36), channel_id=1, source_target_pairs={{0,4},{4,8},{8,12},{12,16},{16,20},{20,24},{24,28},{28,32},{32,36}... | collective-permute-start | bytes 294920 | tf_op jit(solution)/shard_map/ppermute | solution.py:11
  6.7 29.5 %collective-permute-start.1 = (bf16[32,1536]{1,0:T(8,128)(2,1)S(1)}, bf16[32,1536]{1,0:T(8,128)(2,1)S(1)}, u32[]{:S(2)}, u32[]{:S(2)}) collective-permute-start(bf16[32,1536]{1,0:T(8,128)(2,1)S(1)} %get-tuple-element.37), channel_id=1, source_target_pairs={{0,508},{4,0},{8,4},{12,8},{16,12},{20,16},{24,20},{28,24},{32,28}... | collective-permute-start | bytes 294920 | tf_op jit(solution)/shard_map/ppermute | solution.py:11
  16.6 5.3 %copy-start.5 = (s32[64,16]{0,1:T(8,128)S(1)}, s32[64,16]{0,1:T(8,128)}, u32[]{:S(2)}) copy-start(s32[64,16]{0,1:T(8,128)} %param.14) | copy-start | bytes 12292
  16.6 5.4 %copy-start.4 = (s32[64,16]{0,1:T(8,128)S(1)}, s32[64,16]{0,1:T(8,128)}, u32[]{:S(2)}) copy-start(s32[64,16]{0,1:T(8,128)} %param.15) | copy-start | bytes 12292
  16.6 5.5 %copy-start.6 = (s32[64,16]{0,1:T(8,128)S(1)}, s32[64,16]{0,1:T(8,128)}, u32[]{:S(2)}) copy-start(s32[64,16]{0,1:T(8,128)} %param.17) | copy-start | bytes 12292
  16.6 5.5 %copy-start.7 = (bf16[64,16]{0,1:T(8,128)(2,1)S(1)}, bf16[64,16]{0,1:T(8,128)(2,1)}, u32[]{:S(2)}) copy-start(bf16[64,16]{0,1:T(8,128)(2,1)} %param.16) | copy-start | bytes 6148
  25.6 10.7 %copy-start.2 = (f32[128,1536]{1,0:T(8,128)}, f32[128,1536]{1,0:T(8,128)S(1)}, u32[]{:S(2)}) copy-start(f32[128,1536]{1,0:T(8,128)S(1)} %convolution_bitcast_fusion) | copy-start | bytes 2359300
  26.4 17.5 %collective-permute-start.2 = (f32[32,1536]{1,0:T(8,128)}, f32[32,1536]{1,0:T(8,128)}, u32[]{:S(2)}, u32[]{:S(2)}) collective-permute-start(f32[32,1536]{1,0:T(8,128)} %get-tuple-element.40), channel_id=1, source_target_pairs={{0,508},{4,0},{8,4},{12,8},{16,12},{20,16},{24,20},{28,24},{32,28}... | collective-permute-start | bytes 589832 | tf_op jit(solution)/shard_map/ppermute | solution.py:11
  34.3 10.6 %collective-permute-start.3 = (f32[32,1536]{1,0:T(8,128)S(1)}, f32[32,1536]{1,0:T(8,128)S(1)}, u32[]{:S(2)}, u32[]{:S(2)}) collective-permute-start(f32[32,1536]{1,0:T(8,128)S(1)} %get-tuple-element.41), channel_id=1, source_target_pairs={{0,4},{4,8},{8,12},{12,16},{16,20},{20,24},{24,28},{28,32},{32,36}... | collective-permute-start | bytes 589832 | tf_op jit(solution)/shard_map/ppermute | solution.py:11
  39.6 4.3 %copy-start.3 = (f32[128,1536]{1,0:T(8,128)S(1)}, f32[128,1536]{1,0:T(8,128)}, u32[]{:S(2)}) copy-start(f32[128,1536]{1,0:T(8,128)} %copy-done.2) | copy-start | bytes 2359300
  39.6 4.3 %slice-start = ((f32[128,1536]{1,0:T(8,128)}), f32[64,1536]{1,0:T(8,128)S(1)}, s32[]{:S(2)}) async-start(f32[128,1536]{1,0:T(8,128)} %copy-done.2), calls=%async_computation.2 | async-start | bytes 786432 | tf_op jit(solution)/shard_map/slice | solution.py:90
